TPU v7x, 128 devices: a whole 4x4x4 slice. The times are simulated.
128 devices in a mesh: stripe: 8 (over x_lo, y), frame: 16 (over z, x_hi, core).
Axes of the slice: x: 4 (x_hi: 2, x_lo: 2; x = x_hi * 2 + x_lo), y: 4, z: 4, core: 2. Of those that a mesh axis runs over, the one named last changes fastest.
Arguments:
- reference_img: bfloat16 [16384, 2048], P(('stripe', 'frame')), may hold values from -6 to 6
- frames: bfloat16 [256, 128, 2048], P(('stripe', 'frame')), may hold values from -6 to 6
- shifts: int32 [256], P(('stripe', 'frame')), may hold values from 0 to 2047
- dest_device: int32 [32768, 1], P(('stripe', 'frame')), may hold values from 0 to 127; in each aligned block of 256 rows (0 to 255, 256 to 511, ...) at most 4 rows name the same one
- dest_row: int32 [32768], P(('stripe', 'frame')), may hold values from 0 to 127
- visit_order: int32 [4], replicated, may hold values from 0 to 7, as said below
Outputs:
- correlation: float32 [256, 4, 2048], P(('stripe', 'frame'))
- blended: float32 [16384, 2048], P(('stripe', 'frame'))
Inputs may be any that keep to these rules, and one draw needn't show every extreme that they name: `visit_order`: the 4 entries are distinct stripes. `dest_device`: the rows of one device name no band more than 4 times.
All inputs are finite; a program needn't handle non-finite values.
Results may differ from a plain program's by a relative error of at most 0.0057.
Values may be sent and summed in bfloat16 or wider, within the bound.
No kernel may reach another device: no remote copies, remote signals or barrier semaphores. Data moves between devices by JAX's collectives and lax.ppermute only.
A program may use at most 128 MiB of HBM per device.

v0:
```python
import math

import jax
import jax.numpy as jnp
from jax import lax
from jax.sharding import PartitionSpec as P


def broadcast(value, axis, source):
    kept = jnp.where(lax.axis_index(axis) == source, value, 0).astype(value.dtype)
    return lax.psum(kept, axis)


def basis_table(pixels):
    indices = jnp.arange(pixels, dtype=jnp.int32)
    products = indices[:, None] * indices[None, :] % pixels
    phases = products.astype(jnp.float32) * (2.0 * math.pi / pixels)
    return jnp.concatenate([jnp.cos(phases), -jnp.sin(phases)], axis=1).astype(jnp.bfloat16)


def per_device(reference_img, frames, shifts, dest_device, dest_row, visit_order):
    count_frames, band_rows, pixels = frames.shape
    dft_basis = basis_table(pixels)
    high = lax.Precision.HIGHEST
    spectra = jnp.dot(
        frames.reshape(count_frames * band_rows, pixels),
        dft_basis,
        preferred_element_type=jnp.float32,
    )
    spectra = spectra.reshape(count_frames, band_rows, 2 * pixels)
    spec_re = spectra[:, :, :pixels]
    spec_im = spectra[:, :, pixels:]
    frame_power = jnp.sum(spec_re * spec_re + spec_im * spec_im, axis=1)
    own_spectrum = jnp.dot(reference_img, dft_basis, preferred_element_type=jnp.float32).astype(
        jnp.bfloat16
    )
    results = []
    for step in range(visit_order.shape[0]):
        root_idx = visit_order[step]
        band_spec = broadcast(own_spectrum, "stripe", root_idx)
        band_f = band_spec.astype(jnp.float32)
        band_re = band_f[:, :pixels]
        band_im = band_f[:, pixels:]
        band_power = jnp.sum(band_re * band_re + band_im * band_im, axis=0)
        cross_re = jnp.einsum("fiu,iu->fu", spec_re, band_re, precision=high) + jnp.einsum(
            "fiu,iu->fu", spec_im, band_im, precision=high
        )
        cross_im = jnp.einsum("fiu,iu->fu", spec_im, band_re, precision=high) - jnp.einsum(
            "fiu,iu->fu", spec_re, band_im, precision=high
        )
        magnitude = jnp.sqrt(frame_power * band_power[None, :] + 1e-06)
        coherence = jnp.concatenate([cross_re / magnitude, cross_im / magnitude], axis=1).astype(
            jnp.bfloat16
        )
        surface = lax.dot_general(
            coherence, dft_basis, (((1,), (1,)), ((), ())), preferred_element_type=jnp.float32
        )
        results.append(surface * math.sqrt(band_rows / pixels))
    correlation = jnp.stack(results, axis=1)
    stripes = lax.axis_size("stripe")
    blocks = lax.axis_size("frame")
    num_devices = stripes * blocks
    capacity = max(2, 2 * count_frames * band_rows // num_devices)
    placed = jax.vmap(lambda frame_img, amount: jnp.roll(frame_img, amount, axis=1))(frames, shifts)
    placed = placed.reshape(count_frames * band_rows, pixels)
    target_dev = dest_device[:, 0]
    onehot = (target_dev[:, None] == jnp.arange(num_devices, dtype=jnp.int32)[None, :]).astype(
        jnp.int32
    )
    row_rank = jnp.sum((jnp.cumsum(onehot, axis=0) - 1) * onehot, axis=1)
    slot_id = target_dev * capacity + row_rank
    select = slot_id[None, :] == jnp.arange(num_devices * capacity, dtype=jnp.int32)[:, None]
    outgoing = jnp.dot(
        select.astype(jnp.bfloat16), placed, preferred_element_type=jnp.float32
    ).astype(jnp.bfloat16)
    filled = jnp.any(select, axis=1)
    local_row = jnp.sum(jnp.where(select, dest_row[None, :], 0), axis=1)
    out_index = jnp.where(filled, local_row, -1).astype(jnp.float32).astype(jnp.bfloat16)[:, None]
    incoming, in_index = (
        lax.all_to_all(outgoing, ("stripe", "frame"), split_axis=0, concat_axis=0, tiled=True),
        lax.all_to_all(out_index, ("stripe", "frame"), split_axis=0, concat_axis=0, tiled=True),
    )
    index_f = in_index[:, 0].astype(jnp.float32)
    hits = index_f[None, :] == jnp.arange(band_rows, dtype=jnp.float32)[:, None]
    landed = jnp.dot(hits.astype(jnp.bfloat16), incoming, preferred_element_type=jnp.float32)
    land_count = jnp.sum(hits.astype(jnp.float32), axis=1)
    blended = (reference_img.astype(jnp.float32) + landed) / (1.0 + land_count[:, None])
    return (correlation, blended)


def solution(mesh):
    placed = (
        P(("stripe", "frame"), None),
        P(("stripe", "frame"), None, None),
        P(("stripe", "frame")),
        P(("stripe", "frame"), None),
        P(("stripe", "frame")),
        P(),
    )
    return jax.shard_map(
        per_device,
        mesh=mesh,
        in_specs=placed,
        out_specs=(P(("stripe", "frame"), None, None), P(("stripe", "frame"), None)),
        check_vma=False,
    )
```

profile of v0, /device:TPU:0, one launch (start us, length us, event | category | flops | bytes accessed | tf_op | source)
XLA Modules:
  0.0 314.8 jit_solution(8779242937617494023)
XLA Ops:
  11.6 11.2 %all-to-all-start = ((bf16[128,4,1]{1,2,0:T(2,128)(2,1)}), bf16[128,4,1]{1,2,0:T(2,128)(2,1)S(1)}, u32[]{:S(2)}, u32[]{:S(2)}) async-start(bf16[128,4,1]{1,2,0:T(2,128)(2,1)} %convert_element_type.99), calls=%async_computation | async-start | bytes 131072 | tf_op jit(solution)/shard_map/all_to_all | solution.py:81
  22.9 68.2 %negate_convert_fusion = (bf16[2048,2048]{1,0:T(8,128)(2,1)}, bf16[2048,2048]{1,0:T(8,128)(2,1)}) fusion(), kind=kLoop, calls=%fused_computation.9 | loop fusion | flops 71303168 | bytes 16777216 | tf_op jit(solution)/shard_map/convert.10
  94.3 11.0 %select_bitcast_fusion.2 = (bf16[128,4096]{0,1:T(8,128)(2,1)}, bf16[128,4096]{0,1:T(8,128)(2,1)}, bf16[128,4096]{0,1:T(8,128)(2,1)}, bf16[128,4096]{0,1:T(8,128)(2,1)}) fusion(pred[]{:T(512)S(6)} %eq.67, pred[]{:T(512)S(6)} %eq.69, pred[]{:T(512)S(6)} %eq.68, pred[]{:T(512)S(6)} %eq.66, bf16[128,2048]{1,0:T(8,128)(2,1)S(1)} %copy-done.6, ...), kind=kOutput, calls=%fused_computation.62 | convolution fusion | flops 2183659520 | bytes 21495812 | tf_op jit(solution)/shard_map/dot_general | solution.py:34
  105.7 6.0 %while.1 = (s32[]{:T(128)}, bf16[2,128,4096]{2,1,0:T(8,128)(2,1)S(1)}, s32[2,3]{1,0:T(2,128)S(1)}, bf16[2,128,2048]{2,1,0:T(8,128)(2,1)}, s32[]{:T(128)}) while((s32[]{:T(128)}, bf16[2,128,4096]{2,1,0:T(8,128)(2,1)S(1)}, s32[2,3]{1,0:T(2,128)S(1)}, bf16[2,128,2048]{2,1,0:T(8,128)(2,1)}, s32[]{:T(128)}) %tuple.82), condition=%wide.while_cond, body=%wide.while_body.sunk | while | flops 2 | bytes 1049717 | solution.py:64
  106.4 2.3 dynamic-slice_dynamic-update-slice_fusion.2
  109.4 2.3 dynamic-slice_dynamic-update-slice_fusion.2
  111.7 1.9 convolution_convert_fusion.1
  113.6 2.2 all_to_all.13
  115.9 9.9 %all-to-all-start.1 = ((bf16[128,4,2048]{2,1,0:T(4,128)(2,1)}), bf16[128,4,2048]{2,1,0:T(4,128)(2,1)S(1)}, u32[]{:S(2)}, u32[]{:S(2)}) async-start(bf16[128,4,2048]{2,1,0:T(4,128)(2,1)} %all_to_all.13), calls=%async_computation.1 | async-start | bytes 4194304 | tf_op jit(solution)/shard_map/all_to_all | solution.py:80
  125.8 8.9 %fusion.60 = f32[4096,256]{0,1:T(8,128)S(1)} fusion(bf16[256,2048]{1,0:T(8,128)(2,1)S(1)} %bitcast.155, bf16[2048,2048]{1,0:T(8,128)(2,1)} %get-tuple-element.116, bf16[2048,2048]{1,0:T(8,128)(2,1)} %get-tuple-element.117), kind=kOutput, calls=%fused_computation.144 | convolution fusion | flops 4328521728 | bytes 22020096 | tf_op jit(solution)/shard_map/dot_general | solution.py:25
  134.7 1.9 copy-done
  137.5 31.5 %all-to-all-done.1 = bf16[128,4,2048]{2,1,0:T(4,128)(2,1)S(1)} async-done(((bf16[128,4,2048]{2,1,0:T(4,128)(2,1)}), bf16[128,4,2048]{2,1,0:T(4,128)(2,1)S(1)}, u32[]{:S(2)}, u32[]{:S(2)}) %all-to-all-start.1) | async-done | bytes 2097184 | tf_op jit(solution)/shard_map/all_to_all | solution.py:80
  169.0 2.0 all_to_all.15
  171.0 3.1 fusion.6
  174.1 64.1 %all-reduce.4.cloned.1.call-done = (bf16[128,4096]{0,1:T(8,128)(2,1)}, bf16[128,4096]{0,1:T(8,128)(2,1)}, bf16[128,4096]{0,1:T(8,128)(2,1)}, bf16[128,4096]{0,1:T(8,128)(2,1)}) async-done(((bf16[128,4096]{0,1:T(8,128)(2,1)}, bf16[128,4096]{0,1:T(8,128)(2,1)}, bf16[128,4096]{0,1:T(8,128)(2,1)}, bf16[128,4096]{0,1:T(8,128)(2,1)}), (bf16[128,4096]{0,1:T(8,128)(2,1)}, bf16[128,4096]{0,1:T(8,128)(2,1)}, ...) | async-done | bytes 4194320 | tf_op jit(solution)/shard_map/psum | solution.py:11
  239.7 2.7 fusion.26
  242.4 2.7 convert_element_type.88
  251.5 1.6 copy.137
  253.0 2.5 copy.138
  255.6 1.9 fusion.12
  257.5 2.5 copy.144
  260.0 2.5 copy.143
  262.5 1.9 fusion.14
  264.4 2.5 copy.142
  266.9 2.6 copy.141
  269.9 1.6 copy.140
  271.5 1.6 copy.139
  273.0 5.3 %multiply_reduce_fusion.15 = (f32[2048,2]{0,1:T(2,128)S(1)}, f32[2048,2]{0,1:T(2,128)S(1)}, f32[2048,2]{0,1:T(2,128)S(1)}, f32[2048,2]{0,1:T(2,128)S(1)}, f32[20...) fusion(f32[2,128,4096]{2,1,0:T(8,128)} %bitcast.152, ...), kind=kLoop, calls=%fused_computation.42 | loop fusion | flops 16711680 | bytes 12845056 | tf_op jit(solution)/shard_map/fiu,iu->fu/dot_general | solution.py:45
  278.4 8.3 %fusion.9 = f32[2,1,2048]{2,0,1:T(2,128)S(1)} fusion(bf16[2,2048]{1,0:T(2,128)(2,1)S(1)} %get-tuple-element.103, bf16[2,2048]{1,0:T(2,128)(2,1)S(1)} %get-tuple-element.102, bf16[2048,2048]{1,0:T(8,128)(2,1)} %get-tuple-element.116, bf16[2048,2048]{1,0:T(8,128)(2,1)} %get-tuple-element.117), kind=kOutput, calls=%fused_computation.23 | convolution fusion | flops 67145728 | bytes 16809984 | tf_op jit(solution)/shard_map/dot_general | solution.py:55
  286.8 7.0 %fusion.10 = f32[2,1,2048]{2,0,1:T(2,128)S(1)} fusion(bf16[2,2048]{1,0:T(2,128)(2,1)S(1)} %get-tuple-element.101, bf16[2,2048]{1,0:T(2,128)(2,1)S(1)} %get-tuple-element.100, bf16[2048,2048]{1,0:T(8,128)(2,1)S(1)} %bitcast.154, bf16[2048,2048]{1,0:T(8,128)(2,1)} %get-tuple-element.117), kind=kOutput, calls=%fused_computation.25 | convolution fusion | flops 67145728 | bytes 16809984 | tf_op jit(solution)/shard_map/dot_general | solution.py:55
  293.8 6.7 %fusion.7 = f32[2,1,2048]{2,0,1:T(2,128)S(1)} fusion(bf16[2,2048]{1,0:T(2,128)(2,1)S(1)} %get-tuple-element.108, bf16[2,2048]{1,0:T(2,128)(2,1)S(1)} %get-tuple-element.109, bf16[2048,2048]{1,0:T(8,128)(2,1)S(1)} %bitcast.154, bf16[2048,2048]{1,0:T(8,128)(2,1)} %get-tuple-element.117), kind=kOutput, calls=%fused_computation.19 | convolution fusion | flops 67145728 | bytes 16809984 | tf_op jit(solution)/shard_map/dot_general | solution.py:55
  300.5 6.7 %fusion.8 = f32[2,1,2048]{2,0,1:T(2,128)S(1)} fusion(bf16[2,2048]{1,0:T(2,128)(2,1)S(1)} %get-tuple-element.110, bf16[2,2048]{1,0:T(2,128)(2,1)S(1)} %get-tuple-element.111, bf16[2048,2048]{1,0:T(8,128)(2,1)S(1)} %bitcast.154, bf16[2048,2048]{1,0:T(8,128)(2,1)} %get-tuple-element.117), kind=kOutput, calls=%fused_computation.21 | convolution fusion | flops 67145728 | bytes 16809984 | tf_op jit(solution)/shard_map/dot_general | solution.py:55
  (66 shorter events, 16.8 us)
Async XLA Ops:
  11.6 104.3 %all-to-all-start = ((bf16[128,4,1]{1,2,0:T(2,128)(2,1)}), bf16[128,4,1]{1,2,0:T(2,128)(2,1)S(1)}, u32[]{:S(2)}, u32[]{:S(2)}) async-start(bf16[128,4,1]{1,2,0:T(2,128)(2,1)} %convert_element_type.99), calls=%async_computation | async-start | bytes 131072 | tf_op jit(solution)/shard_map/all_to_all | solution.py:81
  22.8 215.4 %all-reduce.4.cloned.1.call-start = ((), (), s32[]{:S(2)}) async-start(), calls=%async_computation.2 | async-start | bytes 8388608 | tf_op jit(solution)/shard_map/psum | solution.py:11
  22.9 68.2 %copy-start.5 = (s32[4]{0:T(128)S(1)}, s32[4]{0:T(128)}, u32[]{:S(2)}) copy-start(s32[4]{0:T(128)} %param.11) | copy-start | bytes 52
  22.9 71.4 %copy-start.6 = (bf16[128,2048]{1,0:T(8,128)(2,1)S(1)}, bf16[128,2048]{1,0:T(8,128)(2,1)}, u32[]{:S(2)}) copy-start(bf16[128,2048]{1,0:T(8,128)(2,1)} %param.6) | copy-start | bytes 1572868
  94.3 11.0 %copy-start.8 = (s32[2]{0:T(128)S(1)}, s32[2]{0:T(128)}, u32[]{:S(2)}) copy-start(s32[2]{0:T(128)} %param.8) | copy-start | bytes 28
  94.3 11.2 %copy-start.4 = (bf16[2,128,2048]{2,1,0:T(8,128)(2,1)S(1)}, bf16[2,128,2048]{2,1,0:T(8,128)(2,1)}, u32[]{:S(2)}) copy-start(bf16[2,128,2048]{2,1,0:T(8,128)(2,1)} %param.7) | copy-start | bytes 3145732
  115.9 53.1 %all-to-all-start.1 = ((bf16[128,4,2048]{2,1,0:T(4,128)(2,1)}), bf16[128,4,2048]{2,1,0:T(4,128)(2,1)S(1)}, u32[]{:S(2)}, u32[]{:S(2)}) async-start(bf16[128,4,2048]{2,1,0:T(4,128)(2,1)} %all_to_all.13), calls=%async_computation.1 | async-start | bytes 4194304 | tf_op jit(solution)/shard_map/all_to_all | solution.py:80
  134.7 1.9 copy-start
  134.7 36.3 %copy-start.7 = (bf16[128,2048]{1,0:T(8,128)(2,1)S(1)}, bf16[128,2048]{1,0:T(8,128)(2,1)}, u32[]{:S(2)}) copy-start(bf16[128,2048]{1,0:T(8,128)(2,1)} %param.6) | copy-start | bytes 1572868
  238.2 6.9 %copy-start.3 = (bf16[128,4096]{0,1:T(8,128)(2,1)S(1)}, bf16[128,4096]{0,1:T(8,128)(2,1)}, u32[]{:S(2)}) copy-start(bf16[128,4096]{0,1:T(8,128)(2,1)} %get-tuple-element.71) | copy-start | bytes 3145732
  238.2 8.4 %copy-start.2 = (bf16[128,4096]{0,1:T(8,128)(2,1)S(1)}, bf16[128,4096]{0,1:T(8,128)(2,1)}, u32[]{:S(2)}) copy-start(bf16[128,4096]{0,1:T(8,128)(2,1)} %get-tuple-element.72) | copy-start | bytes 3145732
  239.7 9.8 %copy-start.1 = (bf16[128,4096]{0,1:T(8,128)(2,1)S(1)}, bf16[128,4096]{0,1:T(8,128)(2,1)}, u32[]{:S(2)}) copy-start(bf16[128,4096]{0,1:T(8,128)(2,1)} %get-tuple-element.73) | copy-start | bytes 3145732
  273.0 13.8 %slice-start = ((s8[8388608]{0:T(1024)(128)(4,1)}), s8[4194304]{0:T(1024)(128)(4,1)S(1)}, s32[]{:S(2)}) async-start(s8[8388608]{0:T(1024)(128)(4,1)} %bitcast.153), calls=%async_computation.3 | async-start | bytes 8388608
  278.4 8.4 %slice-start.1 = ((s8[8388608]{0:T(1024)(128)(4,1)}), s8[4194304]{0:T(1024)(128)(4,1)S(1)}, s32[]{:S(2)}) async-start(s8[8388608]{0:T(1024)(128)(4,1)} %bitcast.153), calls=%async_computation.4 | async-start | bytes 8388608
Sparse Core Ops, SparseCore 0:
  105.5 132.6 all-reduce.3
where the time goes:
time: 316 us; the launch traced here: 315 us
  waiting for transfers between devices  95.6 us (30%)
  other arithmetic  94.9 us (30%)
  matrix products  53.5 us (17%)
  local copies, waits for them, and re-layouts  32.7 us (10%)
  starting transfers between devices  21.1 us (7%)
  between operations  16.9 us (5%)
    another operation x5, other arithmetic  68.6 us
    psum x1, waiting for transfers between devices, broadcast(): return lax.psum(kept, axis)  64.1 us
    all_to_all x1, waiting for transfers between devices, per_device(): lax.all_to_all(outgoing, ('stripe', 'frame'), split_axis=0, concat_axis=0...  31.5 us
    dot_general x4, matrix products, per_device(): lax.dot_general(coherence, dft_basis, (((1,), (1,)), ((), ())), preferred...  28.7 us
    unnamed x33, local copies, waits for them, and re-layouts  20.1 us
    all_to_all x1, starting transfers between devices, per_device(): lax.all_to_all(out_index, ('stripe', 'frame'), split_axis=0, concat_axis=...  11.2 us
    dot_general x1, matrix products, per_device(): jnp.dot(reference_img, dft_basis, preferred_element_type=jnp.float32)  11 us
    all_to_all x1, starting transfers between devices, per_device(): lax.all_to_all(outgoing, ('stripe', 'frame'), split_axis=0, concat_axis=0...  9.93 us
  transfers between devices with their start and end apart: 3, of which 2 were waited for; matrix products, arithmetic and copies ran while one was open for 32% of the time, Pallas kernels for 0%

commit v1 on v0

v1 whole, which is shorter than its diff:
```python
import math

import jax
import jax.numpy as jnp
from jax import lax
from jax.sharding import PartitionSpec as P


def basis_halves(pixels):
    lo_count = 64 if pixels % 64 == 0 else 1
    hi_count = pixels // lo_count
    u = jnp.arange(pixels, dtype=jnp.int32)
    scale = 2.0 * math.pi / pixels
    hi = jnp.arange(hi_count, dtype=jnp.int32)
    lo = jnp.arange(lo_count, dtype=jnp.int32)
    phase_hi = (hi[:, None] * lo_count * u[None, :] % pixels).astype(jnp.float32) * scale
    phase_lo = (lo[:, None] * u[None, :] % pixels).astype(jnp.float32) * scale
    c1, s1 = jnp.cos(phase_hi)[:, None, :], jnp.sin(phase_hi)[:, None, :]
    c2, s2 = jnp.cos(phase_lo)[None, :, :], jnp.sin(phase_lo)[None, :, :]
    cos_t = (c1 * c2 - s1 * s2).reshape(pixels, pixels).astype(jnp.bfloat16)
    nsin_t = (-(s1 * c2 + c1 * s2)).reshape(pixels, pixels).astype(jnp.bfloat16)
    return cos_t, nsin_t


def shift_rows(frame_img, amount):
    pixels = frame_img.shape[-1]
    doubled = jnp.concatenate([frame_img, frame_img], axis=1)
    start = pixels - lax.rem(amount, pixels)
    return lax.dynamic_slice_in_dim(doubled, start, pixels, axis=1)


def per_device(reference_img, frames, shifts, dest_device, dest_row, visit_order):
    count_frames, band_rows, pixels = frames.shape
    cos_t, nsin_t = basis_halves(pixels)
    steps = visit_order.shape[0]

    gathered = lax.all_gather(reference_img, "stripe")
    visited = jnp.take(gathered, visit_order, axis=0, mode="clip")

    frame_flat = frames.reshape(count_frames * band_rows, pixels)
    spec_re = jnp.dot(frame_flat, cos_t, preferred_element_type=jnp.float32).reshape(
        count_frames, band_rows, pixels
    )
    spec_im = jnp.dot(frame_flat, nsin_t, preferred_element_type=jnp.float32).reshape(
        count_frames, band_rows, pixels
    )
    frame_power = jnp.sum(spec_re * spec_re + spec_im * spec_im, axis=1)

    visited_flat = visited.reshape(steps * band_rows, pixels)
    band_re = (
        jnp.dot(visited_flat, cos_t, preferred_element_type=jnp.float32)
        .astype(jnp.bfloat16)
        .astype(jnp.float32)
        .reshape(steps, band_rows, pixels)
    )
    band_im = (
        jnp.dot(visited_flat, nsin_t, preferred_element_type=jnp.float32)
        .astype(jnp.bfloat16)
        .astype(jnp.float32)
        .reshape(steps, band_rows, pixels)
    )
    band_power = jnp.sum(band_re * band_re + band_im * band_im, axis=1)

    fr = spec_re[:, None]
    fi = spec_im[:, None]
    br = band_re[None]
    bi = band_im[None]
    cross_re = jnp.sum(fr * br, axis=2) + jnp.sum(fi * bi, axis=2)
    cross_im = jnp.sum(fi * br, axis=2) - jnp.sum(fr * bi, axis=2)
    magnitude = jnp.sqrt(frame_power[:, None, :] * band_power[None, :, :] + 1e-06)
    coh_re = (cross_re / magnitude).astype(jnp.bfloat16).reshape(count_frames * steps, pixels)
    coh_im = (cross_im / magnitude).astype(jnp.bfloat16).reshape(count_frames * steps, pixels)
    surface = jnp.dot(coh_re, cos_t, preferred_element_type=jnp.float32) + jnp.dot(
        coh_im, nsin_t, preferred_element_type=jnp.float32
    )
    correlation = (surface * math.sqrt(band_rows / pixels)).reshape(count_frames, steps, pixels)

    num_devices = lax.axis_size("stripe") * lax.axis_size("frame")
    frame_rows = count_frames * band_rows
    capacity = max(2, 2 * frame_rows // num_devices)
    placed = jnp.concatenate(
        [shift_rows(frames[f], shifts[f]) for f in range(count_frames)], axis=0
    )
    target_dev = dest_device[:, 0]
    onehot = (target_dev[:, None] == jnp.arange(num_devices, dtype=jnp.int32)[None, :]).astype(
        jnp.int32
    )
    row_rank = jnp.sum((jnp.cumsum(onehot, axis=0) - 1) * onehot, axis=1)
    slot_id = target_dev * capacity + row_rank
    select = slot_id[None, :] == jnp.arange(num_devices * capacity, dtype=jnp.int32)[:, None]
    outgoing = jnp.dot(
        select.astype(jnp.bfloat16), placed, preferred_element_type=jnp.float32
    ).astype(jnp.bfloat16)
    filled = jnp.any(select, axis=1)
    local_row = jnp.sum(jnp.where(select, dest_row[None, :], 0), axis=1)
    out_index = jnp.where(filled, local_row, -1).astype(jnp.float32).astype(jnp.bfloat16)
    lanes = 128
    index_block = jnp.pad(
        out_index.reshape(num_devices, capacity), ((0, 0), (0, lanes - capacity)), constant_values=-1
    )
    packed = jnp.concatenate(
        [outgoing.reshape(num_devices, capacity * pixels), index_block], axis=1
    )
    received = lax.all_to_all(packed, ("stripe", "frame"), split_axis=0, concat_axis=0, tiled=True)
    incoming = received[:, : capacity * pixels].reshape(num_devices * capacity, pixels)
    index_f = received[:, capacity * pixels : capacity * pixels + capacity].reshape(-1).astype(
        jnp.float32
    )
    hits = index_f[None, :] == jnp.arange(band_rows, dtype=jnp.float32)[:, None]
    landed = jnp.dot(hits.astype(jnp.bfloat16), incoming, preferred_element_type=jnp.float32)
    land_count = jnp.sum(hits.astype(jnp.float32), axis=1)
    blended = (reference_img.astype(jnp.float32) + landed) / (1.0 + land_count[:, None])
    return (correlation, blended)


def solution(mesh):
    placed = (
        P(("stripe", "frame"), None),
        P(("stripe", "frame"), None, None),
        P(("stripe", "frame")),
        P(("stripe", "frame"), None),
        P(("stripe", "frame")),
        P(),
    )
    return jax.shard_map(
        per_device,
        mesh=mesh,
        in_specs=placed,
        out_specs=(P(("stripe", "frame"), None, None), P(("stripe", "frame"), None)),
        check_vma=False,
    )
```

time: 316 us -> 150 us (0.47)
  the two profiles are of different devices: /device:TPU:0 before, /device:TPU:24 now
where the time goes in v1:
time: 150 us; the launch traced here: 149 us
  local copies, waits for them, and re-layouts  35.9 us (24%)
  matrix products  33 us (22%)
  waiting for transfers between devices  30.1 us (20%)
  other arithmetic  21.3 us (14%)
  between operations  18.2 us (12%)
  starting transfers between devices  10.3 us (7%)
    all_to_all x1, waiting for transfers between devices, per_device(): lax.all_to_all(packed, ('stripe', 'frame'), split_axis=0, concat_axis=0,...  29.4 us
    unnamed x19, local copies, waits for them, and re-layouts  19.3 us
    all_to_all x1, starting transfers between devices, per_device(): lax.all_to_all(packed, ('stripe', 'frame'), split_axis=0, concat_axis=0,...  10.3 us
    dot_general x1, matrix products, per_device(): jnp.dot(visited_flat, nsin_t, preferred_element_type=jnp.float32)  7.11 us
    dot_general x1, matrix products, per_device(): jnp.dot(visited_flat, cos_t, preferred_element_type=jnp.float32)  6.89 us
    convert_element_type x1, other arithmetic, basis_halves(): cos_t = (c1 * c2 - s1 * s2).reshape(pixels, pixels).astype(jnp.bfloat16)  5.88 us
    all_to_all x2, other arithmetic, per_device(): lax.all_to_all(packed, ('stripe', 'frame'), split_axis=0, concat_axis=0,...  4.7 us
    dot_general x1, matrix products, per_device(): jnp.dot(coh_im, nsin_t, preferred_element_type=jnp.float32)  4.57 us
  transfers between devices with their start and end apart: 2, of which 1 were waited for; matrix products, arithmetic and copies ran while one was open for 37% of the time, Pallas kernels for 0%

profile of v1, /device:TPU:24, one launch (start us, length us, event | category | flops | bytes accessed | tf_op | source)
XLA Modules:
  0.0 148.9 jit_solution(499715121576111951)
XLA Ops:
  7.9 0.8 copy.16
  9.0 1.3 fusion.34
  14.2 0.9 fusion.27
  15.9 0.8 select_reduce_fusion
  16.9 1.3 slice_bitcast_fusion.1
  18.2 0.9 fusion.11
  19.1 0.7 convolution_convert_fusion
  19.9 2.9 %reshape.269 = bf16[128,8192]{1,0:T(8,128)(2,1)} reshape(bf16[512,2048]{1,0:T(8,128)(2,1)S(1)} %convolution_convert_fusion) | data formatting | bytes 4194304 | tf_op jit(solution)/shard_map/reshape | solution.py:102
  22.7 1.8 %fusion.4 = bf16[128,1,8320]{2,0,1:T(8,128)(2,1)S(1)} fusion(bf16[128,4]{1,0:T(8,128)(2,1)S(1)} %convert_element_type.187, bf16[128,8192]{1,0:T(8,128)(2,1)} %reshape.269), kind=kLoop, calls=%fused_computation.18 | loop fusion | flops 6389760 | bytes 4228096 | tf_op jit(solution)/shard_map/all_to_all | solution.py:104
  25.0 2.9 %reduce = bf16[128,8320]{1,0:T(8,128)(2,1)} reduce(bf16[128,1,8320]{2,0,1:T(8,128)(2,1)S(1)} %fusion.4, bf16[]{:T(256)} %broadcast.256), dimensions={1}, to_apply=%copy.18.reduce_sub_computation | reduce | bytes 4259842 | tf_op jit(solution)/shard_map/all_to_all | solution.py:104
  28.0 4.5 %reshape.284 = bf16[128,2,4160]{2,1,0:T(2,128)(2,1)} reshape(bf16[128,8320]{1,0:T(8,128)(2,1)} %reduce) | data formatting | bytes 4259840
  32.5 10.3 %all-to-all-start = ((bf16[128,2,4160]{2,1,0:T(2,128)(2,1)}), bf16[128,2,4160]{2,1,0:T(2,128)(2,1)S(1)}, u32[]{:S(2)}, u32[]{:S(2)}) async-start(bf16[128,2,4160]{2,1,0:T(2,128)(2,1)} %reshape.284), calls=%async_computation | async-start | bytes 4325376 | tf_op jit(solution)/shard_map/all_to_all | solution.py:104
  42.8 2.0 %fusion.21 = (f32[64,2048]{1,0:T(8,128)S(1)}, f32[64,2048]{1,0:T(8,128)S(1)}) fusion(), kind=kLoop, calls=%fused_computation.55 | loop fusion | flops 1835008 | bytes 1048576 | tf_op jit(solution)/shard_map/sin | solution.py:19
  44.9 1.1 fusion.31
  46.0 5.9 %subtract_convert_fusion = (bf16[32,64,2048]{2,1,0:T(8,128)(2,1)S(1)}, bf16[32,64,2048]{2,1,0:T(8,128)(2,1)S(1)}) fusion(f32[64,2048]{1,0:T(8,128)S(1)} %get-tuple-element.24, f32[32,2048]{1,0:T(8,128)S(1)} %get-tuple-element.17, f32[64,2048]{1,0:T(8,128)S(1)} %get-tuple-element.25, f32[32,2048]{1,0:T(8,128)S(1)} %get-tuple-element.16), kind=kLoop, calls=%fused_computation.2 | loop fusion | flops 37748736 | bytes 18350080 | tf_op jit(solution)/shard_map/convert_element_type | solution.py:20
  51.9 2.3 %fusion.36 = f32[2048,256]{0,1:T(8,128)S(1)} fusion(bf16[256,2048]{1,0:T(8,128)(2,1)S(1)} %bitcast.68, bf16[2048,2048]{1,0:T(8,128)(2,1)S(1)} %bitcast.58), kind=kOutput, calls=%fused_computation.84 | convolution fusion | flops 2147483648 | bytes 11534336 | tf_op jit(solution)/shard_map/dot_general | solution.py:41
  54.2 0.9 copy-done.1
  55.1 2.5 %copy-done = bf16[32,64,2048]{2,1,0:T(8,128)(2,1)} copy-done((bf16[32,64,2048]{2,1,0:T(8,128)(2,1)}, bf16[32,64,2048]{2,1,0:T(8,128)(2,1)S(1)}, u32[]{:S(2)}) %copy-start) | copy-done | bytes 8388632
  58.3 3.8 %add_reduce_fusion.1 = (f32[2,2048]{1,0:T(2,128)S(1)}, f32[2048,256]{0,1:T(8,128)}) fusion(f32[2048,256]{0,1:T(8,128)S(1)} %fusion.36, bf16[256,2048]{1,0:T(8,128)(2,1)S(1)} %bitcast.69, bf16[2048,2048]{1,0:T(8,128)(2,1)S(1)} %bitcast.55), kind=kOutput, calls=%fused_computation.20 | convolution fusion | flops 2149576704 | bytes 13647872 | tf_op jit(solution)/shard_map/dot_general | solution.py:44
  62.1 29.4 %all-to-all-done = bf16[128,2,4160]{2,1,0:T(2,128)(2,1)S(1)} async-done(((bf16[128,2,4160]{2,1,0:T(2,128)(2,1)}), bf16[128,2,4160]{2,1,0:T(2,128)(2,1)S(1)}, u32[]{:S(2)}, u32[]{:S(2)}) %all-to-all-start) | async-done | bytes 2129952 | tf_op jit(solution)/shard_map/all_to_all | solution.py:104
  91.5 7.0 %reshape.285 = bf16[128,1,8320]{2,1,0:T(2,128)(2,1)} reshape(bf16[128,2,4160]{2,1,0:T(2,128)(2,1)S(1)} %all-to-all-done) | data formatting | bytes 4259840
  98.5 2.4 %copy.21 = bf16[128,1,8320]{2,0,1:T(8,128)(2,1)S(1)} copy(bf16[128,1,8320]{2,1,0:T(2,128)(2,1)} %reshape.285) | data formatting | bytes 4259840
  100.9 1.6 %slice.36 = bf16[128,8192]{1,0:T(8,128)(2,1)} slice(bf16[128,8320]{1,0:T(8,128)(2,1)S(1)} %bitcast.61), slice={[0:128], [0:8192]} | slice | bytes 4194304 | tf_op jit(solution)/shard_map/slice | solution.py:105
  102.5 4.5 %reshape.270 = bf16[512,2048]{1,0:T(8,128)(2,1)} reshape(bf16[128,8192]{1,0:T(8,128)(2,1)} %slice.36) | data formatting | bytes 4194304 | tf_op jit(solution)/shard_map/reshape | solution.py:105
  107.3 3.0 %fusion.1 = f32[128,2048]{1,0:T(8,128)} fusion(bf16[512,2048]{1,0:T(8,128)(2,1)} %reshape.270, bf16[128,2048]{1,0:T(8,128)(2,1)S(1)} %copy-done.6, f32[128]{0:T(128)S(1)} %broadcast_add_fusion, f32[512]{0:T(512)S(1)} %reshape.273), kind=kOutput, calls=%fused_computation.14 | convolution fusion | flops 269287424 | bytes 3672576 | tf_op jit(solution)/shard_map/dot_general | solution.py:110
  110.3 2.9 %gather_fusion = bf16[4,128,2048]{2,1,0:T(8,128)(2,1)S(1)} fusion(bf16[8,128,2048]{2,1,0:T(8,128)(2,1)} %bitcast.67, s32[1024]{0:T(1024)S(1)} %pad_clamp_fusion), kind=kCustom, calls=%fused_computation | custom fusion | bytes 4194320 | tf_op jit(solution)/shard_map/jit(_take)/gather | solution.py:38
  113.2 6.9 %bitcast_convert_fusion.1 = (f32[4,128,2048]{2,1,0:T(8,128)S(1)}, bf16[512,2048]{1,0:T(8,128)(2,1)S(1)}) fusion(bf16[512,2048]{1,0:T(8,128)(2,1)S(1)} %bitcast.65, bf16[2048,2048]{1,0:T(8,128)(2,1)} %bitcast.59), kind=kOutput, calls=%fused_computation.29 | convolution fusion | flops 4297064448 | bytes 16777216 | tf_op jit(solution)/shard_map/dot_general | solution.py:51
  120.1 7.1 %bitcast_convert_fusion = (f32[4,128,2048]{2,1,0:T(8,128)S(1)}, bf16[512,2048]{1,0:T(8,128)(2,1)S(1)}) fusion(bf16[512,2048]{1,0:T(8,128)(2,1)S(1)} %bitcast.66, bf16[2048,2048]{1,0:T(8,128)(2,1)} %bitcast.56), kind=kOutput, calls=%fused_computation.28 | convolution fusion | flops 4297064448 | bytes 16777216 | tf_op jit(solution)/shard_map/dot_general | solution.py:57
  127.2 0.9 add_reduce_fusion
  129.4 2.7 %multiply_reduce_fusion.1 = (f32[2,4,2048]{2,1,0:T(4,128)S(1)}, f32[2,4,2048]{2,1,0:T(4,128)S(1)}, f32[2,4,2048]{2,1,0:T(4,128)S(1)}, f32[2,4,2048]{2,1,0:T(4,128)S(1)}) fusion(f32[2,128,2048]{2,1,0:T(8,128)S(1)} %bitcast.64, f32[4,128,2048]{2,1,0:T(8,128)S(1)} %get-tuple-element.18, f32[2,128,2048]{2,1,0:T(8,128)S(1)} %bitcast.63, ...), kind=kLoop, calls=%fused_computation.4 | loop fusion | flops 16711680 | bytes 12845056 | tf_op jit(solution)/shard_map/reduce_sum | solution.py:69
  132.2 4.6 %fusion.35 = f32[8,2048]{1,0:T(8,128)S(1)} fusion(bf16[8,2048]{1,0:T(8,128)(2,1)S(1)} %convert_element_type.179, bf16[2048,2048]{1,0:T(8,128)(2,1)} %bitcast.60), kind=kOutput, calls=%fused_computation.83 | convolution fusion | flops 67108864 | bytes 8486912 | tf_op jit(solution)/shard_map/dot_general | solution.py:73
  136.8 4.6 %fusion.2 = f32[8,2048]{1,0:T(8,128)S(1)} fusion(f32[8,2048]{1,0:T(8,128)S(1)} %fusion.35, bf16[8,2048]{1,0:T(8,128)(2,1)S(1)} %convert_element_type.181, bf16[2048,2048]{1,0:T(8,128)(2,1)} %bitcast.57), kind=kOutput, calls=%fused_computation.16 | convolution fusion | flops 67141632 | bytes 8552448 | tf_op jit(solution)/shard_map/dot_general | solution.py:73
  (38 shorter events, 5.5 us)
Async XLA Ops:
  7.2 103.1 %all-gather.3.cloned.1.call-start = ((), (), s32[]{:S(2)}) async-start(), calls=%async_computation.1 | async-start | bytes 4718592 | tf_op jit(solution)/shard_map/all_gather | solution.py:37
  28.0 14.8 %copy-start.7 = (s32[4]{0:T(128)S(1)}, s32[4]{0:T(128)}, u32[]{:S(2)}) copy-start(s32[4]{0:T(128)} %param.11) | copy-start | bytes 52
  32.5 59.0 %all-to-all-start = ((bf16[128,2,4160]{2,1,0:T(2,128)(2,1)}), bf16[128,2,4160]{2,1,0:T(2,128)(2,1)S(1)}, u32[]{:S(2)}, u32[]{:S(2)}) async-start(bf16[128,2,4160]{2,1,0:T(2,128)(2,1)} %reshape.284), calls=%async_computation | async-start | bytes 4325376 | tf_op jit(solution)/shard_map/all_to_all | solution.py:104
  46.0 5.9 %copy-start.5 = (bf16[2,128,2048]{2,1,0:T(8,128)(2,1)S(1)}, bf16[2,128,2048]{2,1,0:T(8,128)(2,1)}, u32[]{:S(2)}) copy-start(bf16[2,128,2048]{2,1,0:T(8,128)(2,1)} %param.7) | copy-start | bytes 3145732
  51.9 3.2 %copy-start.1 = (bf16[32,64,2048]{2,1,0:T(8,128)(2,1)}, bf16[32,64,2048]{2,1,0:T(8,128)(2,1)S(1)}, u32[]{:S(2)}) copy-start(bf16[32,64,2048]{2,1,0:T(8,128)(2,1)S(1)} %get-tuple-element.8) | copy-start | bytes 25165828
  51.9 5.7 %copy-start = (bf16[32,64,2048]{2,1,0:T(8,128)(2,1)}, bf16[32,64,2048]{2,1,0:T(8,128)(2,1)S(1)}, u32[]{:S(2)}) copy-start(bf16[32,64,2048]{2,1,0:T(8,128)(2,1)S(1)} %get-tuple-element.9) | copy-start | bytes 25165828
  55.1 3.2 %copy-start.2 = (f32[2048,256]{0,1:T(8,128)}, f32[2048,256]{0,1:T(8,128)S(1)}, u32[]{:S(2)}) copy-start(f32[2048,256]{0,1:T(8,128)S(1)} %fusion.36) | copy-start | bytes 6291460
  100.9 6.4 %copy-start.6 = (bf16[128,2048]{1,0:T(8,128)(2,1)S(1)}, bf16[128,2048]{1,0:T(8,128)(2,1)}, u32[]{:S(2)}) copy-start(bf16[128,2048]{1,0:T(8,128)(2,1)} %param.6) | copy-start | bytes 1572868
  127.2 1.6 %copy-start.3 = (f32[2048,256]{0,1:T(8,128)S(1)}, f32[2048,256]{0,1:T(8,128)}, u32[]{:S(2)}) copy-start(f32[2048,256]{0,1:T(8,128)} %copy-done.2) | copy-start | bytes 6291460
  127.2 2.2 %copy-start.4 = (f32[2048,256]{0,1:T(8,128)S(1)}, f32[2048,256]{0,1:T(8,128)}, u32[]{:S(2)}) copy-start(f32[2048,256]{0,1:T(8,128)} %get-tuple-element.23) | copy-start | bytes 6291460
Sparse Core Ops, SparseCore 0:
  9.6 78.9 all-gather.2

commit v2 on v1

v2 whole, which is shorter than its diff:
```python
import math

import jax
import jax.numpy as jnp
from jax import lax
from jax.sharding import PartitionSpec as P


def basis_halves(pixels, columns):
    lo_count = 64 if pixels % 64 == 0 else 1
    hi_count = pixels // lo_count
    u = jnp.arange(columns, dtype=jnp.int32)
    scale = 2.0 * math.pi / pixels
    hi = jnp.arange(hi_count, dtype=jnp.int32)
    lo = jnp.arange(lo_count, dtype=jnp.int32)
    phase_hi = (hi[:, None] * lo_count * u[None, :] % pixels).astype(jnp.float32) * scale
    phase_lo = (lo[:, None] * u[None, :] % pixels).astype(jnp.float32) * scale
    c1, s1 = jnp.cos(phase_hi)[:, None, :], jnp.sin(phase_hi)[:, None, :]
    c2, s2 = jnp.cos(phase_lo)[None, :, :], jnp.sin(phase_lo)[None, :, :]
    cos_t = (c1 * c2 - s1 * s2).reshape(pixels, columns).astype(jnp.bfloat16)
    nsin_t = (-(s1 * c2 + c1 * s2)).reshape(pixels, columns).astype(jnp.bfloat16)
    return cos_t, nsin_t


def shift_rows(frame_img, amount):
    pixels = frame_img.shape[-1]
    doubled = jnp.concatenate([frame_img, frame_img], axis=1)
    start = pixels - lax.rem(amount, pixels)
    return lax.dynamic_slice_in_dim(doubled, start, pixels, axis=1)


def per_device(reference_img, frames, shifts, dest_device, dest_row, visit_order):
    count_frames, band_rows, pixels = frames.shape
    steps = visit_order.shape[0]
    half = pixels // 2
    columns = min(pixels, half + 128)
    cos_t, nsin_t = basis_halves(pixels, columns)
    col = jnp.arange(columns, dtype=jnp.int32)
    weight = jnp.where((col == 0) | (col == half), 1.0, jnp.where(col < half, 2.0, 0.0))

    gathered = lax.all_gather(reference_img, "stripe")
    visited = jnp.take(gathered, visit_order, axis=0, mode="clip")

    frame_flat = frames.reshape(count_frames * band_rows, pixels)
    spec_re = jnp.dot(frame_flat, cos_t, preferred_element_type=jnp.float32).reshape(
        count_frames, band_rows, columns
    )
    spec_im = jnp.dot(frame_flat, nsin_t, preferred_element_type=jnp.float32).reshape(
        count_frames, band_rows, columns
    )
    frame_power = jnp.sum(spec_re * spec_re + spec_im * spec_im, axis=1)

    visited_flat = visited.reshape(steps * band_rows, pixels)
    band_re = (
        jnp.dot(visited_flat, cos_t, preferred_element_type=jnp.float32)
        .astype(jnp.bfloat16)
        .astype(jnp.float32)
        .reshape(steps, band_rows, columns)
    )
    band_im = (
        jnp.dot(visited_flat, nsin_t, preferred_element_type=jnp.float32)
        .astype(jnp.bfloat16)
        .astype(jnp.float32)
        .reshape(steps, band_rows, columns)
    )
    band_power = jnp.sum(band_re * band_re + band_im * band_im, axis=1)

    fr = spec_re[:, None]
    fi = spec_im[:, None]
    br = band_re[None]
    bi = band_im[None]
    cross_re = jnp.sum(fr * br, axis=2) + jnp.sum(fi * bi, axis=2)
    cross_im = jnp.sum(fi * br, axis=2) - jnp.sum(fr * bi, axis=2)
    magnitude = jnp.sqrt(frame_power[:, None, :] * band_power[None, :, :] + 1e-06)
    coh_re = (cross_re / magnitude).astype(jnp.bfloat16).astype(jnp.float32) * weight
    coh_im = (cross_im / magnitude).astype(jnp.bfloat16).astype(jnp.float32) * weight
    coh_re = coh_re.astype(jnp.bfloat16).reshape(count_frames * steps, columns)
    coh_im = coh_im.astype(jnp.bfloat16).reshape(count_frames * steps, columns)
    contract = (((1,), (1,)), ((), ()))
    surface = lax.dot_general(
        coh_re, cos_t, contract, preferred_element_type=jnp.float32
    ) + lax.dot_general(coh_im, nsin_t, contract, preferred_element_type=jnp.float32)
    correlation = (surface * math.sqrt(band_rows / pixels)).reshape(count_frames, steps, pixels)

    num_devices = lax.axis_size("stripe") * lax.axis_size("frame")
    frame_rows = count_frames * band_rows
    capacity = max(2, 2 * frame_rows // num_devices)
    placed = jnp.concatenate(
        [shift_rows(frames[f], shifts[f]) for f in range(count_frames)], axis=0
    )
    target_dev = dest_device[:, 0]
    onehot = (target_dev[:, None] == jnp.arange(num_devices, dtype=jnp.int32)[None, :]).astype(
        jnp.int32
    )
    row_rank = jnp.sum((jnp.cumsum(onehot, axis=0) - 1) * onehot, axis=1)
    slot_id = target_dev * capacity + row_rank
    select = slot_id[None, :] == jnp.arange(num_devices * capacity, dtype=jnp.int32)[:, None]
    select3 = select.reshape(num_devices, capacity, frame_rows)
    outgoing = jnp.einsum(
        "dsr,rx->dsx", select3.astype(jnp.bfloat16), placed, preferred_element_type=jnp.float32
    ).astype(jnp.bfloat16)
    filled = jnp.any(select3, axis=2)
    local_row = jnp.sum(jnp.where(select3, dest_row[None, None, :], 0), axis=2)
    out_index = jnp.where(filled, local_row, -1).astype(jnp.float32).astype(jnp.bfloat16)
    lanes = 128
    index_cols = jnp.broadcast_to(out_index[:, :, None], (num_devices, capacity, lanes))
    packed = jnp.concatenate([outgoing, index_cols], axis=2)
    received = lax.all_to_all(packed, ("stripe", "frame"), split_axis=0, concat_axis=0, tiled=True)
    incoming = received[:, :, :pixels]
    index_f = received[:, :, pixels].astype(jnp.float32)
    hits = index_f[None, :, :] == jnp.arange(band_rows, dtype=jnp.float32)[:, None, None]
    landed = jnp.einsum(
        "tps,psx->tx", hits.astype(jnp.bfloat16), incoming, preferred_element_type=jnp.float32
    )
    land_count = jnp.sum(hits.astype(jnp.float32), axis=(1, 2))
    blended = (reference_img.astype(jnp.float32) + landed) / (1.0 + land_count[:, None])
    return (correlation, blended)


def solution(mesh):
    placed = (
        P(("stripe", "frame"), None),
        P(("stripe", "frame"), None, None),
        P(("stripe", "frame")),
        P(("stripe", "frame"), None),
        P(("stripe", "frame")),
        P(),
    )
    return jax.shard_map(
        per_device,
        mesh=mesh,
        in_specs=placed,
        out_specs=(P(("stripe", "frame"), None, None), P(("stripe", "frame"), None)),
        check_vma=False,
    )
```

time: 150 us -> 122 us (0.81)
  the two profiles are of different devices: /device:TPU:24 before, /device:TPU:0 now
where the time goes in v2:
time: 122 us; the launch traced here: 121 us
  waiting for transfers between devices  39.4 us (32%)
  matrix products  23.9 us (20%)
  between operations  18.2 us (15%)
  local copies, waits for them, and re-layouts  15.9 us (13%)
  other arithmetic  12.1 us (10%)
  starting transfers between devices  11.2 us (9%)
    all_to_all x1, waiting for transfers between devices, per_device(): lax.all_to_all(packed, ('stripe', 'frame'), split_axis=0, concat_axis=0,...  31.5 us
    all_to_all x1, starting transfers between devices, per_device(): lax.all_to_all(packed, ('stripe', 'frame'), split_axis=0, concat_axis=0,...  11.2 us
    all_gather x1, waiting for transfers between devices, per_device(): gathered = lax.all_gather(reference_img, 'stripe')  7.26 us
    dot_general x1, matrix products, per_device(): jnp.dot(visited_flat, cos_t, preferred_element_type=jnp.float32)  5.35 us
    unnamed x21, local copies, waits for them, and re-layouts  4.38 us
    dot_general x1, matrix products, per_device(): lax.dot_general(coh_im, nsin_t, contract, preferred_element_type=jnp.floa...  3.65 us
    dot_general x1, matrix products, per_device(): lax.dot_general(coh_re, cos_t, contract, preferred_element_type=jnp.float32)  3.65 us
    convert_element_type x1, other arithmetic, basis_halves(): cos_t = (c1 * c2 - s1 * s2).reshape(pixels, columns).astype(jnp.bfloat16)  3.64 us
  transfers between devices with their start and end apart: 2, of which 2 were waited for; matrix products, arithmetic and copies ran while one was open for 22% of the time, Pallas kernels for 0%

profile of v2, /device:TPU:0, one launch (start us, length us, event | category | flops | bytes accessed | tf_op | source)
XLA Modules:
  0.0 120.6 jit_solution(5017881816425852176)
XLA Ops:
  7.2 0.7 all-gather.3.cloned.1.call-update
  7.9 1.3 %fusion.35 = (s32[1]{0:T(128)}, s32[1]{0:T(128)}) fusion(s32[2]{0:T(128)} %param.8), kind=kLoop, calls=%fused_computation.90 | loop fusion | bytes 16 | tf_op jit(solution)/shard_map/slice | solution.py:89
  13.1 0.8 copy.21
  14.2 0.9 fusion.27
  15.1 0.7 multiply_add_fusion.1
  16.0 0.9 fusion.7
  17.0 1.3 %slice_bitcast_fusion.1 = (bf16[128,2048]{1,0:T(8,128)(2,1)S(1)}, bf16[128,2048]{1,0:T(8,128)(2,1)S(1)}) fusion(bf16[2,128,2048]{2,1,0:T(8,128)(2,1)} %param.7), kind=kLoop, calls=%fused_computation.35 | loop fusion | bytes 2097152 | tf_op jit(solution)/shard_map/squeeze | solution.py:89
  18.3 0.9 fusion.8
  19.2 0.7 convolution_convert_fusion
  20.4 3.1 %copy.23 = bf16[128,4,2176]{2,1,0:T(4,128)(2,1)} copy(bf16[128,4,2176]{2,0,1:T(8,128)(2,1)S(1)} %pad_maximum_fusion) | data formatting | bytes 4456448 | tf_op jit(solution)/shard_map/concatenate | solution.py:107
  23.4 11.2 %all-to-all-start = ((bf16[128,4,2176]{2,1,0:T(4,128)(2,1)}), bf16[128,4,2176]{2,1,0:T(4,128)(2,1)S(1)}, u32[]{:S(2)}, u32[]{:S(2)}) async-start(bf16[128,4,2176]{2,1,0:T(4,128)(2,1)} %copy.23), calls=%async_computation | async-start | bytes 4456448 | tf_op jit(solution)/shard_map/all_to_all | solution.py:108
  34.6 0.7 fusion.31
  35.3 1.2 fusion.21
  36.5 3.6 %subtract_convert_fusion = (bf16[32,64,1152]{2,1,0:T(8,128)(2,1)S(1)}, bf16[32,64,1152]{2,1,0:T(8,128)(2,1)S(1)}) fusion(f32[64,1152]{1,0:T(8,128)S(1)} %get-tuple-element.24, f32[32,1152]{1,0:T(8,128)S(1)} %get-tuple-element.17, f32[64,1152]{1,0:T(8,128)S(1)} %get-tuple-element.25, f32[32,1152]{1,0:T(8,128)S(1)} %get-tuple-element.16), kind=kLoop, calls=%fused_computation.2 | loop fusion | flops 21233664 | bytes 10321920 | tf_op jit(solution)/shard_map/convert_element_type | solution.py:20
  40.1 2.1 %copy-done.1 = bf16[32,64,1152]{2,1,0:T(8,128)(2,1)} copy-done((bf16[32,64,1152]{2,1,0:T(8,128)(2,1)}, bf16[32,64,1152]{2,1,0:T(8,128)(2,1)S(1)}, u32[]{:S(2)}) %copy-start.1) | copy-done | bytes 4718616
  42.3 1.5 %fusion.37 = f32[1152,256]{0,1:T(8,128)S(1)} fusion(bf16[256,2048]{1,0:T(8,128)(2,1)S(1)} %bitcast.74, bf16[2048,1152]{1,0:T(8,128)(2,1)S(1)} %bitcast.66), kind=kOutput, calls=%fused_computation.92 | convolution fusion | flops 1207959552 | bytes 6946816 | tf_op jit(solution)/shard_map/dot_general | solution.py:45
  43.8 1.0 copy-done.2
  44.8 2.6 %add_reduce_fusion.1 = (f32[2,1152]{1,0:T(2,128)S(1)}, f32[1152,256]{0,1:T(8,128)}) fusion(f32[1152,256]{0,1:T(8,128)S(1)} %fusion.37, bf16[256,2048]{1,0:T(8,128)(2,1)S(1)} %bitcast.75, bf16[2048,1152]{1,0:T(8,128)(2,1)S(1)} %bitcast.61), kind=kOutput, calls=%fused_computation.18 | convolution fusion | flops 1209136896 | bytes 8135680 | tf_op jit(solution)/shard_map/dot_general | solution.py:48
  47.4 31.5 %all-to-all-done = bf16[128,4,2176]{2,1,0:T(4,128)(2,1)S(1)} async-done(((bf16[128,4,2176]{2,1,0:T(4,128)(2,1)}), bf16[128,4,2176]{2,1,0:T(4,128)(2,1)S(1)}, u32[]{:S(2)}, u32[]{:S(2)}) %all-to-all-start) | async-done | bytes 2228256 | tf_op jit(solution)/shard_map/all_to_all | solution.py:108
  79.0 1.2 slice.36
  80.4 3.5 %fusion.1 = f32[128,2048]{1,0:T(8,128)} fusion(bf16[128,4,2048]{2,1,0:T(4,128)(2,1)S(1)} %slice.36, bf16[128,2048]{1,0:T(8,128)(2,1)S(1)} %copy-done.6, f32[128]{0:T(128)S(1)} %broadcast_add_fusion, f32[128,4]{0,1:T(4,128)S(1)} %bitcast_convert_fusion.2), kind=kOutput, calls=%fused_computation.12 | convolution fusion | flops 269287424 | bytes 3672576 | tf_op jit(solution)/shard_map/tps,psx->tx/dot_general | solution.py:112
  83.9 7.3 %all-gather.3.cloned.1.call-done = bf16[1024,2048]{1,0:T(8,128)(2,1)} async-done(((bf16[128,2048]{1,0:T(8,128)(2,1)}), bf16[1024,2048]{1,0:T(8,128)(2,1)}) %all-gather.3.cloned.1.call-update) | async-done | bytes 4194320 | tf_op jit(solution)/shard_map/all_gather | solution.py:41
  91.1 2.9 %gather_fusion = bf16[4,128,2048]{2,1,0:T(8,128)(2,1)S(1)} fusion(bf16[8,128,2048]{2,1,0:T(8,128)(2,1)} %bitcast.73, s32[1024]{0:T(1024)S(1)} %pad_clamp_fusion), kind=kCustom, calls=%fused_computation | custom fusion | bytes 4194320 | tf_op jit(solution)/shard_map/jit(_take)/gather | solution.py:42
  94.1 5.4 %bitcast_convert_fusion.1 = (f32[4,128,1152]{2,1,0:T(8,128)S(1)}, bf16[512,1152]{1,0:T(8,128)(2,1)S(1)}) fusion(bf16[512,2048]{1,0:T(8,128)(2,1)S(1)} %bitcast.69, bf16[2048,1152]{1,0:T(8,128)(2,1)} %bitcast.67), kind=kOutput, calls=%fused_computation.30 | convolution fusion | flops 2417098752 | bytes 10354688 | tf_op jit(solution)/shard_map/dot_general | solution.py:55
  99.5 2.9 %bitcast_convert_fusion = (f32[4,128,1152]{2,1,0:T(8,128)S(1)}, bf16[512,1152]{1,0:T(8,128)(2,1)S(1)}) fusion(bf16[512,2048]{1,0:T(8,128)(2,1)S(1)} %bitcast.70, bf16[2048,1152]{1,0:T(8,128)(2,1)S(1)} %bitcast.65), kind=kOutput, calls=%fused_computation.29 | convolution fusion | flops 2417098752 | bytes 10354688 | tf_op jit(solution)/shard_map/dot_general | solution.py:61
  102.3 0.5 add_reduce_fusion
  102.8 0.8 copy-done.3
  103.6 0.4 copy-done.4
  104.0 1.8 %multiply_reduce_fusion.1 = (f32[2,4,1152]{2,1,0:T(4,128)S(1)}, f32[2,4,1152]{2,1,0:T(4,128)S(1)}, f32[2,4,1152]{2,1,0:T(4,128)S(1)}, f32[2,4,1152]{2,1,0:T(4,128)S(1)}) fusion(f32[2,128,1152]{2,1,0:T(8,128)S(1)} %bitcast.72, f32[4,128,1152]{2,1,0:T(8,128)S(1)} %get-tuple-element.18, f32[2,128,1152]{2,1,0:T(8,128)S(1)} %bitcast.71, ...), kind=kLoop, calls=%fused_computation.4 | loop fusion | flops 9400320 | bytes 7225344 | tf_op jit(solution)/shard_map/reduce_sum | solution.py:73
  105.8 3.6 %fusion.36 = f32[8,2048]{1,0:T(8,128)S(1)} fusion(bf16[8,1152]{1,0:T(8,128)(2,1)S(1)} %convert_element_type.225, bf16[2048,1152]{1,0:T(8,128)(2,1)} %bitcast.68), kind=kOutput, calls=%fused_computation.91 | convolution fusion | flops 37748736 | bytes 4802560 | tf_op jit(solution)/shard_map/dot_general | solution.py:80
  109.5 3.6 %fusion.2 = f32[8,2048]{1,0:T(8,128)S(1)} fusion(f32[8,2048]{1,0:T(8,128)S(1)} %fusion.36, bf16[8,1152]{1,0:T(8,128)(2,1)S(1)} %convert_element_type.229, bf16[2048,1152]{1,0:T(8,128)(2,1)} %bitcast.62), kind=kOutput, calls=%fused_computation.16 | convolution fusion | flops 37781504 | bytes 4868096 | tf_op jit(solution)/shard_map/dot_general | solution.py:82
  113.1 0.7 reshape.318
  (40 shorter events, 1.4 us)
Async XLA Ops:
  7.2 84.0 %all-gather.3.cloned.1.call-start = ((), (), s32[]{:S(2)}) async-start(), calls=%async_computation.1 | async-start | bytes 4718592 | tf_op jit(solution)/shard_map/all_gather | solution.py:41
  23.4 11.2 %copy-start.7 = (s32[4]{0:T(128)S(1)}, s32[4]{0:T(128)}, u32[]{:S(2)}) copy-start(s32[4]{0:T(128)} %param.11) | copy-start | bytes 52
  23.4 55.4 %all-to-all-start = ((bf16[128,4,2176]{2,1,0:T(4,128)(2,1)}), bf16[128,4,2176]{2,1,0:T(4,128)(2,1)S(1)}, u32[]{:S(2)}, u32[]{:S(2)}) async-start(bf16[128,4,2176]{2,1,0:T(4,128)(2,1)} %copy.23), calls=%async_computation | async-start | bytes 4456448 | tf_op jit(solution)/shard_map/all_to_all | solution.py:108
  36.5 5.8 %copy-start.5 = (bf16[2,128,2048]{2,1,0:T(8,128)(2,1)S(1)}, bf16[2,128,2048]{2,1,0:T(8,128)(2,1)}, u32[]{:S(2)}) copy-start(bf16[2,128,2048]{2,1,0:T(8,128)(2,1)} %param.7) | copy-start | bytes 3145732
  40.1 2.1 %copy-start.1 = (bf16[32,64,1152]{2,1,0:T(8,128)(2,1)}, bf16[32,64,1152]{2,1,0:T(8,128)(2,1)S(1)}, u32[]{:S(2)}) copy-start(bf16[32,64,1152]{2,1,0:T(8,128)(2,1)S(1)} %get-tuple-element.10) | copy-start | bytes 14155780
  40.1 3.7 %copy-start = (bf16[32,64,1152]{2,1,0:T(8,128)(2,1)}, bf16[32,64,1152]{2,1,0:T(8,128)(2,1)S(1)}, u32[]{:S(2)}) copy-start(bf16[32,64,1152]{2,1,0:T(8,128)(2,1)S(1)} %get-tuple-element.11) | copy-start | bytes 14155780
  43.8 1.0 copy-start.2
  47.4 33.0 %copy-start.6 = (bf16[128,2048]{1,0:T(8,128)(2,1)S(1)}, bf16[128,2048]{1,0:T(8,128)(2,1)}, u32[]{:S(2)}) copy-start(bf16[128,2048]{1,0:T(8,128)(2,1)} %param.6) | copy-start | bytes 1572868
  91.1 8.3 %slice-start = ((s8[4718592]{0:T(1024)(128)(4,1)}), s8[524288]{0:T(1024)(128)(4,1)S(1)}, s32[]{:S(2)}) async-start(s8[4718592]{0:T(1024)(128)(4,1)} %bitcast.63), calls=%async_computation.2 | async-start | bytes 1048576
  94.1 5.4 %slice-start.1 = ((s8[4718592]{0:T(1024)(128)(4,1)}), s8[4194304]{0:T(1024)(128)(4,1)S(1)}, s32[]{:S(2)}) async-start(s8[4718592]{0:T(1024)(128)(4,1)} %bitcast.63), calls=%async_computation.3 | async-start | bytes 8388608
  102.3 1.3 %copy-start.3 = (f32[1152,256]{0,1:T(8,128)S(1)}, f32[1152,256]{0,1:T(8,128)}, u32[]{:S(2)}) copy-start(f32[1152,256]{0,1:T(8,128)} %copy-done.2) | copy-start | bytes 3538948
  102.3 1.6 %copy-start.4 = (f32[1152,256]{0,1:T(8,128)S(1)}, f32[1152,256]{0,1:T(8,128)}, u32[]{:S(2)}) copy-start(f32[1152,256]{0,1:T(8,128)} %get-tuple-element.23) | copy-start | bytes 3538948
Sparse Core Ops, SparseCore 0:
  9.6 81.4 all-gather.2

commit v3 on v2

--- a/solution.py
+++ b/solution.py
@@ -6,20 +6,20 @@
 from jax.sharding import PartitionSpec as P
 
 
-def basis_halves(pixels, columns):
-    lo_count = 64 if pixels % 64 == 0 else 1
-    hi_count = pixels // lo_count
-    u = jnp.arange(columns, dtype=jnp.int32)
+def dft_table(rows, columns, pixels):
+    lo_count = 64 if rows % 64 == 0 else 1
+    hi_count = rows // lo_count
+    c = jnp.arange(columns, dtype=jnp.int32)
     scale = 2.0 * math.pi / pixels
     hi = jnp.arange(hi_count, dtype=jnp.int32)
     lo = jnp.arange(lo_count, dtype=jnp.int32)
-    phase_hi = (hi[:, None] * lo_count * u[None, :] % pixels).astype(jnp.float32) * scale
-    phase_lo = (lo[:, None] * u[None, :] % pixels).astype(jnp.float32) * scale
+    phase_hi = (hi[:, None] * lo_count * c[None, :] % pixels).astype(jnp.float32) * scale
+    phase_lo = (lo[:, None] * c[None, :] % pixels).astype(jnp.float32) * scale
     c1, s1 = jnp.cos(phase_hi)[:, None, :], jnp.sin(phase_hi)[:, None, :]
     c2, s2 = jnp.cos(phase_lo)[None, :, :], jnp.sin(phase_lo)[None, :, :]
-    cos_t = (c1 * c2 - s1 * s2).reshape(pixels, columns).astype(jnp.bfloat16)
-    nsin_t = (-(s1 * c2 + c1 * s2)).reshape(pixels, columns).astype(jnp.bfloat16)
-    return cos_t, nsin_t
+    cos_t = (c1 * c2 - s1 * s2).reshape(rows, columns)
+    nsin_t = (-(s1 * c2 + c1 * s2)).reshape(rows, columns)
+    return cos_t.astype(jnp.bfloat16), nsin_t.astype(jnp.bfloat16)
 
 
 def shift_rows(frame_img, amount):
@@ -34,52 +34,61 @@
     steps = visit_order.shape[0]
     half = pixels // 2
     columns = min(pixels, half + 128)
-    cos_t, nsin_t = basis_halves(pixels, columns)
+    fwd_cos, fwd_sin = dft_table(pixels, columns, pixels)
+    forward = jnp.concatenate([fwd_cos, fwd_sin], axis=1)
+    inv_cos, inv_sin = dft_table(columns, pixels, pixels)
+    inverse = jnp.concatenate([inv_cos, inv_sin], axis=0)
     col = jnp.arange(columns, dtype=jnp.int32)
     weight = jnp.where((col == 0) | (col == half), 1.0, jnp.where(col < half, 2.0, 0.0))
 
-    gathered = lax.all_gather(reference_img, "stripe")
-    visited = jnp.take(gathered, visit_order, axis=0, mode="clip")
+    pieces = 2 if band_rows % 32 == 0 else 1
+    piece_rows = band_rows // pieces
+    gathered = [
+        lax.all_gather(reference_img[p * piece_rows : (p + 1) * piece_rows], "stripe")
+        for p in range(pieces)
+    ]
 
     frame_flat = frames.reshape(count_frames * band_rows, pixels)
-    spec_re = jnp.dot(frame_flat, cos_t, preferred_element_type=jnp.float32).reshape(
-        count_frames, band_rows, columns
+    spectra = jnp.dot(frame_flat, forward, preferred_element_type=jnp.float32).reshape(
+        count_frames, band_rows, 2 * columns
     )
-    spec_im = jnp.dot(frame_flat, nsin_t, preferred_element_type=jnp.float32).reshape(
-        count_frames, band_rows, columns
-    )
+    spec_re = spectra[:, :, :columns]
+    spec_im = spectra[:, :, columns:]
     frame_power = jnp.sum(spec_re * spec_re + spec_im * spec_im, axis=1)
 
-    visited_flat = visited.reshape(steps * band_rows, pixels)
-    band_re = (
-        jnp.dot(visited_flat, cos_t, preferred_element_type=jnp.float32)
-        .astype(jnp.bfloat16)
-        .astype(jnp.float32)
-        .reshape(steps, band_rows, columns)
-    )
-    band_im = (
-        jnp.dot(visited_flat, nsin_t, preferred_element_type=jnp.float32)
-        .astype(jnp.bfloat16)
-        .astype(jnp.float32)
-        .reshape(steps, band_rows, columns)
-    )
-    band_power = jnp.sum(band_re * band_re + band_im * band_im, axis=1)
-
-    fr = spec_re[:, None]
-    fi = spec_im[:, None]
-    br = band_re[None]
-    bi = band_im[None]
-    cross_re = jnp.sum(fr * br, axis=2) + jnp.sum(fi * bi, axis=2)
-    cross_im = jnp.sum(fi * br, axis=2) - jnp.sum(fr * bi, axis=2)
+    band_power = 0.0
+    cross_re = 0.0
+    cross_im = 0.0
+    for p in range(pieces):
+        visited = jnp.take(gathered[p], visit_order, axis=0, mode="clip")
+        band = (
+            jnp.dot(
+                visited.reshape(steps * piece_rows, pixels),
+                forward,
+                preferred_element_type=jnp.float32,
+            )
+            .astype(jnp.bfloat16)
+            .astype(jnp.float32)
+            .reshape(steps, piece_rows, 2 * columns)
+        )
+        band_re = band[:, :, :columns]
+        band_im = band[:, :, columns:]
+        band_power = band_power + jnp.sum(band_re * band_re + band_im * band_im, axis=1)
+        fr = spec_re[:, None, p * piece_rows : (p + 1) * piece_rows]
+        fi = spec_im[:, None, p * piece_rows : (p + 1) * piece_rows]
+        br = band_re[None]
+        bi = band_im[None]
+        cross_re = cross_re + (jnp.sum(fr * br, axis=2) + jnp.sum(fi * bi, axis=2))
+        cross_im = cross_im + (jnp.sum(fi * br, axis=2) - jnp.sum(fr * bi, axis=2))
     magnitude = jnp.sqrt(frame_power[:, None, :] * band_power[None, :, :] + 1e-06)
     coh_re = (cross_re / magnitude).astype(jnp.bfloat16).astype(jnp.float32) * weight
     coh_im = (cross_im / magnitude).astype(jnp.bfloat16).astype(jnp.float32) * weight
-    coh_re = coh_re.astype(jnp.bfloat16).reshape(count_frames * steps, columns)
-    coh_im = coh_im.astype(jnp.bfloat16).reshape(count_frames * steps, columns)
-    contract = (((1,), (1,)), ((), ()))
-    surface = lax.dot_general(
-        coh_re, cos_t, contract, preferred_element_type=jnp.float32
-    ) + lax.dot_general(coh_im, nsin_t, contract, preferred_element_type=jnp.float32)
+    coherence = jnp.concatenate([coh_re, coh_im], axis=2).astype(jnp.bfloat16)
+    surface = jnp.dot(
+        coherence.reshape(count_frames * steps, 2 * columns),
+        inverse,
+        preferred_element_type=jnp.float32,
+    )
     correlation = (surface * math.sqrt(band_rows / pixels)).reshape(count_frames, steps, pixels)
 
     num_devices = lax.axis_size("stripe") * lax.axis_size("frame")

time: 122 us -> 143 us (1.17)
  other arithmetic: 12.1 us -> 21.6 us
  waiting for transfers between devices: 39.4 us -> 47.2 us
  local copies, waits for them, and re-layouts: 15.9 us -> 19.8 us
    all_gather x1 -> x2, waiting for transfers between devices: 7.26 us -> 30.5 us  [per_device(): lax.all_gather(reference_img[p * piece_rows:(p + 1) * piece_rows], 'stripe')]
    all_to_all x1, waiting for transfers between devices: 31.5 us -> 16.2 us  [per_device(): lax.all_to_all(packed, ('stripe', 'frame'), split_axis=0, concat_axis=0,...]
    convert_element_type x2 -> x3, other arithmetic: 3.68 us -> 9.26 us  [the longest x2 9.21 us: dft_table(): return (cos_t.astype(jnp.bfloat16), nsin_t.astype(jnp.bfloat16))]
    slice x0 -> x4, local copies, waits for them, and re-layouts: none -> 4.86 us  [the longest x1 1.95 us: per_device(): reference_img[p * piece_rows:(p + 1) * piece_rows]]
    gather x1 -> x2, local copies, waits for them, and re-layouts: 2.93 us -> 5.39 us  [per_device(): visited = jnp.take(gathered[p], visit_order, axis=0, mode='clip')]
    unnamed x21 -> x23, local copies, waits for them, and re-layouts: 4.38 us -> 2.26 us
    sin x1 -> x2, other arithmetic: 1.16 us -> 3.2 us  [dft_table(): c2, s2 = (jnp.cos(phase_lo)[None, :, :], jnp.sin(phase_lo)[None, :, :])]
    dot_general x6 -> x4, matrix products: 19.6 us -> 20.2 us  [the longest x2 13 us: per_device(): jnp.dot(visited.reshape(steps * piece_rows, pixels), forward, preferred_e...]
  transfers between devices with their start and end apart: 2 -> 3, of which waited for: 2 -> 2; matrix products, arithmetic and copies ran while one was open for 22% -> 31% of each run, Pallas kernels for 0% -> 0%
where the time goes in v3:
time: 143 us
  waiting for transfers between devices  47.2 us (33%)
  matrix products  24.4 us (17%)
  other arithmetic  21.6 us (15%)
  local copies, waits for them, and re-layouts  19.8 us (14%)
  between operations  18.3 us (13%)
  starting transfers between devices  11.4 us (8%)
    all_gather x2, waiting for transfers between devices, per_device(): lax.all_gather(reference_img[p * piece_rows:(p + 1) * piece_rows], 'stripe')  30.5 us
    all_to_all x1, waiting for transfers between devices, per_device(): lax.all_to_all(packed, ('stripe', 'frame'), split_axis=0, concat_axis=0,...  16.2 us
    dot_general x2, matrix products, per_device(): jnp.dot(visited.reshape(steps * piece_rows, pixels), forward, preferred_e...  13 us
    all_to_all x1, starting transfers between devices, per_device(): lax.all_to_all(packed, ('stripe', 'frame'), split_axis=0, concat_axis=0,...  11.2 us
    convert_element_type x2, other arithmetic, dft_table(): return (cos_t.astype(jnp.bfloat16), nsin_t.astype(jnp.bfloat16))  9.21 us
    gather x2, local copies, waits for them, and re-layouts, per_device(): visited = jnp.take(gathered[p], visit_order, axis=0, mode='clip')  5.39 us
    dot_general x1, matrix products, per_device(): jnp.dot(coherence.reshape(count_frames * steps, 2 * columns), inverse, pr...  4.51 us
    dot_general x1, matrix products, per_device(): jnp.einsum('tps,psx->tx', hits.astype(jnp.bfloat16), incoming, preferred_...  3.48 us
  transfers between devices with their start and end apart: 3, of which 2 were waited for; matrix products, arithmetic and copies ran while one was open for 31% of the time, Pallas kernels for 0%

profile of v3, /device:TPU:0, one launch (start us, length us, event | category | flops | bytes accessed | tf_op | source)
XLA Modules:
  0.0 142.8 jit_solution(4921852858157830928)
XLA Ops:
  7.2 2.0 %fusion.72 = (bf16[64,2048]{1,0:T(8,128)(2,1)}, bf16[64,2048]{1,0:T(8,128)(2,1)}) fusion(bf16[128,2048]{1,0:T(8,128)(2,1)} %param.6), kind=kLoop, calls=%fused_computation.139 | loop fusion | bytes 1048576 | tf_op jit(solution)/shard_map/slice | solution.py:47
  9.2 1.3 fusion.73
  14.4 0.8 copy.21
  15.5 0.9 fusion.50
  16.4 0.7 multiply_add_fusion.1
  17.3 0.9 fusion.19
  18.4 0.9 fusion.20
  19.3 0.7 convolution_convert_fusion.2
  20.4 3.1 %copy.23 = bf16[128,4,2176]{2,1,0:T(4,128)(2,1)} copy(bf16[128,4,2176]{2,0,1:T(8,128)(2,1)S(1)} %pad_maximum_fusion.4) | data formatting | bytes 4456448 | tf_op jit(solution)/shard_map/concatenate | solution.py:116
  23.5 11.2 %all-to-all-start = ((bf16[128,4,2176]{2,1,0:T(4,128)(2,1)}), bf16[128,4,2176]{2,1,0:T(4,128)(2,1)S(1)}, u32[]{:S(2)}, u32[]{:S(2)}) async-start(bf16[128,4,2176]{2,1,0:T(4,128)(2,1)} %copy.23), calls=%async_computation | async-start | bytes 4456448 | tf_op jit(solution)/shard_map/all_to_all | solution.py:117
  35.4 1.2 fusion.44
  37.9 3.5 %subtract_convert_fusion.1 = (bf16[32,64,1152]{2,1,0:T(8,128)(2,1)S(1)}, bf16[32,64,1152]{2,1,0:T(8,128)(2,1)S(1)}) fusion(f32[64,1152]{1,0:T(8,128)S(1)} %get-tuple-element.42, f32[32,1152]{1,0:T(8,128)S(1)} %get-tuple-element.37, f32[64,1152]{1,0:T(8,128)S(1)} %get-tuple-element.43, f32[32,1152]{1,0:T(8,128)S(1)} %get-tuple-element.36), kind=kLoop, calls=%fused_computation.10 | loop fusion | flops 21233664 | bytes 10321920 | tf_op jit(solution)/shard_map/convert_element_type | solution.py:22
  41.4 2.7 %fusion.4 = f32[2304,256]{0,1:T(8,128)S(1)} fusion(bf16[256,2048]{1,0:T(8,128)(2,1)S(1)} %bitcast.63, bf16[2048,1152]{1,0:T(8,128)(2,1)S(1)} %bitcast.56, bf16[2048,1152]{1,0:T(8,128)(2,1)S(1)} %bitcast.53), kind=kOutput, calls=%fused_computation.14 | convolution fusion | flops 2434793472 | bytes 12845056 | tf_op jit(solution)/shard_map/dot_general | solution.py:52
  44.0 1.0 copy-done.1
  45.2 2.0 %fusion.33 = (f32[64,2048]{1,0:T(8,128)S(1)}, f32[64,2048]{1,0:T(8,128)S(1)}) fusion(), kind=kLoop, calls=%fused_computation.75 | loop fusion | flops 1835008 | bytes 1048576 | tf_op jit(solution)/shard_map/sin | solution.py:19
  47.2 0.8 fusion.54
  48.1 1.5 %fusion.69 = (f32[2,64,1152]{2,1,0:T(8,128)}, f32[2,64,1152]{2,1,0:T(8,128)}, f32[2,64,1152]{2,1,0:T(8,128)}, f32[2,64,1152]{2,1,0:T(8,128)}) fusion(f32[2,128,2304]{2,1,0:T(8,128)S(1)} %bitcast.52), kind=kLoop, calls=%fused_computation.136 | loop fusion | bytes 4718592 | tf_op jit(solution)/shard_map/slice | solution.py:78
  49.6 5.7 %subtract_convert_fusion = (bf16[18,64,2048]{2,1,0:T(8,128)(2,1)}, bf16[18,64,2048]{2,1,0:T(8,128)(2,1)}) fusion(f32[64,2048]{1,0:T(8,128)S(1)} %get-tuple-element.40, f32[18,2048]{1,0:T(8,128)S(1)} %get-tuple-element.39, f32[64,2048]{1,0:T(8,128)S(1)} %get-tuple-element.41, f32[18,2048]{1,0:T(8,128)S(1)} %get-tuple-element.38), kind=kLoop, calls=%fused_computation.8 | loop fusion | flops 21233664 | bytes 10780672 | tf_op jit(solution)/shard_map/convert_element_type | solution.py:22
  55.3 16.2 %all-to-all-done = bf16[128,4,2176]{2,1,0:T(4,128)(2,1)S(1)} async-done(((bf16[128,4,2176]{2,1,0:T(4,128)(2,1)}), bf16[128,4,2176]{2,1,0:T(4,128)(2,1)S(1)}, u32[]{:S(2)}, u32[]{:S(2)}) %all-to-all-start) | async-done | bytes 2228256 | tf_op jit(solution)/shard_map/all_to_all | solution.py:117
  71.7 1.2 slice.100
  73.1 3.5 %fusion.6 = f32[128,2048]{1,0:T(8,128)} fusion(bf16[128,4,2048]{2,1,0:T(4,128)(2,1)S(1)} %slice.100, bf16[128,2048]{1,0:T(8,128)(2,1)S(1)} %copy-done.8, f32[128]{0:T(128)S(1)} %broadcast_add_fusion, f32[128,4]{0,1:T(4,128)S(1)} %bitcast_convert_fusion), kind=kOutput, calls=%fused_computation.17 | convolution fusion | flops 269287424 | bytes 3672576 | tf_op jit(solution)/shard_map/tps,psx->tx/dot_general | solution.py:121
  76.6 2.2 %gather_fusion = bf16[4,64,2048]{2,1,0:T(8,128)(2,1)S(1)} fusion(bf16[8,64,2048]{2,1,0:T(8,128)(2,1)} %bitcast.64, s32[1024]{0:T(1024)S(1)} %pad_clamp_fusion), kind=kCustom, calls=%fused_computation | custom fusion | bytes 2097168 | tf_op jit(solution)/shard_map/jit(_take)/gather | solution.py:63
  78.8 6.4 %convolution_convert_fusion.1 = bf16[256,2304]{1,0:T(8,128)(2,1)S(1)} fusion(bf16[256,2048]{1,0:T(8,128)(2,1)S(1)} %bitcast.62, bf16[2048,1152]{1,0:T(8,128)(2,1)} %bitcast.57, bf16[2048,1152]{1,0:T(8,128)(2,1)} %bitcast.54), kind=kOutput, calls=%fused_computation.12 | convolution fusion | flops 2435383296 | bytes 11665408 | tf_op jit(solution)/shard_map/dot_general | solution.py:65
  85.2 1.2 fusion.70
  86.6 30.5 %all-gather.7.cloned.1.call-done = bf16[512,2048]{1,0:T(8,128)(2,1)} async-done(((bf16[64,2048]{1,0:T(8,128)(2,1)}), bf16[512,2048]{1,0:T(8,128)(2,1)}) %all-gather.7.cloned.1.call-update) | async-done | bytes 2097168 | tf_op jit(solution)/shard_map/all_gather | solution.py:47
  117.0 3.2 %gather_fusion.1 = bf16[4,64,2048]{2,1,0:T(8,128)(2,1)} fusion(bf16[8,64,2048]{2,1,0:T(8,128)(2,1)} %bitcast.65, s32[1024]{0:T(1024)S(1)} %pad_clamp_fusion), kind=kCustom, calls=%fused_computation.1 | custom fusion | bytes 2097168 | tf_op jit(solution)/shard_map/jit(_take)/gather | solution.py:63
  120.2 6.6 %convolution_convert_fusion = bf16[256,2304]{1,0:T(8,128)(2,1)S(1)} fusion(bf16[256,2048]{1,0:T(8,128)(2,1)} %bitcast.61, bf16[2048,1152]{1,0:T(8,128)(2,1)} %bitcast.58, bf16[2048,1152]{1,0:T(8,128)(2,1)} %bitcast.55), kind=kOutput, calls=%fused_computation.11 | convolution fusion | flops 2435383296 | bytes 11665408 | tf_op jit(solution)/shard_map/dot_general | solution.py:65
  127.7 0.8 copy-done.2
  128.9 0.9 multiply_reduce_fusion.7
  129.8 0.9 multiply_reduce_fusion.5
  130.8 4.5 %fusion.7 = f32[8,2048]{1,0:T(8,128)S(1)} fusion(bf16[1152,2048]{1,0:T(8,128)(2,1)} %bitcast.60, bf16[1152,2048]{1,0:T(8,128)(2,1)} %bitcast.59, bf16[8,1152]{1,0:T(8,128)(2,1)S(1)} %get-tuple-element.33, bf16[8,1152]{1,0:T(8,128)(2,1)S(1)} %get-tuple-element.32), kind=kOutput, calls=%fused_computation.27 | convolution fusion | flops 94461952 | bytes 9539584 | tf_op jit(solution)/shard_map/dot_general | solution.py:87
  135.3 0.7 reshape.367
  (58 shorter events, 5.0 us)
Async XLA Ops:
  7.2 11.1 %copy-start.7 = (bf16[2,128,2048]{2,1,0:T(8,128)(2,1)S(1)}, bf16[2,128,2048]{2,1,0:T(8,128)(2,1)}, u32[]{:S(2)}) copy-start(bf16[2,128,2048]{2,1,0:T(8,128)(2,1)} %param.7) | copy-start | bytes 3145732
  7.2 69.4 %all-gather.5.cloned.1.call-start = ((), (), s32[]{:S(2)}) async-start(), calls=%async_computation.1 | async-start | bytes 2359296 | tf_op jit(solution)/shard_map/all_gather | solution.py:47
  23.5 14.4 %copy-start.10 = (s32[4]{0:T(128)S(1)}, s32[4]{0:T(128)}, u32[]{:S(2)}) copy-start(s32[4]{0:T(128)} %param.11) | copy-start | bytes 52
  23.5 48.1 %all-to-all-start = ((bf16[128,4,2176]{2,1,0:T(4,128)(2,1)}), bf16[128,4,2176]{2,1,0:T(4,128)(2,1)S(1)}, u32[]{:S(2)}, u32[]{:S(2)}) async-start(bf16[128,4,2176]{2,1,0:T(4,128)(2,1)} %copy.23), calls=%async_computation | async-start | bytes 4456448 | tf_op jit(solution)/shard_map/all_to_all | solution.py:117
  34.7 82.4 %all-gather.7.cloned.1.call-start = ((), (), s32[]{:S(2)}) async-start(), calls=%async_computation.2 | async-start | bytes 2359296 | tf_op jit(solution)/shard_map/all_gather | solution.py:47
  41.3 2.7 %copy-start = (bf16[32,64,1152]{2,1,0:T(8,128)(2,1)}, bf16[32,64,1152]{2,1,0:T(8,128)(2,1)S(1)}, u32[]{:S(2)}) copy-start(bf16[32,64,1152]{2,1,0:T(8,128)(2,1)S(1)} %get-tuple-element.26) | copy-start | bytes 14155780
  41.3 3.7 %copy-start.1 = (bf16[32,64,1152]{2,1,0:T(8,128)(2,1)}, bf16[32,64,1152]{2,1,0:T(8,128)(2,1)S(1)}, u32[]{:S(2)}) copy-start(bf16[32,64,1152]{2,1,0:T(8,128)(2,1)S(1)} %get-tuple-element.27) | copy-start | bytes 14155780
  55.3 17.7 %copy-start.8 = (bf16[128,2048]{1,0:T(8,128)(2,1)S(1)}, bf16[128,2048]{1,0:T(8,128)(2,1)}, u32[]{:S(2)}) copy-start(bf16[128,2048]{1,0:T(8,128)(2,1)} %param.6) | copy-start | bytes 1572868
  127.3 1.3 copy-start.2
  127.3 1.4 copy-start.5
  127.3 1.6 %copy-start.6 = (f32[2,64,1152]{2,1,0:T(8,128)S(1)}, f32[2,64,1152]{2,1,0:T(8,128)}, u32[]{:S(2)}) copy-start(f32[2,64,1152]{2,1,0:T(8,128)} %get-tuple-element.17) | copy-start | bytes 1769476
  127.7 2.1 %copy-start.3 = (f32[2,64,1152]{2,1,0:T(8,128)S(1)}, f32[2,64,1152]{2,1,0:T(8,128)}, u32[]{:S(2)}) copy-start(f32[2,64,1152]{2,1,0:T(8,128)} %get-tuple-element.15) | copy-start | bytes 1769476
  127.7 2.1 %copy-start.4 = (f32[2,64,1152]{2,1,0:T(8,128)S(1)}, f32[2,64,1152]{2,1,0:T(8,128)}, u32[]{:S(2)}) copy-start(f32[2,64,1152]{2,1,0:T(8,128)} %get-tuple-element.16) | copy-start | bytes 1769476
  129.8 1.0 copy-start.9
Sparse Core Ops, SparseCore 0:
  9.6 64.9 all-gather.4
  76.3 40.7 all-gather.6

commit v4 on v3

--- a/solution.py
+++ b/solution.py
@@ -32,6 +32,7 @@
 def per_device(reference_img, frames, shifts, dest_device, dest_row, visit_order):
     count_frames, band_rows, pixels = frames.shape
     steps = visit_order.shape[0]
+    stripes = lax.axis_size("stripe")
     half = pixels // 2
     columns = min(pixels, half + 128)
     fwd_cos, fwd_sin = dft_table(pixels, columns, pixels)
@@ -41,45 +42,53 @@
     col = jnp.arange(columns, dtype=jnp.int32)
     weight = jnp.where((col == 0) | (col == half), 1.0, jnp.where(col < half, 2.0, 0.0))
 
-    pieces = 2 if band_rows % 32 == 0 else 1
-    piece_rows = band_rows // pieces
-    gathered = [
-        lax.all_gather(reference_img[p * piece_rows : (p + 1) * piece_rows], "stripe")
-        for p in range(pieces)
-    ]
+    chunk = band_rows // stripes
+    frame_part = frames.reshape(count_frames, stripes, chunk, pixels).transpose(1, 0, 2, 3)
+    frame_part = frame_part.reshape(stripes, count_frames * chunk, pixels)
+    band_part = reference_img.reshape(stripes, chunk, pixels)
+    outbound = jnp.concatenate([frame_part, band_part], axis=1)
+    inbound = lax.all_to_all(outbound, "stripe", split_axis=0, concat_axis=0, tiled=True)
+    frame_rows_in = inbound[:, : count_frames * chunk].reshape(stripes * count_frames * chunk, pixels)
+    band_in = inbound[:, count_frames * chunk :]
+    visited = jnp.take(band_in, visit_order, axis=0, mode="clip").reshape(steps * chunk, pixels)
 
-    frame_flat = frames.reshape(count_frames * band_rows, pixels)
-    spectra = jnp.dot(frame_flat, forward, preferred_element_type=jnp.float32).reshape(
-        count_frames, band_rows, 2 * columns
+    spectra = jnp.dot(frame_rows_in, forward, preferred_element_type=jnp.float32).reshape(
+        stripes, count_frames, 1, chunk, 2 * columns
     )
-    spec_re = spectra[:, :, :columns]
-    spec_im = spectra[:, :, columns:]
-    frame_power = jnp.sum(spec_re * spec_re + spec_im * spec_im, axis=1)
+    spec_re = spectra[..., :columns]
+    spec_im = spectra[..., columns:]
+    band = (
+        jnp.dot(visited, forward, preferred_element_type=jnp.float32)
+        .astype(jnp.bfloat16)
+        .astype(jnp.float32)
+        .reshape(steps, chunk, 2 * columns)
+    )
+    band_re = band[..., :columns]
+    band_im = band[..., columns:]
+    frame_power = jnp.sum(spec_re * spec_re + spec_im * spec_im, axis=3)[:, :, 0]
+    band_power = jnp.sum(band_re * band_re + band_im * band_im, axis=1)
+    br = band_re[None, None]
+    bi = band_im[None, None]
+    cross_re = jnp.sum(spec_re * br, axis=3) + jnp.sum(spec_im * bi, axis=3)
+    cross_im = jnp.sum(spec_im * br, axis=3) - jnp.sum(spec_re * bi, axis=3)
+    partial = jnp.concatenate(
+        [
+            cross_re.reshape(stripes, count_frames * steps, columns),
+            cross_im.reshape(stripes, count_frames * steps, columns),
+            frame_power,
+            jnp.broadcast_to(band_power[None], (stripes, steps, columns)),
+        ],
+        axis=1,
+    )
+    total = jnp.sum(
+        lax.all_to_all(partial, "stripe", split_axis=0, concat_axis=0, tiled=True), axis=0
+    )
+    pairs = count_frames * steps
+    cross_re = total[:pairs].reshape(count_frames, steps, columns)
+    cross_im = total[pairs : 2 * pairs].reshape(count_frames, steps, columns)
+    frame_power = total[2 * pairs : 2 * pairs + count_frames]
+    band_power = total[2 * pairs + count_frames :]
 
-    band_power = 0.0
-    cross_re = 0.0
-    cross_im = 0.0
-    for p in range(pieces):
-        visited = jnp.take(gathered[p], visit_order, axis=0, mode="clip")
-        band = (
-            jnp.dot(
-                visited.reshape(steps * piece_rows, pixels),
-                forward,
-                preferred_element_type=jnp.float32,
-            )
-            .astype(jnp.bfloat16)
-            .astype(jnp.float32)
-            .reshape(steps, piece_rows, 2 * columns)
-        )
-        band_re = band[:, :, :columns]
-        band_im = band[:, :, columns:]
-        band_power = band_power + jnp.sum(band_re * band_re + band_im * band_im, axis=1)
-        fr = spec_re[:, None, p * piece_rows : (p + 1) * piece_rows]
-        fi = spec_im[:, None, p * piece_rows : (p + 1) * piece_rows]
-        br = band_re[None]
-        bi = band_im[None]
-        cross_re = cross_re + (jnp.sum(fr * br, axis=2) + jnp.sum(fi * bi, axis=2))
-        cross_im = cross_im + (jnp.sum(fi * br, axis=2) - jnp.sum(fr * bi, axis=2))
     magnitude = jnp.sqrt(frame_power[:, None, :] * band_power[None, :, :] + 1e-06)
     coh_re = (cross_re / magnitude).astype(jnp.bfloat16).astype(jnp.float32) * weight
     coh_im = (cross_im / magnitude).astype(jnp.bfloat16).astype(jnp.float32) * weight

time: 143 us -> 124 us (0.87); the launches traced: 143 us -> 122 us
  waiting for transfers between devices: 47.2 us -> 30.9 us
  between operations: 18.3 us -> 4.85 us
  other arithmetic: 21.6 us -> 33.7 us
  starting transfers between devices: 11.4 us -> 18.7 us
  local copies, waits for them, and re-layouts: 19.8 us -> 13.2 us
  matrix products: 24.4 us -> 20.8 us
    all_gather x2 -> x0, waiting for transfers between devices: 30.5 us -> none  [per_device(): lax.all_gather(reference_img[p * piece_rows:(p + 1) * piece_rows], 'stripe')]
    all_to_all x0 -> x2, waiting for transfers between devices: none -> 13.3 us  [the longest x1 8.94 us: per_device(): lax.all_to_all(partial, 'stripe', split_axis=0, concat_axis=0, tiled=True)]
    all_to_all x0 -> x2, starting transfers between devices: none -> 9.14 us  [the longest x1 5.51 us: per_device(): lax.all_to_all(outbound, 'stripe', split_axis=0, concat_axis=0, tiled=True)]
    reduce_sum x5 -> x3, other arithmetic: 2.34 us -> 7.27 us  [the longest x1 6.09 us: per_device(): cross_re = jnp.sum(spec_re * br, axis=3) + jnp.sum(spec_im * bi, axis=3)]
    dot_general x3 -> x2, matrix products: 15.7 us -> 12 us  [the longest x1 6.4 us: per_device(): jnp.dot(frame_rows_in, forward, preferred_element_type=jnp.float32)]
    convert_element_type x2, other arithmetic: 9.21 us -> 12.6 us  [dft_table(): return (cos_t.astype(jnp.bfloat16), nsin_t.astype(jnp.bfloat16))]
    concatenate x0 -> x2, other arithmetic: none -> 3.31 us  [the longest x1 2.31 us: per_device(): outbound = jnp.concatenate([frame_part, band_part], axis=1)]
    gather x2 -> x1, local copies, waits for them, and re-layouts: 5.39 us -> 2.31 us  [per_device(): jnp.take(band_in, visit_order, axis=0, mode='clip')]
  transfers between devices with their start and end apart: 3 -> 3, of which waited for: 2 -> 3; matrix products, arithmetic and copies ran while one was open for 31% -> 24% of each run, Pallas kernels for 0% -> 0%
where the time goes in v4:
time: 124 us; the launch traced here: 122 us
  other arithmetic  33.7 us (27%)
  waiting for transfers between devices  30.9 us (25%)
  matrix products  20.8 us (17%)
  starting transfers between devices  18.7 us (15%)
  local copies, waits for them, and re-layouts  13.2 us (11%)
  between operations  4.85 us (4%)
    all_to_all x1, waiting for transfers between devices, per_device(): lax.all_to_all(packed, ('stripe', 'frame'), split_axis=0, concat_axis=0,...  17.7 us
    convert_element_type x2, other arithmetic, dft_table(): return (cos_t.astype(jnp.bfloat16), nsin_t.astype(jnp.bfloat16))  12.6 us
    all_to_all x1, starting transfers between devices, per_device(): lax.all_to_all(packed, ('stripe', 'frame'), split_axis=0, concat_axis=0,...  9.58 us
    all_to_all x1, waiting for transfers between devices, per_device(): lax.all_to_all(partial, 'stripe', split_axis=0, concat_axis=0, tiled=True)  8.94 us
    dot_general x1, matrix products, per_device(): jnp.dot(frame_rows_in, forward, preferred_element_type=jnp.float32)  6.4 us
    reduce_sum x1, other arithmetic, per_device(): cross_re = jnp.sum(spec_re * br, axis=3) + jnp.sum(spec_im * bi, axis=3)  6.09 us
    dot_general x1, matrix products, per_device(): jnp.dot(visited, forward, preferred_element_type=jnp.float32)  5.65 us
    all_to_all x1, starting transfers between devices, per_device(): lax.all_to_all(outbound, 'stripe', split_axis=0, concat_axis=0, tiled=True)  5.51 us
  transfers between devices with their start and end apart: 3, of which 3 were waited for; matrix products, arithmetic and copies ran while one was open for 24% of the time, Pallas kernels for 0%

profile of v4, /device:TPU:0, one launch (start us, length us, event | category | flops | bytes accessed | tf_op | source)
XLA Modules:
  0.0 122.3 jit_solution(14726871426248038632)
XLA Ops:
  0.6 1.4 %copy.34 = bf16[8,2,16,2048]{3,2,1,0:T(8,128)(2,1)S(1)} copy(bf16[8,2,16,2048]{3,2,0,1:T(8,128)(2,1)} %bitcast.64) | data formatting | bytes 2097152 | tf_op jit(solution)/shard_map/transpose | solution.py:46
  2.1 2.3 %pad_maximum_fusion.6 = bf16[8,48,2048]{2,1,0:T(8,128)(2,1)} fusion(bf16[8,16,2048]{2,1,0:T(8,128)(2,1)} %bitcast.67, bf16[8,32,2048]{2,1,0:T(8,128)(2,1)S(1)} %bitcast.63), kind=kLoop, calls=%fused_computation.26 | loop fusion | flops 3145728 | bytes 3145728 | tf_op jit(solution)/shard_map/concatenate | solution.py:49
  4.4 5.5 %all-to-all-start = ((bf16[8,48,2048]{2,1,0:T(8,128)(2,1)}), bf16[8,48,2048]{2,1,0:T(8,128)(2,1)}, u32[]{:S(2)}, u32[]{:S(2)}) async-start(bf16[8,48,2048]{2,1,0:T(8,128)(2,1)} %pad_maximum_fusion.6), calls=%async_computation | async-start | bytes 3145728 | tf_op jit(solution)/shard_map/all_to_all | solution.py:50
  14.5 1.2 fusion.48
  16.9 0.9 fusion.24
  17.8 0.7 convolution_convert_fusion
  18.6 0.7 fusion.60
  19.2 6.9 %subtract_convert_fusion.1 = (bf16[32,64,1152]{2,1,0:T(8,128)(2,1)}, bf16[32,64,1152]{2,1,0:T(8,128)(2,1)}) fusion(f32[64,1152]{1,0:T(8,128)S(1)} %get-tuple-element.29, f32[32,1152]{1,0:T(8,128)S(1)} %get-tuple-element.24, f32[64,1152]{1,0:T(8,128)S(1)} %get-tuple-element.30, f32[32,1152]{1,0:T(8,128)S(1)} %get-tuple-element.23), kind=kLoop, calls=%fused_computation.11 | loop fusion | flops 21233664 | bytes 10321920 | tf_op jit(solution)/shard_map/convert_element_type | solution.py:22
  26.1 4.3 %all-to-all-done = bf16[8,48,2048]{2,1,0:T(8,128)(2,1)} async-done(((bf16[8,48,2048]{2,1,0:T(8,128)(2,1)}), bf16[8,48,2048]{2,1,0:T(8,128)(2,1)}, u32[]{:S(2)}, u32[]{:S(2)}) %all-to-all-start) | async-done | bytes 1572896 | tf_op jit(solution)/shard_map/all_to_all | solution.py:50
  30.4 1.3 %slice.74 = bf16[8,32,2048]{2,1,0:T(8,128)(2,1)S(1)} slice(bf16[8,48,2048]{2,1,0:T(8,128)(2,1)} %all-to-all-done), slice={[0:8], [0:32], [0:2048]} | slice | bytes 2097152 | tf_op jit(solution)/shard_map/slice | solution.py:51
  31.7 6.4 %fusion.7 = f32[8,2,1,16,2304]{4,3,1,0,2:T(8,128)S(1)} fusion(bf16[8,2,16,2048]{3,2,1,0:T(8,128)(2,1)S(1)} %bitcast.66, bf16[2048,1152]{1,0:T(8,128)(2,1)} %bitcast.59, bf16[2048,1152]{1,0:T(8,128)(2,1)} %bitcast.57), kind=kOutput, calls=%fused_computation.17 | convolution fusion | flops 2434793472 | bytes 12845056 | tf_op jit(solution)/shard_map/dot_general | solution.py:55
  38.1 1.4 %slice_bitcast_fusion = (f32[8,2,16,1152]{3,2,1,0:T(8,128)S(1)}, f32[8,2,1152]{2,1,0:T(2,128)S(1)}, f32[8,2,16,1152]{3,2,1,0:T(8,128)}) fusion(f32[8,2,1,16,2304]{4,3,1,0,2:T(8,128)S(1)} %fusion.7), kind=kLoop, calls=%fused_computation.28 | loop fusion | flops 1161216 | bytes 4792320 | tf_op jit(solution)/shard_map/mul | solution.py:72
  39.5 1.9 %slice.76 = bf16[8,16,2048]{2,1,0:T(8,128)(2,1)} slice(bf16[8,48,2048]{2,1,0:T(8,128)(2,1)} %all-to-all-done), slice={[0:8], [32:48], [0:2048]} | slice | bytes 1048576 | tf_op jit(solution)/shard_map/slice | solution.py:52
  41.4 2.3 %gather_fusion = bf16[4,16,2048]{2,1,0:T(8,128)(2,1)} fusion(bf16[8,16,2048]{2,1,0:T(8,128)(2,1)} %slice.76, s32[1024]{0:T(1024)S(1)} %pad_clamp_fusion), kind=kCustom, calls=%fused_computation | custom fusion | bytes 524304 | tf_op jit(solution)/shard_map/jit(_take)/gather | solution.py:53
  43.7 5.6 %fusion.10 = bf16[64,2304]{1,0:T(8,128)(2,1)S(1)} fusion(bf16[64,2048]{1,0:T(8,128)(2,1)} %bitcast.68, bf16[2048,1152]{1,0:T(8,128)(2,1)} %bitcast.60, bf16[2048,1152]{1,0:T(8,128)(2,1)} %bitcast.58), kind=kOutput, calls=%fused_computation.18 | convolution fusion | flops 623001600 | bytes 9994240 | tf_op jit(solution)/shard_map/dot_general | solution.py:61
  49.4 0.9 bitcast_convert_fusion.1
  50.3 6.1 %multiply_reduce_fusion.3 = (f32[8,2,4,1152]{3,2,1,0:T(4,128)S(1)}, f32[8,2,4,1152]{3,2,1,0:T(4,128)}, f32[8,2,4,1152]{3,2,1,0:T(4,128)}, f32[8,2,4,1152]{3,2,1,0:T(4,128)S(1)}) fusion(f32[4,16,1152]{2,1,0:T(8,128)S(1)} %get-tuple-element.18, f32[8,2,16,1152]{3,2,1,0:T(8,128)S(1)} %copy-done, f32[4,16,1152]{2,1,0:T(8,128)S(1)} %get-tuple-element.17, ...), kind=kLoop, calls=%fused_computation.16 | loop fusion | flops 9142272 | bytes 4128768 | tf_op jit(solution)/shard_map/reduce_sum | solution.py:72
  56.6 1.1 sub.32
  57.8 1.1 add_reduce_fusion.1
  59.0 1.0 pad_maximum_fusion.7
  60.0 3.6 %all-to-all-start.1 = ((f32[8,22,1152]{2,1,0:T(8,128)}), f32[8,22,1152]{2,1,0:T(8,128)S(1)}, u32[]{:S(2)}, u32[]{:S(2)}) async-start(f32[8,22,1152]{2,1,0:T(8,128)} %pad_maximum_fusion.7), calls=%async_computation.1 | async-start | bytes 1769472 | tf_op jit(solution)/shard_map/all_to_all | solution.py:84
  64.0 3.1 %copy.38 = bf16[128,4,2176]{2,1,0:T(4,128)(2,1)} copy(bf16[128,4,2176]{2,0,1:T(8,128)(2,1)S(1)} %pad_maximum_fusion.5) | data formatting | bytes 4456448 | tf_op jit(solution)/shard_map/concatenate | solution.py:125
  67.1 0.8 fusion.58
  67.9 8.9 %all-to-all-done.1 = f32[8,22,1152]{2,1,0:T(8,128)S(1)} async-done(((f32[8,22,1152]{2,1,0:T(8,128)}), f32[8,22,1152]{2,1,0:T(8,128)S(1)}, u32[]{:S(2)}, u32[]{:S(2)}) %all-to-all-start.1) | async-done | bytes 811040 | tf_op jit(solution)/shard_map/all_to_all | solution.py:84
  76.9 9.6 %all-to-all-start.2 = ((bf16[128,4,2176]{2,1,0:T(4,128)(2,1)}), bf16[128,4,2176]{2,1,0:T(4,128)(2,1)S(1)}, u32[]{:S(2)}, u32[]{:S(2)}) async-start(bf16[128,4,2176]{2,1,0:T(4,128)(2,1)} %copy.38), calls=%async_computation.2 | async-start | bytes 4456448 | tf_op jit(solution)/shard_map/all_to_all | solution.py:126
  86.4 2.0 %fusion.37 = (f32[64,2048]{1,0:T(8,128)S(1)}, f32[64,2048]{1,0:T(8,128)S(1)}) fusion(), kind=kLoop, calls=%fused_computation.72 | loop fusion | flops 1835008 | bytes 1048576 | tf_op jit(solution)/shard_map/sin | solution.py:19
  88.5 5.8 %subtract_convert_fusion = (bf16[18,64,2048]{2,1,0:T(8,128)(2,1)}, bf16[18,64,2048]{2,1,0:T(8,128)(2,1)}) fusion(f32[64,2048]{1,0:T(8,128)S(1)} %get-tuple-element.27, f32[18,2048]{1,0:T(8,128)S(1)} %get-tuple-element.26, f32[64,2048]{1,0:T(8,128)S(1)} %get-tuple-element.28, f32[18,2048]{1,0:T(8,128)S(1)} %get-tuple-element.25), kind=kLoop, calls=%fused_computation.9 | loop fusion | flops 21233664 | bytes 10780672 | tf_op jit(solution)/shard_map/convert_element_type | solution.py:22
  94.4 4.5 %fusion.13 = f32[8,2048]{1,0:T(8,128)S(1)} fusion(bf16[1152,2048]{1,0:T(8,128)(2,1)} %bitcast.62, bf16[1152,2048]{1,0:T(8,128)(2,1)} %bitcast.61, bf16[8,1152]{1,0:T(8,128)(2,1)S(1)} %get-tuple-element.20, bf16[8,1152]{1,0:T(8,128)(2,1)S(1)} %get-tuple-element.19), kind=kOutput, calls=%fused_computation.24 | convolution fusion | flops 94461952 | bytes 9539584 | tf_op jit(solution)/shard_map/dot_general | solution.py:96
  98.9 0.7 reshape.354
  99.6 17.7 %all-to-all-done.2 = bf16[128,4,2176]{2,1,0:T(4,128)(2,1)S(1)} async-done(((bf16[128,4,2176]{2,1,0:T(4,128)(2,1)}), bf16[128,4,2176]{2,1,0:T(4,128)(2,1)S(1)}, u32[]{:S(2)}, u32[]{:S(2)}) %all-to-all-start.2) | async-done | bytes 2228256 | tf_op jit(solution)/shard_map/all_to_all | solution.py:126
  117.6 1.2 slice.86
  118.8 3.5 %fusion.12 = f32[128,2048]{1,0:T(8,128)} fusion(bf16[128,4,2048]{2,1,0:T(4,128)(2,1)S(1)} %slice.86, bf16[128,2048]{1,0:T(8,128)(2,1)S(1)} %copy-done.2, f32[128]{0:T(128)S(1)} %broadcast_add_fusion, f32[128,4]{0,1:T(4,128)S(1)} %bitcast_convert_fusion), kind=kOutput, calls=%fused_computation.22 | convolution fusion | flops 269287424 | bytes 3672576 | tf_op jit(solution)/shard_map/tps,psx->tx/dot_general | solution.py:130
  (51 shorter events, 3.0 us)
Async XLA Ops:
  0.6 13.8 %copy-start.1 = (bf16[2,128,2048]{2,1,0:T(8,128)(2,1)S(1)}, bf16[2,128,2048]{2,1,0:T(8,128)(2,1)}, u32[]{:S(2)}) copy-start(bf16[2,128,2048]{2,1,0:T(8,128)(2,1)} %param.7) | copy-start | bytes 3145732
  0.6 9.3 %copy-start.4 = (s32[2]{0:T(128)S(1)}, s32[2]{0:T(128)}, u32[]{:S(2)}) copy-start(s32[2]{0:T(128)} %param.8) | copy-start | bytes 28
  2.0 13.6 %copy-start.3 = (s32[256,1]{0,1:T(1,128)S(1)}, s32[256,1]{0,1:T(1,128)}, u32[]{:S(2)}) copy-start(s32[256,1]{0,1:T(1,128)} %param.9) | copy-start | bytes 3076
  2.1 14.5 %copy-start.5 = (s32[256]{0:T(256)S(1)}, s32[256]{0:T(256)}, u32[]{:S(2)}) copy-start(s32[256]{0:T(256)} %param.10) | copy-start | bytes 3076
  2.1 14.8 %copy-start.6 = (s32[4]{0:T(128)S(1)}, s32[4]{0:T(128)}, u32[]{:S(2)}) copy-start(s32[4]{0:T(128)} %param.11) | copy-start | bytes 52
  4.4 26.0 %all-to-all-start = ((bf16[8,48,2048]{2,1,0:T(8,128)(2,1)}), bf16[8,48,2048]{2,1,0:T(8,128)(2,1)}, u32[]{:S(2)}, u32[]{:S(2)}) async-start(bf16[8,48,2048]{2,1,0:T(8,128)(2,1)} %pad_maximum_fusion.6), calls=%async_computation | async-start | bytes 3145728 | tf_op jit(solution)/shard_map/all_to_all | solution.py:50
  43.7 6.6 %copy-start = (f32[8,2,16,1152]{3,2,1,0:T(8,128)S(1)}, f32[8,2,16,1152]{3,2,1,0:T(8,128)}, u32[]{:S(2)}) copy-start(f32[8,2,16,1152]{3,2,1,0:T(8,128)} %get-tuple-element.10) | copy-start | bytes 3538948
  60.0 16.9 %all-to-all-start.1 = ((f32[8,22,1152]{2,1,0:T(8,128)}), f32[8,22,1152]{2,1,0:T(8,128)S(1)}, u32[]{:S(2)}, u32[]{:S(2)}) async-start(f32[8,22,1152]{2,1,0:T(8,128)} %pad_maximum_fusion.7), calls=%async_computation.1 | async-start | bytes 1769472 | tf_op jit(solution)/shard_map/all_to_all | solution.py:84
  76.9 40.4 %all-to-all-start.2 = ((bf16[128,4,2176]{2,1,0:T(4,128)(2,1)}), bf16[128,4,2176]{2,1,0:T(4,128)(2,1)S(1)}, u32[]{:S(2)}, u32[]{:S(2)}) async-start(bf16[128,4,2176]{2,1,0:T(4,128)(2,1)} %copy.38), calls=%async_computation.2 | async-start | bytes 4456448 | tf_op jit(solution)/shard_map/all_to_all | solution.py:126
  98.9 19.8 %copy-start.2 = (bf16[128,2048]{1,0:T(8,128)(2,1)S(1)}, bf16[128,2048]{1,0:T(8,128)(2,1)}, u32[]{:S(2)}) copy-start(bf16[128,2048]{1,0:T(8,128)(2,1)} %param.6) | copy-start | bytes 1572868

commit v5 on v4

--- a/solution.py
+++ b/solution.py
@@ -29,6 +29,26 @@
     return lax.dynamic_slice_in_dim(doubled, start, pixels, axis=1)
 
 
+def stripe_exchange(blocks, axis):
+    count = blocks.shape[0]
+    me = lax.axis_index(axis)
+    received = [lax.dynamic_index_in_dim(blocks, me, 0, keepdims=False)]
+    for d in range(1, count):
+        outgoing = lax.dynamic_index_in_dim(blocks, lax.rem(me + d, count), 0, keepdims=False)
+        pairs = [(i, (i + d) % count) for i in range(count)]
+        received.append(lax.ppermute(outgoing, axis, pairs))
+    return jnp.stack(received)
+
+
+def stripe_return(blocks, axis):
+    count = blocks.shape[0]
+    total = blocks[0]
+    for d in range(1, count):
+        pairs = [(i, (i - d) % count) for i in range(count)]
+        total = total + lax.ppermute(blocks[d], axis, pairs)
+    return total
+
+
 def per_device(reference_img, frames, shifts, dest_device, dest_row, visit_order):
     count_frames, band_rows, pixels = frames.shape
     steps = visit_order.shape[0]
@@ -47,10 +67,11 @@
     frame_part = frame_part.reshape(stripes, count_frames * chunk, pixels)
     band_part = reference_img.reshape(stripes, chunk, pixels)
     outbound = jnp.concatenate([frame_part, band_part], axis=1)
-    inbound = lax.all_to_all(outbound, "stripe", split_axis=0, concat_axis=0, tiled=True)
+    inbound = stripe_exchange(outbound, "stripe")
     frame_rows_in = inbound[:, : count_frames * chunk].reshape(stripes * count_frames * chunk, pixels)
     band_in = inbound[:, count_frames * chunk :]
-    visited = jnp.take(band_in, visit_order, axis=0, mode="clip").reshape(steps * chunk, pixels)
+    source = lax.rem(lax.axis_index("stripe") - visit_order + stripes, stripes)
+    visited = jnp.take(band_in, source, axis=0, mode="clip").reshape(steps * chunk, pixels)
 
     spectra = jnp.dot(frame_rows_in, forward, preferred_element_type=jnp.float32).reshape(
         stripes, count_frames, 1, chunk, 2 * columns
@@ -80,9 +101,7 @@
         ],
         axis=1,
     )
-    total = jnp.sum(
-        lax.all_to_all(partial, "stripe", split_axis=0, concat_axis=0, tiled=True), axis=0
-    )
+    total = stripe_return(partial, "stripe")
     pairs = count_frames * steps
     cross_re = total[:pairs].reshape(count_frames, steps, columns)
     cross_im = total[pairs : 2 * pairs].reshape(count_frames, steps, columns)

time: 124 us -> 132 us (1.065)
  starting transfers between devices: 18.7 us -> 34.9 us
  waiting for transfers between devices: 30.9 us -> 21.2 us
  local copies, waits for them, and re-layouts: 13.2 us -> 18.3 us
  matrix products: 20.8 us -> 17.1 us
  other arithmetic: 33.7 us -> 35.2 us
    ppermute x0 -> x14, starting transfers between devices: none -> 25.3 us  [the longest x7 13.7 us: stripe_exchange(): received.append(lax.ppermute(outgoing, axis, pairs))]
    ppermute x0 -> x14, waiting for transfers between devices: none -> 21.2 us  [the longest x7 14.4 us: stripe_exchange(): received.append(lax.ppermute(outgoing, axis, pairs))]
    all_to_all x1, waiting for transfers between devices: 17.7 us -> 0.01 us  [per_device(): lax.all_to_all(packed, ('stripe', 'frame'), split_axis=0, concat_axis=0,...]
    all_to_all x2 -> x0, waiting for transfers between devices: 13.3 us -> none  [the longest x1 8.94 us: per_device(): lax.all_to_all(partial, 'stripe', split_axis=0, concat_axis=0, tiled=True)]
    all_to_all x2 -> x0, starting transfers between devices: 9.14 us -> none  [the longest x1 5.51 us: per_device(): lax.all_to_all(outbound, 'stripe', split_axis=0, concat_axis=0, tiled=True)]
    unnamed x15 -> x37, local copies, waits for them, and re-layouts: 0.15 us -> 3.98 us
    dot_general x1, matrix products: 6.4 us -> 2.66 us  [per_device(): jnp.dot(frame_rows_in, forward, preferred_element_type=jnp.float32)]
    squeeze x0 -> x2, other arithmetic: none -> 2.65 us  [stripe_exchange(): lax.dynamic_index_in_dim(blocks, lax.rem(me + d, count), 0, keepdims=False)]
  transfers between devices with their start and end apart: 3 -> 15, of which waited for: 3 -> 5; matrix products, arithmetic and copies ran while one was open for 24% -> 47% of each run, Pallas kernels for 0% -> 0%
where the time goes in v5:
time: 132 us
  other arithmetic  35.2 us (27%)
  starting transfers between devices  34.9 us (26%)
  waiting for transfers between devices  21.2 us (16%)
  local copies, waits for them, and re-layouts  18.3 us (14%)
  matrix products  17.1 us (13%)
  between operations  4.97 us (4%)
    ppermute x7, waiting for transfers between devices, stripe_exchange(): received.append(lax.ppermute(outgoing, axis, pairs))  14.4 us
    ppermute x7, starting transfers between devices, stripe_exchange(): received.append(lax.ppermute(outgoing, axis, pairs))  13.7 us
    ppermute x7, starting transfers between devices, stripe_return(): total = total + lax.ppermute(blocks[d], axis, pairs)  11.6 us
    convert_element_type x2, other arithmetic, dft_table(): return (cos_t.astype(jnp.bfloat16), nsin_t.astype(jnp.bfloat16))  10.1 us
    all_to_all x1, starting transfers between devices, per_device(): lax.all_to_all(packed, ('stripe', 'frame'), split_axis=0, concat_axis=0,...  9.66 us
    ppermute x7, waiting for transfers between devices, stripe_return(): total = total + lax.ppermute(blocks[d], axis, pairs)  6.76 us
    reduce_sum x1, other arithmetic, per_device(): cross_re = jnp.sum(spec_re * br, axis=3) + jnp.sum(spec_im * bi, axis=3)  5.94 us
    dot_general x1, matrix products, per_device(): jnp.dot(visited, forward, preferred_element_type=jnp.float32)  5.64 us
  transfers between devices with their start and end apart: 15, of which 5 were waited for; matrix products, arithmetic and copies ran while one was open for 47% of the time, Pallas kernels for 0%

profile of v5, /device:TPU:0, one launch (start us, length us, event | category | flops | bytes accessed | tf_op | source)
XLA Modules:
  0.0 131.6 jit_solution(9568010691100925888)
XLA Ops:
  0.7 1.4 %copy.25 = bf16[8,2,16,2048]{3,2,1,0:T(8,128)(2,1)S(1)} copy(bf16[8,2,16,2048]{3,2,0,1:T(8,128)(2,1)} %bitcast.123) | data formatting | bytes 2097152 | tf_op jit(solution)/shard_map/transpose | solution.py:66
  2.1 1.9 %fusion.60 = (bf16[48,2048]{1,0:T(8,128)(2,1)S(1)}, bf16[8,48,2048]{2,1,0:T(8,128)(2,1)}, bf16[48,2048]{1,0:T(8,128)(2,1)}, bf16[48,2048]{1,0:T(8,128)(2,1)S(1)}...) fusion(s32[]{:T(128)S(6)} %select_n.131, bf16[8,16,2048]{2,1,0:T(8,128)(2,1)} %bitcast.125, ...), kind=kLoop, calls=%fused_computation.121 | loop fusion | flops 2359295 | bytes 2752536 | tf_op jit(solution)/shard_map/jit(dynamic_index_in_dim)/squeeze | solution.py:37
  4.0 1.7 %collective-permute-start = (bf16[48,2048]{1,0:T(8,128)(2,1)}, bf16[48,2048]{1,0:T(8,128)(2,1)}, u32[]{:S(2)}, u32[]{:S(2)}) collective-permute-start(bf16[48,2048]{1,0:T(8,128)(2,1)} %get-tuple-element.13), channel_id=1, source_target_pairs={{0,16},{16,32},{32,48},{48,64},{64,80},{80,96},{96,112},{112,0},{1... | collective-permute-start | bytes 589832 | tf_op jit(solution)/shard_map/ppermute | solution.py:39
  5.7 2.9 %collective-permute-start.1 = (bf16[48,2048]{1,0:T(8,128)(2,1)S(1)}, bf16[48,2048]{1,0:T(8,128)(2,1)}, u32[]{:S(2)}, u32[]{:S(2)}) collective-permute-start(bf16[48,2048]{1,0:T(8,128)(2,1)S(1)} %get-tuple-element.14), channel_id=1, source_target_pairs={{0,32},{16,48},{32,64},{48,80},{64,96},{80,112},{96,0},{112,16},{1... | collective-permute-start | bytes 589832 | tf_op jit(solution)/shard_map/ppermute | solution.py:39
  8.6 2.3 %collective-permute-start.2 = (bf16[48,2048]{1,0:T(8,128)(2,1)S(1)}, bf16[48,2048]{1,0:T(8,128)(2,1)}, u32[]{:S(2)}, u32[]{:S(2)}) collective-permute-start(bf16[48,2048]{1,0:T(8,128)(2,1)S(1)} %get-tuple-element.15), channel_id=1, source_target_pairs={{0,48},{16,64},{32,80},{48,96},{64,112},{80,0},{96,16},{112,32},{1... | collective-permute-start | bytes 589832 | tf_op jit(solution)/shard_map/ppermute | solution.py:39
  12.2 1.6 %collective-permute-start.4 = (bf16[48,2048]{1,0:T(8,128)(2,1)}, bf16[48,2048]{1,0:T(8,128)(2,1)S(1)}, u32[]{:S(2)}, u32[]{:S(2)}) collective-permute-start(bf16[48,2048]{1,0:T(8,128)(2,1)} %get-tuple-element.18), channel_id=1, source_target_pairs={{0,80},{16,96},{32,112},{48,0},{64,16},{80,32},{96,48},{112,64},{1... | collective-permute-start | bytes 589832 | tf_op jit(solution)/shard_map/ppermute | solution.py:39
  21.6 3.1 %copy.28 = bf16[128,4,2176]{2,1,0:T(4,128)(2,1)} copy(bf16[128,4,2176]{2,0,1:T(8,128)(2,1)S(1)} %pad_maximum_fusion.5) | data formatting | bytes 4456448 | tf_op jit(solution)/shard_map/concatenate | solution.py:144
  24.7 9.7 %all-to-all-start = ((bf16[128,4,2176]{2,1,0:T(4,128)(2,1)}), bf16[128,4,2176]{2,1,0:T(4,128)(2,1)S(1)}, u32[]{:S(2)}, u32[]{:S(2)}) async-start(bf16[128,4,2176]{2,1,0:T(4,128)(2,1)} %copy.28), calls=%async_computation | async-start | bytes 4456448 | tf_op jit(solution)/shard_map/all_to_all | solution.py:145
  36.3 1.6 %fusion.81 = (f32[18,2048]{1,0:T(8,128)}, f32[18,2048]{1,0:T(8,128)}) fusion(s32[18]{0:T(128)S(1)} %iota_multiply_fusion), kind=kLoop, calls=%fused_computation.153 | loop fusion | flops 516096 | bytes 294984 | tf_op jit(solution)/shard_map/cos | solution.py:18
  37.9 3.4 %subtract_convert_fusion.1 = (bf16[32,64,1152]{2,1,0:T(8,128)(2,1)S(1)}, bf16[32,64,1152]{2,1,0:T(8,128)(2,1)S(1)}) fusion(f32[64,1152]{1,0:T(8,128)S(1)} %get-tuple-element.44, f32[32,1152]{1,0:T(8,128)S(1)} %get-tuple-element.39, f32[64,1152]{1,0:T(8,128)S(1)} %get-tuple-element.45, f32[32,1152]{1,0:T(8,128)S(1)} %get-tuple-element.38), kind=kLoop, calls=%fused_computation.11 | loop fusion | flops 21233664 | bytes 10321920 | tf_op jit(solution)/shard_map/convert_element_type | solution.py:22
  41.4 3.4 %fusion.37 = (f32[64,2048]{1,0:T(8,128)}, f32[64,2048]{1,0:T(8,128)}) fusion(), kind=kLoop, calls=%fused_computation.87 | loop fusion | flops 1835008 | bytes 1048576 | tf_op jit(solution)/shard_map/sin | solution.py:19
  44.8 3.2 %collective-permute-start.5 = (bf16[48,2048]{1,0:T(8,128)(2,1)S(1)}, bf16[48,2048]{1,0:T(8,128)(2,1)S(1)}, u32[]{:S(2)}, u32[]{:S(2)}) collective-permute-start(bf16[48,2048]{1,0:T(8,128)(2,1)S(1)} %copy-done.10), channel_id=1, source_target_pairs={{0,96},{16,112},{32,0},{48,16},{64,32},{80,48},{96,64},{112,80},{1... | collective-permute-start | bytes 589832 | tf_op jit(solution)/shard_map/ppermute | solution.py:39
  49.0 1.5 %collective-permute-start.6 = (bf16[48,2048]{1,0:T(8,128)(2,1)S(1)}, bf16[48,2048]{1,0:T(8,128)(2,1)S(1)}, u32[]{:S(2)}, u32[]{:S(2)}) collective-permute-start(bf16[48,2048]{1,0:T(8,128)(2,1)S(1)} %get-tuple-element.11), channel_id=1, source_target_pairs={{0,112},{16,0},{32,16},{48,32},{64,48},{80,64},{96,80},{112,96},{1... | collective-permute-start | bytes 589832 | tf_op jit(solution)/shard_map/ppermute | solution.py:39
  53.3 12.0 %collective-permute-done.5 = bf16[48,2048]{1,0:T(8,128)(2,1)S(1)} collective-permute-done((bf16[48,2048]{1,0:T(8,128)(2,1)S(1)}, bf16[48,2048]{1,0:T(8,128)(2,1)S(1)}, u32[]{:S(2)}, u32[]{:S(2)}) %collective-permute-start.5) | collective-permute-done | bytes 196640 | tf_op jit(solution)/shard_map/ppermute | solution.py:39
  65.4 2.4 %collective-permute-done.6 = bf16[48,2048]{1,0:T(8,128)(2,1)S(1)} collective-permute-done((bf16[48,2048]{1,0:T(8,128)(2,1)S(1)}, bf16[48,2048]{1,0:T(8,128)(2,1)S(1)}, u32[]{:S(2)}, u32[]{:S(2)}) %collective-permute-start.6) | collective-permute-done | bytes 196640 | tf_op jit(solution)/shard_map/ppermute | solution.py:39
  68.7 2.7 %fusion.7 = f32[8,2,1,16,2304]{4,3,1,0,2:T(8,128)S(1)} fusion(bf16[8,2,16,2048]{3,2,1,0:T(8,128)(2,1)S(1)} %bitcast.127, bf16[2048,1152]{1,0:T(8,128)(2,1)S(1)} %bitcast.119, bf16[2048,1152]{1,0:T(8,128)(2,1)S(1)} %bitcast.117), kind=kOutput, calls=%fused_computation.17 | convolution fusion | flops 2434793472 | bytes 12845056 | tf_op jit(solution)/shard_map/dot_general | solution.py:76
  71.4 1.4 %slice_bitcast_fusion = (f32[8,2,16,1152]{3,2,1,0:T(8,128)S(1)}, f32[8,2,1152]{2,1,0:T(2,128)S(1)}, f32[8,2,16,1152]{3,2,1,0:T(8,128)}) fusion(f32[8,2,1,16,2304]{4,3,1,0,2:T(8,128)S(1)} %fusion.7), kind=kLoop, calls=%fused_computation.43 | loop fusion | flops 1161216 | bytes 4792320 | tf_op jit(solution)/shard_map/mul | solution.py:93
  72.8 2.3 %gather_fusion = bf16[4,16,2048]{2,1,0:T(8,128)(2,1)} fusion(bf16[8,16,2048]{2,1,0:T(8,128)(2,1)} %slice.108, s32[1024]{0:T(1024)S(1)} %pad_clamp_fusion), kind=kCustom, calls=%fused_computation | custom fusion | bytes 524304 | tf_op jit(solution)/shard_map/jit(_take)/gather | solution.py:74
  75.2 5.6 %fusion.10 = bf16[64,2304]{1,0:T(8,128)(2,1)S(1)} fusion(bf16[64,2048]{1,0:T(8,128)(2,1)} %bitcast.128, bf16[2048,1152]{1,0:T(8,128)(2,1)} %bitcast.120, bf16[2048,1152]{1,0:T(8,128)(2,1)} %bitcast.118), kind=kOutput, calls=%fused_computation.26 | convolution fusion | flops 623001600 | bytes 9994240 | tf_op jit(solution)/shard_map/dot_general | solution.py:82
  81.7 5.9 %multiply_reduce_fusion.3 = (f32[8,2,4,1152]{3,2,1,0:T(4,128)S(1)}, f32[8,2,4,1152]{3,2,1,0:T(4,128)}, f32[8,2,4,1152]{3,2,1,0:T(4,128)}, f32[8,2,4,1152]{3,2,1,0:T(4,128)S(1)}) fusion(f32[4,16,1152]{2,1,0:T(8,128)S(1)} %get-tuple-element.33, f32[8,2,16,1152]{3,2,1,0:T(8,128)S(1)} %copy-done.2, f32[4,16,1152]{2,1,0:T(8,128)S(1)} %get-tuple-element.32, ...), kind=kLoop, calls=%fused_computation.16 | loop fusion | flops 9142272 | bytes 4128768 | tf_op jit(solution)/shard_map/reduce_sum | solution.py:93
  88.5 1.8 %add.218 = f32[8,8,1152]{2,1,0:T(8,128)} reshape(f32[8,2,4,1152]{3,2,1,0:T(4,128)} %add.217) | data formatting | bytes 589824 | tf_op jit(solution)/shard_map/add | solution.py:93
  90.2 1.8 %sub.40 = f32[8,2,4,1152]{3,2,1,0:T(4,128)} subtract(f32[8,2,4,1152]{3,2,1,0:T(4,128)} %get-tuple-element.6, f32[8,2,4,1152]{3,2,1,0:T(4,128)} %get-tuple-element.5) | non-fusion elementwise | flops 73728 | bytes 884736 | tf_op jit(solution)/shard_map/sub | solution.py:94
  92.1 1.8 %sub.41 = f32[8,8,1152]{2,1,0:T(8,128)} reshape(f32[8,2,4,1152]{3,2,1,0:T(4,128)} %sub.40) | data formatting | bytes 589824 | tf_op jit(solution)/shard_map/sub | solution.py:94
  96.2 1.5 %collective-permute-start.10 = (f32[22,1152]{1,0:T(8,128)S(1)}, f32[22,1152]{1,0:T(8,128)S(1)}, u32[]{:S(2)}, u32[]{:S(2)}) collective-permute-start(f32[22,1152]{1,0:T(8,128)S(1)} %get-tuple-element.27), channel_id=1, source_target_pairs={{0,64},{16,80},{32,96},{48,112},{64,0},{80,16},{96,32},{112,48},{1... | collective-permute-start | bytes 304136 | tf_op jit(solution)/shard_map/ppermute | solution.py:48
  97.8 3.2 %collective-permute-start.11 = (f32[22,1152]{1,0:T(8,128)S(1)}, f32[22,1152]{1,0:T(8,128)S(1)}, u32[]{:S(2)}, u32[]{:S(2)}) collective-permute-start(f32[22,1152]{1,0:T(8,128)S(1)} %get-tuple-element.26), channel_id=1, source_target_pairs={{0,48},{16,64},{32,80},{48,96},{64,112},{80,0},{96,16},{112,32},{1... | collective-permute-start | bytes 304136 | tf_op jit(solution)/shard_map/ppermute | solution.py:48
  101.0 6.6 %subtract_convert_fusion = (bf16[18,64,2048]{2,1,0:T(8,128)(2,1)}, bf16[18,64,2048]{2,1,0:T(8,128)(2,1)}) fusion(f32[64,2048]{1,0:T(8,128)S(1)} %copy-done.6, f32[18,2048]{1,0:T(8,128)} %get-tuple-element.41, f32[64,2048]{1,0:T(8,128)S(1)} %copy-done.7, f32[18,2048]{1,0:T(8,128)S(1)} %copy-done.9), kind=kLoop, calls=%fused_computation.9 | loop fusion | flops 21233664 | bytes 10780672 | tf_op jit(solution)/shard_map/convert_element_type | solution.py:22
  108.6 3.5 %collective-permute-start.7 = (f32[22,1152]{1,0:T(8,128)S(1)}, f32[22,1152]{1,0:T(8,128)S(1)}, u32[]{:S(2)}, u32[]{:S(2)}) collective-permute-start(f32[22,1152]{1,0:T(8,128)S(1)} %get-tuple-element.23), channel_id=1, source_target_pairs={{0,112},{16,0},{32,16},{48,32},{64,48},{80,64},{96,80},{112,96},{1... | collective-permute-start | bytes 304136 | tf_op jit(solution)/shard_map/ppermute | solution.py:48
  112.1 2.0 %collective-permute-start.8 = (f32[22,1152]{1,0:T(8,128)S(1)}, f32[22,1152]{1,0:T(8,128)S(1)}, u32[]{:S(2)}, u32[]{:S(2)}) collective-permute-start(f32[22,1152]{1,0:T(8,128)S(1)} %get-tuple-element.29), channel_id=1, source_target_pairs={{0,96},{16,112},{32,0},{48,16},{64,32},{80,48},{96,64},{112,80},{1... | collective-permute-start | bytes 304136 | tf_op jit(solution)/shard_map/ppermute | solution.py:48
  114.5 1.7 %collective-permute-done.12 = f32[22,1152]{1,0:T(8,128)S(1)} collective-permute-done((f32[22,1152]{1,0:T(8,128)S(1)}, f32[22,1152]{1,0:T(8,128)S(1)}, u32[]{:S(2)}, u32[]{:S(2)}) %collective-permute-start.12) | collective-permute-done | bytes 101408 | tf_op jit(solution)/shard_map/ppermute | solution.py:48
  116.6 4.6 %collective-permute-done.8 = f32[22,1152]{1,0:T(8,128)S(1)} collective-permute-done((f32[22,1152]{1,0:T(8,128)S(1)}, f32[22,1152]{1,0:T(8,128)S(1)}, u32[]{:S(2)}, u32[]{:S(2)}) %collective-permute-start.8) | collective-permute-done | bytes 101408 | tf_op jit(solution)/shard_map/ppermute | solution.py:48
  121.4 4.5 %fusion.13 = f32[8,2048]{1,0:T(8,128)S(1)} fusion(bf16[1152,2048]{1,0:T(8,128)(2,1)} %bitcast.122, bf16[1152,2048]{1,0:T(8,128)(2,1)} %bitcast.121, bf16[8,1152]{1,0:T(8,128)(2,1)S(1)} %get-tuple-element.35, bf16[8,1152]{1,0:T(8,128)(2,1)S(1)} %get-tuple-element.34), kind=kOutput, calls=%fused_computation.32 | convolution fusion | flops 94461952 | bytes 9539584 | tf_op jit(solution)/shard_map/dot_general | solution.py:115
  128.1 3.5 %fusion.12 = f32[128,2048]{1,0:T(8,128)} fusion(bf16[128,4,2048]{2,1,0:T(4,128)(2,1)S(1)} %slice.126, bf16[128,2048]{1,0:T(8,128)(2,1)S(1)} %copy-done.5, f32[128]{0:T(128)S(1)} %broadcast_add_fusion, f32[128,4]{0,1:T(4,128)S(1)} %bitcast_convert_fusion), kind=kOutput, calls=%fused_computation.30 | convolution fusion | flops 269287424 | bytes 3672576 | tf_op jit(solution)/shard_map/tps,psx->tx/dot_general | solution.py:149
  (101 shorter events, 19.9 us)
Async XLA Ops:
  0.6 17.6 %copy-start.3 = (bf16[2,128,2048]{2,1,0:T(8,128)(2,1)S(1)}, bf16[2,128,2048]{2,1,0:T(8,128)(2,1)}, u32[]{:S(2)}) copy-start(bf16[2,128,2048]{2,1,0:T(8,128)(2,1)} %param.7) | copy-start | bytes 3145732
  0.6 10.8 %copy-start.4 = (bf16[128,2048]{1,0:T(8,128)(2,1)S(1)}, bf16[128,2048]{1,0:T(8,128)(2,1)}, u32[]{:S(2)}) copy-start(bf16[128,2048]{1,0:T(8,128)(2,1)} %param.6) | copy-start | bytes 1572868
  0.7 13.2 %copy-start.12 = (s32[2]{0:T(128)S(1)}, s32[2]{0:T(128)}, u32[]{:S(2)}) copy-start(s32[2]{0:T(128)} %param.8) | copy-start | bytes 28
  0.7 17.7 %copy-start.11 = (s32[256,1]{0,1:T(1,128)S(1)}, s32[256,1]{0,1:T(1,128)}, u32[]{:S(2)}) copy-start(s32[256,1]{0,1:T(1,128)} %param.9) | copy-start | bytes 3076
  2.1 17.2 %copy-start.13 = (s32[256]{0:T(256)S(1)}, s32[256]{0:T(256)}, u32[]{:S(2)}) copy-start(s32[256]{0:T(256)} %param.10) | copy-start | bytes 3076
  4.0 40.8 %collective-permute-start = (bf16[48,2048]{1,0:T(8,128)(2,1)}, bf16[48,2048]{1,0:T(8,128)(2,1)}, u32[]{:S(2)}, u32[]{:S(2)}) collective-permute-start(bf16[48,2048]{1,0:T(8,128)(2,1)} %get-tuple-element.13), channel_id=1, source_target_pairs={{0,16},{16,32},{32,48},{48,64},{64,80},{80,96},{96,112},{112,0},{1... | collective-permute-start | bytes 589832 | tf_op jit(solution)/shard_map/ppermute | solution.py:39
  5.7 43.3 %collective-permute-start.1 = (bf16[48,2048]{1,0:T(8,128)(2,1)S(1)}, bf16[48,2048]{1,0:T(8,128)(2,1)}, u32[]{:S(2)}, u32[]{:S(2)}) collective-permute-start(bf16[48,2048]{1,0:T(8,128)(2,1)S(1)} %get-tuple-element.14), channel_id=1, source_target_pairs={{0,32},{16,48},{32,64},{48,80},{64,96},{80,112},{96,0},{112,16},{1... | collective-permute-start | bytes 589832 | tf_op jit(solution)/shard_map/ppermute | solution.py:39
  8.6 42.8 %collective-permute-start.2 = (bf16[48,2048]{1,0:T(8,128)(2,1)S(1)}, bf16[48,2048]{1,0:T(8,128)(2,1)}, u32[]{:S(2)}, u32[]{:S(2)}) collective-permute-start(bf16[48,2048]{1,0:T(8,128)(2,1)S(1)} %get-tuple-element.15), channel_id=1, source_target_pairs={{0,48},{16,64},{32,80},{48,96},{64,112},{80,0},{96,16},{112,32},{1... | collective-permute-start | bytes 589832 | tf_op jit(solution)/shard_map/ppermute | solution.py:39
  10.9 41.5 %collective-permute-start.3 = (bf16[48,2048]{1,0:T(8,128)(2,1)S(1)}, bf16[48,2048]{1,0:T(8,128)(2,1)}, u32[]{:S(2)}, u32[]{:S(2)}) collective-permute-start(bf16[48,2048]{1,0:T(8,128)(2,1)S(1)} %get-tuple-element.16), channel_id=1, source_target_pairs={{0,64},{16,80},{32,96},{48,112},{64,0},{80,16},{96,32},{112,48},{1... | collective-permute-start | bytes 589832 | tf_op jit(solution)/shard_map/ppermute | solution.py:39
  12.2 41.1 %collective-permute-start.4 = (bf16[48,2048]{1,0:T(8,128)(2,1)}, bf16[48,2048]{1,0:T(8,128)(2,1)S(1)}, u32[]{:S(2)}, u32[]{:S(2)}) collective-permute-start(bf16[48,2048]{1,0:T(8,128)(2,1)} %get-tuple-element.18), channel_id=1, source_target_pairs={{0,80},{16,96},{32,112},{48,0},{64,16},{80,32},{96,48},{112,64},{1... | collective-permute-start | bytes 589832 | tf_op jit(solution)/shard_map/ppermute | solution.py:39
  21.6 14.6 %copy-start.14 = (s32[4]{0:T(128)S(1)}, s32[4]{0:T(128)}, u32[]{:S(2)}) copy-start(s32[4]{0:T(128)} %param.11) | copy-start | bytes 52
  24.7 101.8 %all-to-all-start = ((bf16[128,4,2176]{2,1,0:T(4,128)(2,1)}), bf16[128,4,2176]{2,1,0:T(4,128)(2,1)S(1)}, u32[]{:S(2)}, u32[]{:S(2)}) async-start(bf16[128,4,2176]{2,1,0:T(4,128)(2,1)} %copy.28), calls=%async_computation | async-start | bytes 4456448 | tf_op jit(solution)/shard_map/all_to_all | solution.py:145
  37.9 6.9 %copy-start.10 = (bf16[48,2048]{1,0:T(8,128)(2,1)S(1)}, bf16[48,2048]{1,0:T(8,128)(2,1)}, u32[]{:S(2)}) copy-start(bf16[48,2048]{1,0:T(8,128)(2,1)} %get-tuple-element.17) | copy-start | bytes 589828
  37.9 10.2 %copy-start.8 = (bf16[8,48,2048]{2,1,0:T(8,128)(2,1)S(1)}, bf16[8,48,2048]{2,1,0:T(8,128)(2,1)}, u32[]{:S(2)}) copy-start(bf16[8,48,2048]{2,1,0:T(8,128)(2,1)} %get-tuple-element.12) | copy-start | bytes 4718596
  41.3 30.1 %copy-start = (bf16[32,64,1152]{2,1,0:T(8,128)(2,1)}, bf16[32,64,1152]{2,1,0:T(8,128)(2,1)S(1)}, u32[]{:S(2)}) copy-start(bf16[32,64,1152]{2,1,0:T(8,128)(2,1)S(1)} %get-tuple-element.30) | copy-start | bytes 14155780
  41.3 30.1 %copy-start.1 = (bf16[32,64,1152]{2,1,0:T(8,128)(2,1)}, bf16[32,64,1152]{2,1,0:T(8,128)(2,1)S(1)}, u32[]{:S(2)}) copy-start(bf16[32,64,1152]{2,1,0:T(8,128)(2,1)S(1)} %get-tuple-element.31) | copy-start | bytes 14155780
  44.8 20.5 %collective-permute-start.5 = (bf16[48,2048]{1,0:T(8,128)(2,1)S(1)}, bf16[48,2048]{1,0:T(8,128)(2,1)S(1)}, u32[]{:S(2)}, u32[]{:S(2)}) collective-permute-start(bf16[48,2048]{1,0:T(8,128)(2,1)S(1)} %copy-done.10), channel_id=1, source_target_pairs={{0,96},{16,112},{32,0},{48,16},{64,32},{80,48},{96,64},{112,80},{1... | collective-permute-start | bytes 589832 | tf_op jit(solution)/shard_map/ppermute | solution.py:39
  49.0 18.8 %collective-permute-start.6 = (bf16[48,2048]{1,0:T(8,128)(2,1)S(1)}, bf16[48,2048]{1,0:T(8,128)(2,1)S(1)}, u32[]{:S(2)}, u32[]{:S(2)}) collective-permute-start(bf16[48,2048]{1,0:T(8,128)(2,1)S(1)} %get-tuple-element.11), channel_id=1, source_target_pairs={{0,112},{16,0},{32,16},{48,32},{64,48},{80,64},{96,80},{112,96},{1... | collective-permute-start | bytes 589832 | tf_op jit(solution)/shard_map/ppermute | solution.py:39
  75.2 6.6 %copy-start.2 = (f32[8,2,16,1152]{3,2,1,0:T(8,128)S(1)}, f32[8,2,16,1152]{3,2,1,0:T(8,128)}, u32[]{:S(2)}) copy-start(f32[8,2,16,1152]{3,2,1,0:T(8,128)} %get-tuple-element.10) | copy-start | bytes 3538948
  87.7 13.3 %copy-start.6 = (f32[64,2048]{1,0:T(8,128)S(1)}, f32[64,2048]{1,0:T(8,128)}, u32[]{:S(2)}) copy-start(f32[64,2048]{1,0:T(8,128)} %get-tuple-element.42) | copy-start | bytes 1572868
  87.7 13.3 %copy-start.7 = (f32[64,2048]{1,0:T(8,128)S(1)}, f32[64,2048]{1,0:T(8,128)}, u32[]{:S(2)}) copy-start(f32[64,2048]{1,0:T(8,128)} %get-tuple-element.43) | copy-start | bytes 1572868
  87.7 13.3 %copy-start.9 = (f32[18,2048]{1,0:T(8,128)S(1)}, f32[18,2048]{1,0:T(8,128)}, u32[]{:S(2)}) copy-start(f32[18,2048]{1,0:T(8,128)} %get-tuple-element.40) | copy-start | bytes 442372
  96.2 15.9 %collective-permute-start.10 = (f32[22,1152]{1,0:T(8,128)S(1)}, f32[22,1152]{1,0:T(8,128)S(1)}, u32[]{:S(2)}, u32[]{:S(2)}) collective-permute-start(f32[22,1152]{1,0:T(8,128)S(1)} %get-tuple-element.27), channel_id=1, source_target_pairs={{0,64},{16,80},{32,96},{48,112},{64,0},{80,16},{96,32},{112,48},{1... | collective-permute-start | bytes 304136 | tf_op jit(solution)/shard_map/ppermute | solution.py:48
  97.8 16.3 %collective-permute-start.11 = (f32[22,1152]{1,0:T(8,128)S(1)}, f32[22,1152]{1,0:T(8,128)S(1)}, u32[]{:S(2)}, u32[]{:S(2)}) collective-permute-start(f32[22,1152]{1,0:T(8,128)S(1)} %get-tuple-element.26), channel_id=1, source_target_pairs={{0,48},{16,64},{32,80},{48,96},{64,112},{80,0},{96,16},{112,32},{1... | collective-permute-start | bytes 304136 | tf_op jit(solution)/shard_map/ppermute | solution.py:48
  107.7 8.5 %collective-permute-start.12 = (f32[22,1152]{1,0:T(8,128)S(1)}, f32[22,1152]{1,0:T(8,128)S(1)}, u32[]{:S(2)}, u32[]{:S(2)}) collective-permute-start(f32[22,1152]{1,0:T(8,128)S(1)} %get-tuple-element.25), channel_id=1, source_target_pairs={{0,32},{16,48},{32,64},{48,80},{64,96},{80,112},{96,0},{112,16},{1... | collective-permute-start | bytes 304136 | tf_op jit(solution)/shard_map/ppermute | solution.py:48
  108.0 8.6 %collective-permute-start.13 = (f32[22,1152]{1,0:T(8,128)S(1)}, f32[22,1152]{1,0:T(8,128)S(1)}, u32[]{:S(2)}, u32[]{:S(2)}) collective-permute-start(f32[22,1152]{1,0:T(8,128)S(1)} %get-tuple-element.24), channel_id=1, source_target_pairs={{0,16},{16,32},{32,48},{48,64},{64,80},{80,96},{96,112},{112,0},{1... | collective-permute-start | bytes 304136 | tf_op jit(solution)/shard_map/ppermute | solution.py:48
  108.6 8.0 %collective-permute-start.7 = (f32[22,1152]{1,0:T(8,128)S(1)}, f32[22,1152]{1,0:T(8,128)S(1)}, u32[]{:S(2)}, u32[]{:S(2)}) collective-permute-start(f32[22,1152]{1,0:T(8,128)S(1)} %get-tuple-element.23), channel_id=1, source_target_pairs={{0,112},{16,0},{32,16},{48,32},{64,48},{80,64},{96,80},{112,96},{1... | collective-permute-start | bytes 304136 | tf_op jit(solution)/shard_map/ppermute | solution.py:48
  112.1 9.1 %collective-permute-start.8 = (f32[22,1152]{1,0:T(8,128)S(1)}, f32[22,1152]{1,0:T(8,128)S(1)}, u32[]{:S(2)}, u32[]{:S(2)}) collective-permute-start(f32[22,1152]{1,0:T(8,128)S(1)} %get-tuple-element.29), channel_id=1, source_target_pairs={{0,96},{16,112},{32,0},{48,16},{64,32},{80,48},{96,64},{112,80},{1... | collective-permute-start | bytes 304136 | tf_op jit(solution)/shard_map/ppermute | solution.py:48
  114.1 7.1 %collective-permute-start.9 = (f32[22,1152]{1,0:T(8,128)S(1)}, f32[22,1152]{1,0:T(8,128)S(1)}, u32[]{:S(2)}, u32[]{:S(2)}) collective-permute-start(f32[22,1152]{1,0:T(8,128)S(1)} %get-tuple-element.28), channel_id=1, source_target_pairs={{0,80},{16,96},{32,112},{48,0},{64,16},{80,32},{96,48},{112,64},{1... | collective-permute-start | bytes 304136 | tf_op jit(solution)/shard_map/ppermute | solution.py:48
  125.9 2.2 %copy-start.5 = (bf16[128,2048]{1,0:T(8,128)(2,1)S(1)}, bf16[128,2048]{1,0:T(8,128)(2,1)}, u32[]{:S(2)}) copy-start(bf16[128,2048]{1,0:T(8,128)(2,1)} %param.6) | copy-start | bytes 1572868

commit v6 on v3

--- a/solution.py
+++ b/solution.py
@@ -36,17 +36,17 @@
     columns = min(pixels, half + 128)
     fwd_cos, fwd_sin = dft_table(pixels, columns, pixels)
     forward = jnp.concatenate([fwd_cos, fwd_sin], axis=1)
-    inv_cos, inv_sin = dft_table(columns, pixels, pixels)
-    inverse = jnp.concatenate([inv_cos, inv_sin], axis=0)
     col = jnp.arange(columns, dtype=jnp.int32)
     weight = jnp.where((col == 0) | (col == half), 1.0, jnp.where(col < half, 2.0, 0.0))
 
-    pieces = 2 if band_rows % 32 == 0 else 1
-    piece_rows = band_rows // pieces
-    gathered = [
-        lax.all_gather(reference_img[p * piece_rows : (p + 1) * piece_rows], "stripe")
-        for p in range(pieces)
-    ]
+    stripes = lax.axis_size("stripe")
+    split = (band_rows * 5 // 8) // 16 * 16 if band_rows % 16 == 0 else band_rows
+    bounds = [(0, split)] + ([(split, band_rows)] if split < band_rows else [])
+    gathered = [lax.all_gather(reference_img[:split], "stripe")]
+    if split < band_rows:
+        rest = reference_img[split:]
+        spread = jnp.broadcast_to(rest[None], (stripes,) + rest.shape)
+        gathered.append(lax.all_to_all(spread, "stripe", split_axis=0, concat_axis=0, tiled=True))
 
     frame_flat = frames.reshape(count_frames * band_rows, pixels)
     spectra = jnp.dot(frame_flat, forward, preferred_element_type=jnp.float32).reshape(
@@ -59,7 +59,8 @@
     band_power = 0.0
     cross_re = 0.0
     cross_im = 0.0
-    for p in range(pieces):
+    for p, (lo, hi) in enumerate(bounds):
+        piece_rows = hi - lo
         visited = jnp.take(gathered[p], visit_order, axis=0, mode="clip")
         band = (
             jnp.dot(
@@ -74,8 +75,8 @@
         band_re = band[:, :, :columns]
         band_im = band[:, :, columns:]
         band_power = band_power + jnp.sum(band_re * band_re + band_im * band_im, axis=1)
-        fr = spec_re[:, None, p * piece_rows : (p + 1) * piece_rows]
-        fi = spec_im[:, None, p * piece_rows : (p + 1) * piece_rows]
+        fr = spec_re[:, None, lo:hi]
+        fi = spec_im[:, None, lo:hi]
         br = band_re[None]
         bi = band_im[None]
         cross_re = cross_re + (jnp.sum(fr * br, axis=2) + jnp.sum(fi * bi, axis=2))
@@ -84,9 +85,10 @@
     coh_re = (cross_re / magnitude).astype(jnp.bfloat16).astype(jnp.float32) * weight
     coh_im = (cross_im / magnitude).astype(jnp.bfloat16).astype(jnp.float32) * weight
     coherence = jnp.concatenate([coh_re, coh_im], axis=2).astype(jnp.bfloat16)
-    surface = jnp.dot(
+    surface = lax.dot_general(
         coherence.reshape(count_frames * steps, 2 * columns),
-        inverse,
+        forward,
+        (((1,), (1,)), ((), ())),
         preferred_element_type=jnp.float32,
     )
     correlation = (surface * math.sqrt(band_rows / pixels)).reshape(count_frames, steps, pixels)

time: 143 us -> 125 us (0.87)
  waiting for transfers between devices: 47.2 us -> 32.1 us
  other arithmetic: 21.6 us -> 10.9 us
  starting transfers between devices: 11.4 us -> 17.4 us
  local copies, waits for them, and re-layouts: 19.8 us -> 21.5 us
    all_gather x2 -> x1, waiting for transfers between devices: 30.5 us -> 0.01 us  [per_device(): gathered = [lax.all_gather(reference_img[:split], 'stripe')]]
    all_to_all x0 -> x1, waiting for transfers between devices: none -> 8.69 us  [per_device(): lax.all_to_all(spread, 'stripe', split_axis=0, concat_axis=0, tiled=True)]
    all_to_all x1, waiting for transfers between devices: 16.2 us -> 23.4 us  [per_device(): lax.all_to_all(packed, ('stripe', 'frame'), split_axis=0, concat_axis=0,...]
    convert_element_type x2 -> x1, other arithmetic: 9.21 us -> 3.4 us  [dft_table(): return (cos_t.astype(jnp.bfloat16), nsin_t.astype(jnp.bfloat16))]
    all_to_all x0 -> x1, starting transfers between devices: none -> 5.64 us  [per_device(): lax.all_to_all(spread, 'stripe', split_axis=0, concat_axis=0, tiled=True)]
    sin x2 -> x1, other arithmetic: 3.2 us -> 1.16 us  [dft_table(): c2, s2 = (jnp.cos(phase_lo)[None, :, :], jnp.sin(phase_lo)[None, :, :])]
    slice x2 -> x4, local copies, waits for them, and re-layouts: 3.46 us -> 4.52 us  [the longest x2 1.82 us: per_device(): fi = spec_im[:, None, lo:hi]]
  transfers between devices with their start and end apart: 3 -> 3, of which waited for: 2 -> 2; matrix products, arithmetic and copies ran while one was open for 31% -> 28% of each run, Pallas kernels for 0% -> 0%
where the time goes in v6:
time: 125 us; the launch traced here: 124 us
  waiting for transfers between devices  32.1 us (26%)
  matrix products  24 us (19%)
  local copies, waits for them, and re-layouts  21.5 us (17%)
  between operations  18.2 us (15%)
  starting transfers between devices  17.4 us (14%)
  other arithmetic  10.9 us (9%)
    all_to_all x1, waiting for transfers between devices, per_device(): lax.all_to_all(packed, ('stripe', 'frame'), split_axis=0, concat_axis=0,...  23.4 us
    dot_general x2, matrix products, per_device(): jnp.dot(visited.reshape(steps * piece_rows, pixels), forward, preferred_e...  12 us
    all_to_all x1, starting transfers between devices, per_device(): lax.all_to_all(packed, ('stripe', 'frame'), split_axis=0, concat_axis=0,...  11.7 us
    all_to_all x1, waiting for transfers between devices, per_device(): lax.all_to_all(spread, 'stripe', split_axis=0, concat_axis=0, tiled=True)  8.69 us
    all_to_all x1, starting transfers between devices, per_device(): lax.all_to_all(spread, 'stripe', split_axis=0, concat_axis=0, tiled=True)  5.64 us
    dot_general x1, matrix products, per_device(): lax.dot_general(coherence.reshape(count_frames * steps, 2 * columns), for...  5.1 us
    gather x2, local copies, waits for them, and re-layouts, per_device(): visited = jnp.take(gathered[p], visit_order, axis=0, mode='clip')  4.39 us
    dot_general x1, matrix products, per_device(): jnp.einsum('tps,psx->tx', hits.astype(jnp.bfloat16), incoming, preferred_...  3.48 us
  transfers between devices with their start and end apart: 3, of which 2 were waited for; matrix products, arithmetic and copies ran while one was open for 28% of the time, Pallas kernels for 0%

profile of v6, /device:TPU:0, one launch (start us, length us, event | category | flops | bytes accessed | tf_op | source)
XLA Modules:
  0.0 124.1 jit_solution(2553751802996160383)
XLA Ops:
  7.2 1.8 %slice.65 = bf16[80,2048]{1,0:T(8,128)(2,1)} slice(bf16[128,2048]{1,0:T(8,128)(2,1)} %param.6), slice={[0:80], [0:2048]} | slice | bytes 655360 | tf_op jit(solution)/shard_map/slice | solution.py:45
  9.0 0.9 slice.70
  10.0 1.3 %broadcast_in_dim.34 = bf16[8,48,2048]{2,1,0:T(8,128)(2,1)} broadcast(bf16[48,2048]{1,0:T(8,128)(2,1)S(1)} %slice.70), dimensions={1,2} | broadcast | bytes 1769472 | tf_op jit(solution)/shard_map/broadcast_in_dim | solution.py:48
  11.3 5.6 %all-to-all-start = ((bf16[8,48,2048]{2,1,0:T(8,128)(2,1)}), bf16[8,48,2048]{2,1,0:T(8,128)(2,1)}, u32[]{:S(2)}, u32[]{:S(2)}) async-start(bf16[8,48,2048]{2,1,0:T(8,128)(2,1)} %broadcast_in_dim.34), calls=%async_computation | async-start | bytes 3145728 | tf_op jit(solution)/shard_map/all_to_all | solution.py:49
  16.9 1.2 fusion.22
  18.1 0.6 select_select_fusion
  18.7 0.6 fusion.47
  23.2 0.7 fusion.32
  25.1 0.9 fusion.9
  26.1 0.7 convolution_convert_fusion.2
  27.2 3.1 %copy.23 = bf16[128,4,2176]{2,1,0:T(4,128)(2,1)} copy(bf16[128,4,2176]{2,0,1:T(8,128)(2,1)S(1)} %pad_maximum_fusion.1) | data formatting | bytes 4456448 | tf_op jit(solution)/shard_map/concatenate | solution.py:118
  30.3 3.4 %subtract_convert_fusion = (bf16[32,64,1152]{2,1,0:T(8,128)(2,1)S(1)}, bf16[32,64,1152]{2,1,0:T(8,128)(2,1)S(1)}) fusion(f32[64,1152]{1,0:T(8,128)S(1)} %get-tuple-element.34, f32[32,1152]{1,0:T(8,128)S(1)} %get-tuple-element.33, f32[64,1152]{1,0:T(8,128)S(1)} %get-tuple-element.35, f32[32,1152]{1,0:T(8,128)S(1)} %get-tuple-element.32), kind=kLoop, calls=%fused_computation.4 | loop fusion | flops 21233664 | bytes 10321920 | tf_op jit(solution)/shard_map/convert_element_type | solution.py:22
  33.8 2.7 %fusion.42 = f32[2304,256]{0,1:T(8,128)S(1)} fusion(bf16[256,2048]{1,0:T(8,128)(2,1)S(1)} %bitcast.60, bf16[2048,1152]{1,0:T(8,128)(2,1)S(1)} %bitcast.55, bf16[2048,1152]{1,0:T(8,128)(2,1)S(1)} %bitcast.51), kind=kOutput, calls=%fused_computation.103 | convolution fusion | flops 2434793472 | bytes 12845056 | tf_op jit(solution)/shard_map/dot_general | solution.py:52
  36.5 0.9 copy-done.1
  37.5 0.8 fusion.44
  38.3 8.7 %all-to-all-done = bf16[8,48,2048]{2,1,0:T(8,128)(2,1)} async-done(((bf16[8,48,2048]{2,1,0:T(8,128)(2,1)}), bf16[8,48,2048]{2,1,0:T(8,128)(2,1)}, u32[]{:S(2)}, u32[]{:S(2)}) %all-to-all-start) | async-done | bytes 1572896 | tf_op jit(solution)/shard_map/all_to_all | solution.py:49
  47.0 11.7 %all-to-all-start.1 = ((bf16[128,4,2176]{2,1,0:T(4,128)(2,1)}), bf16[128,4,2176]{2,1,0:T(4,128)(2,1)}, u32[]{:S(2)}, u32[]{:S(2)}) async-start(bf16[128,4,2176]{2,1,0:T(4,128)(2,1)} %copy.23), calls=%async_computation.1 | async-start | bytes 4456448 | tf_op jit(solution)/shard_map/all_to_all | solution.py:119
  58.7 1.0 fusion.43
  59.7 2.0 %gather_fusion.1 = bf16[4,48,2048]{2,1,0:T(8,128)(2,1)S(1)} fusion(bf16[8,48,2048]{2,1,0:T(8,128)(2,1)} %all-to-all-done, s32[1024]{0:T(1024)S(1)} %pad_clamp_fusion), kind=kCustom, calls=%fused_computation.1 | custom fusion | bytes 1572880 | tf_op jit(solution)/shard_map/jit(_take)/gather | solution.py:64
  61.8 5.0 %convolution_convert_fusion.1 = bf16[192,2304]{1,0:T(8,128)(2,1)S(1)} fusion(bf16[192,2048]{1,0:T(8,128)(2,1)S(1)} %bitcast.61, bf16[2048,1152]{1,0:T(8,128)(2,1)} %bitcast.56, bf16[2048,1152]{1,0:T(8,128)(2,1)} %bitcast.52), kind=kOutput, calls=%fused_computation.6 | convolution fusion | flops 1831256064 | bytes 11108352 | tf_op jit(solution)/shard_map/dot_general | solution.py:66
  67.2 0.7 copy-done.3
  67.9 0.8 multiply_reduce_fusion.7
  68.7 23.4 %all-to-all-done.1 = bf16[128,4,2176]{2,1,0:T(4,128)(2,1)} async-done(((bf16[128,4,2176]{2,1,0:T(4,128)(2,1)}), bf16[128,4,2176]{2,1,0:T(4,128)(2,1)}, u32[]{:S(2)}, u32[]{:S(2)}) %all-to-all-start.1) | async-done | bytes 2228256 | tf_op jit(solution)/shard_map/all_to_all | solution.py:119
  92.0 1.0 slice.99
  93.1 2.6 %slice.100 = bf16[128,4,2048]{2,1,0:T(4,128)(2,1)S(1)} slice(bf16[128,4,2176]{2,1,0:T(4,128)(2,1)} %all-to-all-done.1), slice={[0:128], [0:4], [0:2048]} | slice | bytes 4194304 | tf_op jit(solution)/shard_map/slice | solution.py:120
  95.9 3.5 %fusion.1 = f32[128,2048]{1,0:T(8,128)} fusion(bf16[128,4,2048]{2,1,0:T(4,128)(2,1)S(1)} %slice.100, bf16[128,2048]{1,0:T(8,128)(2,1)S(1)} %copy-done.5, f32[128]{0:T(128)S(1)} %broadcast_add_fusion, f32[128,4]{0,1:T(4,128)S(1)} %bitcast_convert_fusion), kind=kOutput, calls=%fused_computation.14 | convolution fusion | flops 269287424 | bytes 3672576 | tf_op jit(solution)/shard_map/tps,psx->tx/dot_general | solution.py:123
  99.4 2.4 %gather_fusion = bf16[4,80,2048]{2,1,0:T(8,128)(2,1)S(1)} fusion(bf16[8,80,2048]{2,1,0:T(8,128)(2,1)} %bitcast.62, s32[1024]{0:T(1024)S(1)} %pad_clamp_fusion), kind=kCustom, calls=%fused_computation | custom fusion | bytes 2621456 | tf_op jit(solution)/shard_map/jit(_take)/gather | solution.py:64
  101.7 7.0 %convolution_convert_fusion = bf16[320,2304]{1,0:T(8,128)(2,1)S(1)} fusion(bf16[320,2048]{1,0:T(8,128)(2,1)S(1)} %bitcast.59, bf16[2048,1152]{1,0:T(8,128)(2,1)} %bitcast.57, bf16[2048,1152]{1,0:T(8,128)(2,1)} %bitcast.53), kind=kOutput, calls=%fused_computation.5 | convolution fusion | flops 3039510528 | bytes 12222464 | tf_op jit(solution)/shard_map/dot_general | solution.py:66
  109.5 0.8 copy-done.2
  110.3 1.0 multiply_reduce_fusion.3
  111.5 5.1 %convolution_multiply_fusion = f32[8,2048]{1,0:T(8,128)S(1)} fusion(bf16[8,1152]{1,0:T(8,128)(2,1)S(1)} %get-tuple-element.29, bf16[8,1152]{1,0:T(8,128)(2,1)S(1)} %get-tuple-element.28, bf16[2048,1152]{1,0:T(8,128)(2,1)} %bitcast.58, bf16[2048,1152]{1,0:T(8,128)(2,1)} %bitcast.54), kind=kOutput, calls=%fused_computation.16 | convolution fusion | flops 94461952 | bytes 9539584 | tf_op jit(solution)/shard_map/dot_general | solution.py:88
  116.6 0.7 reshape.261
  (56 shorter events, 3.3 us)
Async XLA Ops:
  7.2 92.2 %all-gather.3.cloned.1.call-start = ((), (), s32[]{:S(2)}) async-start(), calls=%async_computation.2 | async-start | bytes 2949120 | tf_op jit(solution)/shard_map/all_gather | solution.py:45
  9.0 9.7 %copy-start.8 = (s32[2]{0:T(128)S(1)}, s32[2]{0:T(128)}, u32[]{:S(2)}) copy-start(s32[2]{0:T(128)} %param.8) | copy-start | bytes 28
  9.9 13.9 %copy-start.7 = (s32[256,1]{0,1:T(1,128)S(1)}, s32[256,1]{0,1:T(1,128)}, u32[]{:S(2)}) copy-start(s32[256,1]{0,1:T(1,128)} %param.9) | copy-start | bytes 3076
  11.3 13.5 %copy-start.9 = (s32[256]{0:T(256)S(1)}, s32[256]{0:T(256)}, u32[]{:S(2)}) copy-start(s32[256]{0:T(256)} %param.10) | copy-start | bytes 3076
  11.3 13.7 %copy-start.4 = (bf16[2,128,2048]{2,1,0:T(8,128)(2,1)S(1)}, bf16[2,128,2048]{2,1,0:T(8,128)(2,1)}, u32[]{:S(2)}) copy-start(bf16[2,128,2048]{2,1,0:T(8,128)(2,1)} %param.7) | copy-start | bytes 3145732
  11.3 35.7 %all-to-all-start = ((bf16[8,48,2048]{2,1,0:T(8,128)(2,1)}), bf16[8,48,2048]{2,1,0:T(8,128)(2,1)}, u32[]{:S(2)}, u32[]{:S(2)}) async-start(bf16[8,48,2048]{2,1,0:T(8,128)(2,1)} %broadcast_in_dim.34), calls=%async_computation | async-start | bytes 3145728 | tf_op jit(solution)/shard_map/all_to_all | solution.py:49
  33.8 2.7 %copy-start = (bf16[32,64,1152]{2,1,0:T(8,128)(2,1)}, bf16[32,64,1152]{2,1,0:T(8,128)(2,1)S(1)}, u32[]{:S(2)}) copy-start(bf16[32,64,1152]{2,1,0:T(8,128)(2,1)S(1)} %get-tuple-element.24) | copy-start | bytes 14155780
  33.8 3.6 %copy-start.1 = (bf16[32,64,1152]{2,1,0:T(8,128)(2,1)}, bf16[32,64,1152]{2,1,0:T(8,128)(2,1)S(1)}, u32[]{:S(2)}) copy-start(bf16[32,64,1152]{2,1,0:T(8,128)(2,1)S(1)} %get-tuple-element.25) | copy-start | bytes 14155780
  37.5 21.2 %copy-start.10 = (s32[4]{0:T(128)S(1)}, s32[4]{0:T(128)}, u32[]{:S(2)}) copy-start(s32[4]{0:T(128)} %param.11) | copy-start | bytes 52
  47.0 45.0 %all-to-all-start.1 = ((bf16[128,4,2176]{2,1,0:T(4,128)(2,1)}), bf16[128,4,2176]{2,1,0:T(4,128)(2,1)}, u32[]{:S(2)}, u32[]{:S(2)}) async-start(bf16[128,4,2176]{2,1,0:T(4,128)(2,1)} %copy.23), calls=%async_computation.1 | async-start | bytes 4456448 | tf_op jit(solution)/shard_map/all_to_all | solution.py:119
  66.9 1.0 copy-start.3
  68.7 27.2 %copy-start.5 = (bf16[128,2048]{1,0:T(8,128)(2,1)S(1)}, bf16[128,2048]{1,0:T(8,128)(2,1)}, u32[]{:S(2)}) copy-start(bf16[128,2048]{1,0:T(8,128)(2,1)} %param.6) | copy-start | bytes 1572868
  109.2 1.1 copy-start.2
  109.4 2.0 %copy-start.6 = (f32[1152]{0:T(1024)S(1)}, f32[1152]{0:T(1024)}, u32[]{:S(2)}) copy-start(f32[1152]{0:T(1024)} %select_select_fusion) | copy-start | bytes 13828
Sparse Core Ops, SparseCore 0:
  9.6 76.8 all-gather.2

commit v7 on v2

--- a/solution.py
+++ b/solution.py
@@ -105,6 +105,7 @@
     lanes = 128
     index_cols = jnp.broadcast_to(out_index[:, :, None], (num_devices, capacity, lanes))
     packed = jnp.concatenate([outgoing, index_cols], axis=2)
+    packed, _ = lax.optimization_barrier((packed, gathered))
     received = lax.all_to_all(packed, ("stripe", "frame"), split_axis=0, concat_axis=0, tiled=True)
     incoming = received[:, :, :pixels]
     index_f = received[:, :, pixels].astype(jnp.float32)

time: 122 us -> 120 us (0.984)
  starting transfers between devices: 11.2 us -> 7.68 us
    all_to_all x1, waiting for transfers between devices: 31.5 us -> 6.22 us  [per_device(): lax.all_to_all(packed, ('stripe', 'frame'), split_axis=0, concat_axis=0,...]
    all_gather x1, waiting for transfers between devices: 7.26 us -> 32.3 us  [per_device(): gathered = lax.all_gather(reference_img, 'stripe')]
    all_to_all x1, starting transfers between devices: 11.2 us -> 7.64 us  [per_device(): lax.all_to_all(packed, ('stripe', 'frame'), split_axis=0, concat_axis=0,...]
    concatenate x1 -> x0, local copies, waits for them, and re-layouts: 3.07 us -> none  [per_device(): packed = jnp.concatenate([outgoing, index_cols], axis=2)]
    optimization_barrier x0 -> x1, local copies, waits for them, and re-layouts: none -> 3.07 us  [per_device(): packed, _ = lax.optimization_barrier((packed, gathered))]
    gather x1, local copies, waits for them, and re-layouts: 2.93 us -> 4.21 us  [per_device(): visited = jnp.take(gathered, visit_order, axis=0, mode='clip')]
    squeeze x1, local copies, waits for them, and re-layouts: 1.3 us -> 0.07 us  [per_device(): frames[f]]
  transfers between devices with their start and end apart: 2 -> 2, of which waited for: 2 -> 2; matrix products, arithmetic and copies ran while one was open for 22% -> 35% of each run, Pallas kernels for 0% -> 0%
where the time goes in v7:
time: 120 us; the launch traced here: 118 us
  waiting for transfers between devices  39.2 us (33%)
  matrix products  24.6 us (20%)
  between operations  18.2 us (15%)
  local copies, waits for them, and re-layouts  15.9 us (13%)
  other arithmetic  12.6 us (10%)
  starting transfers between devices  7.68 us (6%)
    all_gather x1, waiting for transfers between devices, per_device(): gathered = lax.all_gather(reference_img, 'stripe')  32.3 us
    all_to_all x1, starting transfers between devices, per_device(): lax.all_to_all(packed, ('stripe', 'frame'), split_axis=0, concat_axis=0,...  7.64 us
    all_to_all x1, waiting for transfers between devices, per_device(): lax.all_to_all(packed, ('stripe', 'frame'), split_axis=0, concat_axis=0,...  6.22 us
    dot_general x1, matrix products, per_device(): jnp.dot(visited_flat, cos_t, preferred_element_type=jnp.float32)  5.98 us
    unnamed x21, local copies, waits for them, and re-layouts  4.37 us
    gather x1, local copies, waits for them, and re-layouts, per_device(): visited = jnp.take(gathered, visit_order, axis=0, mode='clip')  4.21 us
    dot_general x1, matrix products, per_device(): lax.dot_general(coh_im, nsin_t, contract, preferred_element_type=jnp.floa...  3.67 us
    dot_general x1, matrix products, per_device(): lax.dot_general(coh_re, cos_t, contract, preferred_element_type=jnp.float32)  3.65 us
  transfers between devices with their start and end apart: 2, of which 2 were waited for; matrix products, arithmetic and copies ran while one was open for 35% of the time, Pallas kernels for 0%

profile of v7, /device:TPU:0, one launch (start us, length us, event | category | flops | bytes accessed | tf_op | source)
XLA Modules:
  0.0 118.1 jit_solution(18354956028245277689)
XLA Ops:
  7.2 0.7 all-gather.3.cloned.1.call-update
  7.9 1.3 %fusion.35 = (s32[1]{0:T(128)}, s32[1]{0:T(128)}) fusion(s32[2]{0:T(128)} %param.8), kind=kLoop, calls=%fused_computation.90 | loop fusion | bytes 16 | tf_op jit(solution)/shard_map/slice | solution.py:89
  13.1 0.8 copy.21
  14.3 0.7 pad_clamp_fusion
  14.9 0.9 fusion.27
  15.8 0.7 multiply_add_fusion.1
  16.7 0.9 fusion.7
  17.7 1.2 fusion.21
  18.9 0.9 fusion.8
  19.9 0.7 convolution_convert_fusion
  21.0 0.7 fusion.31
  21.6 3.5 %subtract_convert_fusion = (bf16[32,64,1152]{2,1,0:T(8,128)(2,1)S(1)}, bf16[32,64,1152]{2,1,0:T(8,128)(2,1)S(1)}) fusion(f32[64,1152]{1,0:T(8,128)S(1)} %get-tuple-element.26, f32[32,1152]{1,0:T(8,128)S(1)} %get-tuple-element.19, f32[64,1152]{1,0:T(8,128)S(1)} %get-tuple-element.27, f32[32,1152]{1,0:T(8,128)S(1)} %get-tuple-element.18), kind=kLoop, calls=%fused_computation.2 | loop fusion | flops 21233664 | bytes 10321920 | tf_op jit(solution)/shard_map/convert_element_type | solution.py:20
  25.1 2.1 %copy-done.1 = bf16[32,64,1152]{2,1,0:T(8,128)(2,1)} copy-done((bf16[32,64,1152]{2,1,0:T(8,128)(2,1)}, bf16[32,64,1152]{2,1,0:T(8,128)(2,1)S(1)}, u32[]{:S(2)}) %copy-start.1) | copy-done | bytes 4718616
  27.2 1.5 %fusion.37 = f32[1152,256]{0,1:T(8,128)S(1)} fusion(bf16[256,2048]{1,0:T(8,128)(2,1)S(1)} %bitcast.74, bf16[2048,1152]{1,0:T(8,128)(2,1)S(1)} %bitcast.66), kind=kOutput, calls=%fused_computation.92 | convolution fusion | flops 1207959552 | bytes 6946816 | tf_op jit(solution)/shard_map/dot_general | solution.py:45
  28.8 1.0 copy-done.3
  29.8 2.6 %add_reduce_fusion.1 = (f32[2,1152]{1,0:T(2,128)S(1)}, f32[1152,256]{0,1:T(8,128)}) fusion(f32[1152,256]{0,1:T(8,128)S(1)} %fusion.37, bf16[256,2048]{1,0:T(8,128)(2,1)S(1)} %bitcast.75, bf16[2048,1152]{1,0:T(8,128)(2,1)S(1)} %bitcast.61), kind=kOutput, calls=%fused_computation.18 | convolution fusion | flops 1209136896 | bytes 8135680 | tf_op jit(solution)/shard_map/dot_general | solution.py:48
  32.4 32.3 %all-gather.3.cloned.1.call-done = bf16[1024,2048]{1,0:T(8,128)(2,1)} async-done(((bf16[128,2048]{1,0:T(8,128)(2,1)}), bf16[1024,2048]{1,0:T(8,128)(2,1)}) %all-gather.3.cloned.1.call-update) | async-done | bytes 4194320 | tf_op jit(solution)/shard_map/all_gather | solution.py:41
  64.7 3.1 %copy.23 = bf16[128,4,2176]{2,1,0:T(4,128)(2,1)} copy(bf16[128,4,2176]{2,0,1:T(8,128)(2,1)S(1)} %pad_maximum_fusion) | data formatting | bytes 4456448 | tf_op jit(solution)/shard_map/optimization_barrier | solution.py:108
  67.7 7.6 %all-to-all-start = ((bf16[128,4,2176]{2,1,0:T(4,128)(2,1)}), bf16[128,4,2176]{2,1,0:T(4,128)(2,1)S(1)}, u32[]{:S(2)}, u32[]{:S(2)}) async-start(bf16[128,4,2176]{2,1,0:T(4,128)(2,1)} %copy.23), calls=%async_computation | async-start | bytes 4456448 | tf_op jit(solution)/shard_map/all_to_all | solution.py:109
  75.4 4.2 %gather_fusion = bf16[4,128,2048]{2,1,0:T(8,128)(2,1)} fusion(bf16[8,128,2048]{2,1,0:T(8,128)(2,1)} %bitcast.73, s32[1024]{0:T(1024)S(1)} %pad_clamp_fusion), kind=kCustom, calls=%fused_computation | custom fusion | bytes 4194320 | tf_op jit(solution)/shard_map/jit(_take)/gather | solution.py:42
  79.6 6.0 %bitcast_convert_fusion.1 = (f32[4,128,1152]{2,1,0:T(8,128)S(1)}, bf16[512,1152]{1,0:T(8,128)(2,1)S(1)}) fusion(bf16[512,2048]{1,0:T(8,128)(2,1)} %bitcast.69, bf16[2048,1152]{1,0:T(8,128)(2,1)} %bitcast.67), kind=kOutput, calls=%fused_computation.30 | convolution fusion | flops 2417098752 | bytes 10354688 | tf_op jit(solution)/shard_map/dot_general | solution.py:55
  85.6 2.9 %bitcast_convert_fusion = (f32[4,128,1152]{2,1,0:T(8,128)S(1)}, bf16[512,1152]{1,0:T(8,128)(2,1)S(1)}) fusion(bf16[512,2048]{1,0:T(8,128)(2,1)S(1)} %bitcast.70, bf16[2048,1152]{1,0:T(8,128)(2,1)S(1)} %bitcast.65), kind=kOutput, calls=%fused_computation.29 | convolution fusion | flops 2417098752 | bytes 10354688 | tf_op jit(solution)/shard_map/dot_general | solution.py:61
  88.6 0.5 add_reduce_fusion
  89.1 0.8 copy-done.4
  89.8 0.4 copy-done.5
  90.2 1.8 %multiply_reduce_fusion.1 = (f32[2,4,1152]{2,1,0:T(4,128)S(1)}, f32[2,4,1152]{2,1,0:T(4,128)S(1)}, f32[2,4,1152]{2,1,0:T(4,128)S(1)}, f32[2,4,1152]{2,1,0:T(4,128)S(1)}) fusion(f32[2,128,1152]{2,1,0:T(8,128)S(1)} %bitcast.72, f32[4,128,1152]{2,1,0:T(8,128)S(1)} %get-tuple-element.20, f32[2,128,1152]{2,1,0:T(8,128)S(1)} %bitcast.71, ...), kind=kLoop, calls=%fused_computation.4 | loop fusion | flops 9400320 | bytes 7225344 | tf_op jit(solution)/shard_map/reduce_sum | solution.py:73
  92.0 3.6 %fusion.36 = f32[8,2048]{1,0:T(8,128)S(1)} fusion(bf16[8,1152]{1,0:T(8,128)(2,1)S(1)} %convert_element_type.225, bf16[2048,1152]{1,0:T(8,128)(2,1)} %bitcast.68), kind=kOutput, calls=%fused_computation.91 | convolution fusion | flops 37748736 | bytes 4802560 | tf_op jit(solution)/shard_map/dot_general | solution.py:80
  95.7 3.7 %fusion.2 = f32[8,2048]{1,0:T(8,128)S(1)} fusion(f32[8,2048]{1,0:T(8,128)S(1)} %fusion.36, bf16[8,1152]{1,0:T(8,128)(2,1)S(1)} %convert_element_type.229, bf16[2048,1152]{1,0:T(8,128)(2,1)} %bitcast.62), kind=kOutput, calls=%fused_computation.16 | convolution fusion | flops 37781504 | bytes 4868096 | tf_op jit(solution)/shard_map/dot_general | solution.py:82
  99.3 0.7 reshape.318
  100.0 6.2 %all-to-all-done = bf16[128,4,2176]{2,1,0:T(4,128)(2,1)S(1)} async-done(((bf16[128,4,2176]{2,1,0:T(4,128)(2,1)}), bf16[128,4,2176]{2,1,0:T(4,128)(2,1)S(1)}, u32[]{:S(2)}, u32[]{:S(2)}) %all-to-all-start) | async-done | bytes 2228256 | tf_op jit(solution)/shard_map/all_to_all | solution.py:109
  106.6 1.2 slice.36
  107.8 3.5 %fusion.1 = f32[128,2048]{1,0:T(8,128)} fusion(bf16[128,4,2048]{2,1,0:T(4,128)(2,1)S(1)} %slice.36, bf16[128,2048]{1,0:T(8,128)(2,1)S(1)} %copy-done.7, f32[128]{0:T(128)S(1)} %broadcast_add_fusion, f32[128,4]{0,1:T(4,128)S(1)} %bitcast_convert_fusion.2), kind=kOutput, calls=%fused_computation.12 | convolution fusion | flops 269287424 | bytes 3672576 | tf_op jit(solution)/shard_map/tps,psx->tx/dot_general | solution.py:113
  (40 shorter events, 1.5 us)
Async XLA Ops:
  7.2 11.7 %copy-start.6 = (bf16[2,128,2048]{2,1,0:T(8,128)(2,1)S(1)}, bf16[2,128,2048]{2,1,0:T(8,128)(2,1)}, u32[]{:S(2)}) copy-start(bf16[2,128,2048]{2,1,0:T(8,128)(2,1)} %param.7) | copy-start | bytes 3145732
  7.2 57.5 %all-gather.3.cloned.1.call-start = ((), (), s32[]{:S(2)}) async-start(), calls=%async_computation.1 | async-start | bytes 4718592 | tf_op jit(solution)/shard_map/all_gather | solution.py:41
  25.1 2.1 %copy-start.1 = (bf16[32,64,1152]{2,1,0:T(8,128)(2,1)}, bf16[32,64,1152]{2,1,0:T(8,128)(2,1)S(1)}, u32[]{:S(2)}) copy-start(bf16[32,64,1152]{2,1,0:T(8,128)(2,1)S(1)} %get-tuple-element.12) | copy-start | bytes 14155780
  25.1 3.7 %copy-start = (bf16[32,64,1152]{2,1,0:T(8,128)(2,1)}, bf16[32,64,1152]{2,1,0:T(8,128)(2,1)S(1)}, u32[]{:S(2)}) copy-start(bf16[32,64,1152]{2,1,0:T(8,128)(2,1)S(1)} %get-tuple-element.13) | copy-start | bytes 14155780
  28.8 1.0 copy-start.3
  67.7 38.5 %all-to-all-start = ((bf16[128,4,2176]{2,1,0:T(4,128)(2,1)}), bf16[128,4,2176]{2,1,0:T(4,128)(2,1)S(1)}, u32[]{:S(2)}, u32[]{:S(2)}) async-start(bf16[128,4,2176]{2,1,0:T(4,128)(2,1)} %copy.23), calls=%async_computation | async-start | bytes 4456448 | tf_op jit(solution)/shard_map/all_to_all | solution.py:109
  75.4 10.2 %slice-start = ((s8[4718592]{0:T(1024)(128)(4,1)}), s8[524288]{0:T(1024)(128)(4,1)S(1)}, s32[]{:S(2)}) async-start(s8[4718592]{0:T(1024)(128)(4,1)} %bitcast.63), calls=%async_computation.2 | async-start | bytes 1048576
  79.6 6.0 %slice-start.1 = ((s8[4718592]{0:T(1024)(128)(4,1)}), s8[4194304]{0:T(1024)(128)(4,1)S(1)}, s32[]{:S(2)}) async-start(s8[4718592]{0:T(1024)(128)(4,1)} %bitcast.63), calls=%async_computation.3 | async-start | bytes 8388608
  79.6 6.0 %copy-start.2 = (bf16[4,128,2048]{2,1,0:T(8,128)(2,1)S(1)}, bf16[4,128,2048]{2,1,0:T(8,128)(2,1)}, u32[]{:S(2)}) copy-start(bf16[4,128,2048]{2,1,0:T(8,128)(2,1)} %gather_fusion) | copy-start | bytes 6291460
  88.5 1.3 %copy-start.4 = (f32[1152,256]{0,1:T(8,128)S(1)}, f32[1152,256]{0,1:T(8,128)}, u32[]{:S(2)}) copy-start(f32[1152,256]{0,1:T(8,128)} %copy-done.3) | copy-start | bytes 3538948
  88.5 1.6 %copy-start.5 = (f32[1152,256]{0,1:T(8,128)S(1)}, f32[1152,256]{0,1:T(8,128)}, u32[]{:S(2)}) copy-start(f32[1152,256]{0,1:T(8,128)} %get-tuple-element.25) | copy-start | bytes 3538948
  99.3 8.4 %copy-start.7 = (bf16[128,2048]{1,0:T(8,128)(2,1)S(1)}, bf16[128,2048]{1,0:T(8,128)(2,1)}, u32[]{:S(2)}) copy-start(bf16[128,2048]{1,0:T(8,128)(2,1)} %param.6) | copy-start | bytes 1572868
Sparse Core Ops, SparseCore 0:
  9.6 55.0 all-gather.2

commit v8 on v4

--- a/solution.py
+++ b/solution.py
@@ -37,8 +37,6 @@
     columns = min(pixels, half + 128)
     fwd_cos, fwd_sin = dft_table(pixels, columns, pixels)
     forward = jnp.concatenate([fwd_cos, fwd_sin], axis=1)
-    inv_cos, inv_sin = dft_table(columns, pixels, pixels)
-    inverse = jnp.concatenate([inv_cos, inv_sin], axis=0)
     col = jnp.arange(columns, dtype=jnp.int32)
     weight = jnp.where((col == 0) | (col == half), 1.0, jnp.where(col < half, 2.0, 0.0))
 
@@ -48,6 +46,31 @@
     band_part = reference_img.reshape(stripes, chunk, pixels)
     outbound = jnp.concatenate([frame_part, band_part], axis=1)
     inbound = lax.all_to_all(outbound, "stripe", split_axis=0, concat_axis=0, tiled=True)
+    num_devices = lax.axis_size("stripe") * lax.axis_size("frame")
+    frame_rows = count_frames * band_rows
+    capacity = max(2, 2 * frame_rows // num_devices)
+    placed = jnp.concatenate(
+        [shift_rows(frames[f], shifts[f]) for f in range(count_frames)], axis=0
+    )
+    target_dev = dest_device[:, 0]
+    onehot = (target_dev[:, None] == jnp.arange(num_devices, dtype=jnp.int32)[None, :]).astype(
+        jnp.int32
+    )
+    row_rank = jnp.sum((jnp.cumsum(onehot, axis=0) - 1) * onehot, axis=1)
+    slot_id = target_dev * capacity + row_rank
+    select = slot_id[None, :] == jnp.arange(num_devices * capacity, dtype=jnp.int32)[:, None]
+    select3 = select.reshape(num_devices, capacity, frame_rows)
+    outgoing = jnp.einsum(
+        "dsr,rx->dsx", select3.astype(jnp.bfloat16), placed, preferred_element_type=jnp.float32
+    ).astype(jnp.bfloat16)
+    filled = jnp.any(select3, axis=2)
+    local_row = jnp.sum(jnp.where(select3, dest_row[None, None, :], 0), axis=2)
+    out_index = jnp.where(filled, local_row, -1).astype(jnp.float32).astype(jnp.bfloat16)
+    lanes = 128
+    index_cols = jnp.broadcast_to(out_index[:, :, None], (num_devices, capacity, lanes))
+    packed = jnp.concatenate([outgoing, index_cols], axis=2)
+    packed, inbound = lax.optimization_barrier((packed, inbound))
+    received = lax.all_to_all(packed, ("stripe", "frame"), split_axis=0, concat_axis=0, tiled=True)
     frame_rows_in = inbound[:, : count_frames * chunk].reshape(stripes * count_frames * chunk, pixels)
     band_in = inbound[:, count_frames * chunk :]
     visited = jnp.take(band_in, visit_order, axis=0, mode="clip").reshape(steps * chunk, pixels)
@@ -80,6 +103,7 @@
         ],
         axis=1,
     )
+    partial, received = lax.optimization_barrier((partial, received))
     total = jnp.sum(
         lax.all_to_all(partial, "stripe", split_axis=0, concat_axis=0, tiled=True), axis=0
     )
@@ -93,37 +117,14 @@
     coh_re = (cross_re / magnitude).astype(jnp.bfloat16).astype(jnp.float32) * weight
     coh_im = (cross_im / magnitude).astype(jnp.bfloat16).astype(jnp.float32) * weight
     coherence = jnp.concatenate([coh_re, coh_im], axis=2).astype(jnp.bfloat16)
-    surface = jnp.dot(
+    surface = lax.dot_general(
         coherence.reshape(count_frames * steps, 2 * columns),
-        inverse,
+        forward,
+        (((1,), (1,)), ((), ())),
         preferred_element_type=jnp.float32,
     )
     correlation = (surface * math.sqrt(band_rows / pixels)).reshape(count_frames, steps, pixels)
 
-    num_devices = lax.axis_size("stripe") * lax.axis_size("frame")
-    frame_rows = count_frames * band_rows
-    capacity = max(2, 2 * frame_rows // num_devices)
-    placed = jnp.concatenate(
-        [shift_rows(frames[f], shifts[f]) for f in range(count_frames)], axis=0
-    )
-    target_dev = dest_device[:, 0]
-    onehot = (target_dev[:, None] == jnp.arange(num_devices, dtype=jnp.int32)[None, :]).astype(
-        jnp.int32
-    )
-    row_rank = jnp.sum((jnp.cumsum(onehot, axis=0) - 1) * onehot, axis=1)
-    slot_id = target_dev * capacity + row_rank
-    select = slot_id[None, :] == jnp.arange(num_devices * capacity, dtype=jnp.int32)[:, None]
-    select3 = select.reshape(num_devices, capacity, frame_rows)
-    outgoing = jnp.einsum(
-        "dsr,rx->dsx", select3.astype(jnp.bfloat16), placed, preferred_element_type=jnp.float32
-    ).astype(jnp.bfloat16)
-    filled = jnp.any(select3, axis=2)
-    local_row = jnp.sum(jnp.where(select3, dest_row[None, None, :], 0), axis=2)
-    out_index = jnp.where(filled, local_row, -1).astype(jnp.float32).astype(jnp.bfloat16)
-    lanes = 128
-    index_cols = jnp.broadcast_to(out_index[:, :, None], (num_devices, capacity, lanes))
-    packed = jnp.concatenate([outgoing, index_cols], axis=2)
-    received = lax.all_to_all(packed, ("stripe", "frame"), split_axis=0, concat_axis=0, tiled=True)
     incoming = received[:, :, :pixels]
     index_f = received[:, :, pixels].astype(jnp.float32)
     hits = index_f[None, :, :] == jnp.arange(band_rows, dtype=jnp.float32)[:, None, None]

time: 124 us -> 115 us (0.927)
  other arithmetic: 33.7 us -> 24 us
  local copies, waits for them, and re-layouts: 13.2 us -> 16.2 us
  waiting for transfers between devices: 30.9 us -> 29.3 us
    optimization_barrier x0 -> x3, local copies, waits for them, and re-layouts: none -> 6.99 us  [the longest x2 3.78 us: per_device(): partial, received = lax.optimization_barrier((partial, received))]
    convert_element_type x2 -> x1, other arithmetic: 12.6 us -> 6.79 us  [dft_table(): return (cos_t.astype(jnp.bfloat16), nsin_t.astype(jnp.bfloat16))]
    concatenate x1 -> x0, local copies, waits for them, and re-layouts: 3.08 us -> none  [per_device(): packed = jnp.concatenate([outgoing, index_cols], axis=2)]
    all_to_all x1, waiting for transfers between devices: 8.94 us -> 6.55 us  [per_device(): lax.all_to_all(partial, 'stripe', split_axis=0, concat_axis=0, tiled=True)]
    sin x2 -> x1, other arithmetic: 3.2 us -> 1.16 us  [dft_table(): c2, s2 = (jnp.cos(phase_lo)[None, :, :], jnp.sin(phase_lo)[None, :, :])]
    gather x1, local copies, waits for them, and re-layouts: 2.31 us -> 0.56 us  [per_device(): jnp.take(band_in, visit_order, axis=0, mode='clip')]
    dot_general x1, matrix products: 6.4 us -> 7.8 us  [per_device(): jnp.dot(frame_rows_in, forward, preferred_element_type=jnp.float32)]
  transfers between devices with their start and end apart: 3 -> 3, of which waited for: 3 -> 3; matrix products, arithmetic and copies ran while one was open for 24% -> 28% of each run, Pallas kernels for 0% -> 0%
where the time goes in v8:
time: 115 us; the launch traced here: 114 us
  waiting for transfers between devices  29.3 us (25%)
  other arithmetic  24 us (21%)
  matrix products  21.1 us (18%)
  starting transfers between devices  18.5 us (16%)
  local copies, waits for them, and re-layouts  16.2 us (14%)
  between operations  4.86 us (4%)
    all_to_all x1, waiting for transfers between devices, per_device(): lax.all_to_all(packed, ('stripe', 'frame'), split_axis=0, concat_axis=0,...  18.7 us
    all_to_all x1, starting transfers between devices, per_device(): lax.all_to_all(packed, ('stripe', 'frame'), split_axis=0, concat_axis=0,...  9.43 us
    dot_general x1, matrix products, per_device(): jnp.dot(frame_rows_in, forward, preferred_element_type=jnp.float32)  7.8 us
    convert_element_type x1, other arithmetic, dft_table(): return (cos_t.astype(jnp.bfloat16), nsin_t.astype(jnp.bfloat16))  6.79 us
    all_to_all x1, waiting for transfers between devices, per_device(): lax.all_to_all(partial, 'stripe', split_axis=0, concat_axis=0, tiled=True)  6.55 us
    all_to_all x1, starting transfers between devices, per_device(): lax.all_to_all(outbound, 'stripe', split_axis=0, concat_axis=0, tiled=True)  5.51 us
    reduce_sum x1, other arithmetic, per_device(): cross_re = jnp.sum(spec_re * br, axis=3) + jnp.sum(spec_im * bi, axis=3)  5.21 us
    dot_general x1, matrix products, per_device(): lax.dot_general(coherence.reshape(count_frames * steps, 2 * columns), for...  5.1 us
  transfers between devices with their start and end apart: 3, of which 3 were waited for; matrix products, arithmetic and copies ran while one was open for 28% of the time, Pallas kernels for 0%

profile of v8, /device:TPU:0, one launch (start us, length us, event | category | flops | bytes accessed | tf_op | source)
XLA Modules:
  0.0 114.0 jit_solution(9123884405530489732)
XLA Ops:
  0.6 1.4 %copy.36 = bf16[8,2,16,2048]{3,2,1,0:T(8,128)(2,1)S(1)} copy(bf16[8,2,16,2048]{3,2,0,1:T(8,128)(2,1)} %bitcast.64) | data formatting | bytes 2097152 | tf_op jit(solution)/shard_map/transpose | solution.py:44
  2.1 2.3 %pad_maximum_fusion.7 = bf16[8,48,2048]{2,1,0:T(8,128)(2,1)} fusion(bf16[8,16,2048]{2,1,0:T(8,128)(2,1)} %bitcast.67, bf16[8,32,2048]{2,1,0:T(8,128)(2,1)S(1)} %bitcast.63), kind=kLoop, calls=%fused_computation.20 | loop fusion | flops 3145728 | bytes 3145728 | tf_op jit(solution)/shard_map/concatenate | solution.py:47
  4.4 5.5 %all-to-all-start = ((bf16[8,48,2048]{2,1,0:T(8,128)(2,1)}), bf16[8,48,2048]{2,1,0:T(8,128)(2,1)}, u32[]{:S(2)}, u32[]{:S(2)}) async-start(bf16[8,48,2048]{2,1,0:T(8,128)(2,1)} %pad_maximum_fusion.7), calls=%async_computation | async-start | bytes 3145728 | tf_op jit(solution)/shard_map/all_to_all | solution.py:48
  9.9 1.2 %fusion.27 = (f32[64,1152]{1,0:T(8,128)S(1)}, f32[64,1152]{1,0:T(8,128)S(1)}) fusion(), kind=kLoop, calls=%fused_computation.61 | loop fusion | flops 1032192 | bytes 589824 | tf_op jit(solution)/shard_map/sin | solution.py:19
  11.2 0.6 fusion.51
  15.7 0.7 fusion.37
  17.6 0.9 fusion.14
  18.5 0.7 convolution_convert_fusion.1
  19.6 6.8 %subtract_convert_fusion = (bf16[32,64,1152]{2,1,0:T(8,128)(2,1)}, bf16[32,64,1152]{2,1,0:T(8,128)(2,1)}) fusion(f32[64,1152]{1,0:T(8,128)S(1)} %get-tuple-element.31, f32[32,1152]{1,0:T(8,128)S(1)} %get-tuple-element.30, f32[64,1152]{1,0:T(8,128)S(1)} %get-tuple-element.32, f32[32,1152]{1,0:T(8,128)S(1)} %get-tuple-element.29), kind=kLoop, calls=%fused_computation.5 | loop fusion | flops 21233664 | bytes 10321920 | tf_op jit(solution)/shard_map/convert_element_type | solution.py:22
  26.4 4.0 %all-to-all-done = bf16[8,48,2048]{2,1,0:T(8,128)(2,1)} async-done(((bf16[8,48,2048]{2,1,0:T(8,128)(2,1)}), bf16[8,48,2048]{2,1,0:T(8,128)(2,1)}, u32[]{:S(2)}, u32[]{:S(2)}) %all-to-all-start) | async-done | bytes 1572896 | tf_op jit(solution)/shard_map/all_to_all | solution.py:48
  30.4 1.1 slice.62
  31.5 2.3 %slice.60 = bf16[8,32,2048]{2,1,0:T(8,128)(2,1)} slice(bf16[8,48,2048]{2,1,0:T(8,128)(2,1)} %all-to-all-done), slice={[0:8], [0:32], [0:2048]} | slice | bytes 2097152 | tf_op jit(solution)/shard_map/slice | solution.py:74
  33.8 0.6 gather_fusion
  34.4 5.0 %convolution_convert_fusion = bf16[64,2304]{1,0:T(8,128)(2,1)S(1)} fusion(bf16[64,2048]{1,0:T(8,128)(2,1)S(1)} %bitcast.68, bf16[2048,1152]{1,0:T(8,128)(2,1)} %bitcast.60, bf16[2048,1152]{1,0:T(8,128)(2,1)} %bitcast.57), kind=kOutput, calls=%fused_computation.11 | convolution fusion | flops 623001600 | bytes 9994240 | tf_op jit(solution)/shard_map/dot_general | solution.py:84
  39.4 7.8 %fusion.2 = f32[8,2,1,16,2304]{4,3,1,0,2:T(8,128)} fusion(bf16[8,2,16,2048]{3,2,1,0:T(8,128)(2,1)S(1)} %bitcast.66, bf16[2048,1152]{1,0:T(8,128)(2,1)} %bitcast.61, bf16[2048,1152]{1,0:T(8,128)(2,1)} %bitcast.58), kind=kOutput, calls=%fused_computation.10 | convolution fusion | flops 2434793472 | bytes 12845056 | tf_op jit(solution)/shard_map/dot_general | solution.py:78
  47.2 3.2 %copy.37 = bf16[128,4,2176]{2,1,0:T(4,128)(2,1)} copy(bf16[128,4,2176]{2,0,1:T(8,128)(2,1)S(1)} %pad_maximum_fusion.4) | data formatting | bytes 4456448 | tf_op jit(solution)/shard_map/optimization_barrier | solution.py:72
  50.4 9.4 %all-to-all-start.1 = ((bf16[128,4,2176]{2,1,0:T(4,128)(2,1)}), bf16[128,4,2176]{2,1,0:T(4,128)(2,1)S(1)}, u32[]{:S(2)}, u32[]{:S(2)}) async-start(bf16[128,4,2176]{2,1,0:T(4,128)(2,1)} %copy.37), calls=%async_computation.1 | async-start | bytes 4456448 | tf_op jit(solution)/shard_map/all_to_all | solution.py:73
  59.9 2.2 %slice_bitcast_fusion = (f32[8,2,16,1152]{3,2,1,0:T(8,128)S(1)}, f32[8,2,1152]{2,1,0:T(2,128)S(1)}, f32[8,2,16,1152]{3,2,1,0:T(8,128)S(1)}) fusion(f32[8,2,1,16,2304]{4,3,1,0,2:T(8,128)} %fusion.2), kind=kLoop, calls=%fused_computation.22 | loop fusion | flops 1161216 | bytes 4792320 | tf_op jit(solution)/shard_map/mul | solution.py:95
  62.1 5.2 %multiply_reduce_fusion.3 = (f32[8,2,4,1152]{3,2,1,0:T(4,128)S(1)}, f32[8,2,4,1152]{3,2,1,0:T(4,128)S(1)}, f32[8,2,4,1152]{3,2,1,0:T(4,128)S(1)}, f32[8,2,4,1152]{3,2,1,0:T(4,128)S(1)}) fusion(f32[4,16,1152]{2,1,0:T(8,128)S(1)} %get-tuple-element.24, f32[8,2,16,1152]{3,2,1,0:T(8,128)S(1)} %get-tuple-element.18, f32[4,16,1152]{2,1,0:T(8,128)S(1)} %get-tuple-element.23, ...), kind=kLoop, calls=%fused_computation.9 | loop fusion | flops 9142272 | bytes 4128768 | tf_op jit(solution)/shard_map/reduce_sum | solution.py:95
  67.3 0.8 sub.32
  68.1 1.1 sub.33
  69.2 0.8 add.99
  70.0 1.1 add.100
  71.2 1.0 pad_maximum_fusion.8
  72.2 18.7 %all-to-all-done.1 = bf16[128,4,2176]{2,1,0:T(4,128)(2,1)S(1)} async-done(((bf16[128,4,2176]{2,1,0:T(4,128)(2,1)}), bf16[128,4,2176]{2,1,0:T(4,128)(2,1)S(1)}, u32[]{:S(2)}, u32[]{:S(2)}) %all-to-all-start.1) | async-done | bytes 2228256 | tf_op jit(solution)/shard_map/all_to_all | solution.py:73
  90.9 3.6 %all-to-all-start.2 = ((f32[8,22,1152]{2,1,0:T(8,128)}), f32[8,22,1152]{2,1,0:T(8,128)S(1)}, u32[]{:S(2)}, u32[]{:S(2)}) async-start(f32[8,22,1152]{2,1,0:T(8,128)} %pad_maximum_fusion.8), calls=%async_computation.2 | async-start | bytes 1769472 | tf_op jit(solution)/shard_map/all_to_all | solution.py:108
  94.5 3.6 %copy.39 = bf16[128,4,2176]{0,1,2:T(4,128)(2,1)} copy(bf16[128,4,2176]{2,1,0:T(4,128)(2,1)S(1)} %all-to-all-done.1) | data formatting | bytes 4456448 | tf_op jit(solution)/shard_map/optimization_barrier | solution.py:106
  98.0 0.6 fusion.45
  99.0 2.5 %fusion.7 = f32[128,2048]{1,0:T(8,128)} fusion(bf16[128,4,2176]{2,0,1:T(8,128)(2,1)S(1)} %copy.40, bf16[128,2048]{1,0:T(8,128)(2,1)} %param.6, f32[128]{0:T(128)S(1)} %broadcast_add_fusion, f32[128,4]{0,1:T(4,128)S(1)} %fusion.45), kind=kOutput, calls=%fused_computation.16 | convolution fusion | flops 269287424 | bytes 3672576 | tf_op jit(solution)/shard_map/tps,psx->tx/dot_general | solution.py:131
  101.5 6.5 %all-to-all-done.2 = f32[8,22,1152]{2,1,0:T(8,128)S(1)} async-done(((f32[8,22,1152]{2,1,0:T(8,128)}), f32[8,22,1152]{2,1,0:T(8,128)S(1)}, u32[]{:S(2)}, u32[]{:S(2)}) %all-to-all-start.2) | async-done | bytes 811040 | tf_op jit(solution)/shard_map/all_to_all | solution.py:108
  108.2 5.1 %fusion.8 = f32[8,2048]{1,0:T(8,128)S(1)} fusion(bf16[2048,1152]{1,0:T(8,128)(2,1)} %bitcast.62, bf16[2048,1152]{1,0:T(8,128)(2,1)} %bitcast.59, bf16[8,1152]{1,0:T(8,128)(2,1)S(1)} %get-tuple-element.26, bf16[8,1152]{1,0:T(8,128)(2,1)S(1)} %get-tuple-element.25), kind=kOutput, calls=%fused_computation.18 | convolution fusion | flops 94461952 | bytes 9539584 | tf_op jit(solution)/shard_map/dot_general | solution.py:120
  113.3 0.7 reshape.248
  (44 shorter events, 2.3 us)
Async XLA Ops:
  0.6 10.5 %copy-start = (bf16[2,128,2048]{2,1,0:T(8,128)(2,1)S(1)}, bf16[2,128,2048]{2,1,0:T(8,128)(2,1)}, u32[]{:S(2)}) copy-start(bf16[2,128,2048]{2,1,0:T(8,128)(2,1)} %param.7) | copy-start | bytes 3145732
  2.0 9.2 %copy-start.3 = (s32[2]{0:T(128)S(1)}, s32[2]{0:T(128)}, u32[]{:S(2)}) copy-start(s32[2]{0:T(128)} %param.8) | copy-start | bytes 28
  2.0 14.3 %copy-start.2 = (s32[256,1]{0,1:T(1,128)S(1)}, s32[256,1]{0,1:T(1,128)}, u32[]{:S(2)}) copy-start(s32[256,1]{0,1:T(1,128)} %param.9) | copy-start | bytes 3076
  2.0 15.2 %copy-start.4 = (s32[256]{0:T(256)S(1)}, s32[256]{0:T(256)}, u32[]{:S(2)}) copy-start(s32[256]{0:T(256)} %param.10) | copy-start | bytes 3076
  2.1 15.5 %copy-start.5 = (s32[4]{0:T(128)S(1)}, s32[4]{0:T(128)}, u32[]{:S(2)}) copy-start(s32[4]{0:T(128)} %param.11) | copy-start | bytes 52
  4.4 26.0 %all-to-all-start = ((bf16[8,48,2048]{2,1,0:T(8,128)(2,1)}), bf16[8,48,2048]{2,1,0:T(8,128)(2,1)}, u32[]{:S(2)}, u32[]{:S(2)}) async-start(bf16[8,48,2048]{2,1,0:T(8,128)(2,1)} %pad_maximum_fusion.7), calls=%async_computation | async-start | bytes 3145728 | tf_op jit(solution)/shard_map/all_to_all | solution.py:48
  34.4 5.0 %copy-start.1 = (bf16[8,32,2048]{2,1,0:T(8,128)(2,1)S(1)}, bf16[8,32,2048]{2,1,0:T(8,128)(2,1)}, u32[]{:S(2)}) copy-start(bf16[8,32,2048]{2,1,0:T(8,128)(2,1)} %slice.60) | copy-start | bytes 3145732
  50.4 40.5 %all-to-all-start.1 = ((bf16[128,4,2176]{2,1,0:T(4,128)(2,1)}), bf16[128,4,2176]{2,1,0:T(4,128)(2,1)S(1)}, u32[]{:S(2)}, u32[]{:S(2)}) async-start(bf16[128,4,2176]{2,1,0:T(4,128)(2,1)} %copy.37), calls=%async_computation.1 | async-start | bytes 4456448 | tf_op jit(solution)/shard_map/all_to_all | solution.py:73
  90.9 17.1 %all-to-all-start.2 = ((f32[8,22,1152]{2,1,0:T(8,128)}), f32[8,22,1152]{2,1,0:T(8,128)S(1)}, u32[]{:S(2)}, u32[]{:S(2)}) async-start(f32[8,22,1152]{2,1,0:T(8,128)} %pad_maximum_fusion.8), calls=%async_computation.2 | async-start | bytes 1769472 | tf_op jit(solution)/shard_map/all_to_all | solution.py:108

commit v9 on v8

--- a/solution.py
+++ b/solution.py
@@ -71,12 +71,18 @@
     packed = jnp.concatenate([outgoing, index_cols], axis=2)
     packed, inbound = lax.optimization_barrier((packed, inbound))
     received = lax.all_to_all(packed, ("stripe", "frame"), split_axis=0, concat_axis=0, tiled=True)
-    frame_rows_in = inbound[:, : count_frames * chunk].reshape(stripes * count_frames * chunk, pixels)
+    frame_rows_in = (
+        inbound[:, : count_frames * chunk]
+        .reshape(stripes, count_frames, chunk, pixels)
+        .transpose(2, 0, 1, 3)
+        .reshape(chunk * stripes * count_frames, pixels)
+    )
     band_in = inbound[:, count_frames * chunk :]
-    visited = jnp.take(band_in, visit_order, axis=0, mode="clip").reshape(steps * chunk, pixels)
+    visited = jnp.take(band_in, visit_order, axis=0, mode="clip").transpose(1, 0, 2)
+    visited = visited.reshape(chunk * steps, pixels)
 
     spectra = jnp.dot(frame_rows_in, forward, preferred_element_type=jnp.float32).reshape(
-        stripes, count_frames, 1, chunk, 2 * columns
+        chunk, stripes * count_frames, 1, 2 * columns
     )
     spec_re = spectra[..., :columns]
     spec_im = spectra[..., columns:]
@@ -84,16 +90,15 @@
         jnp.dot(visited, forward, preferred_element_type=jnp.float32)
         .astype(jnp.bfloat16)
         .astype(jnp.float32)
-        .reshape(steps, chunk, 2 * columns)
+        .reshape(chunk, 1, steps, 2 * columns)
     )
     band_re = band[..., :columns]
     band_im = band[..., columns:]
-    frame_power = jnp.sum(spec_re * spec_re + spec_im * spec_im, axis=3)[:, :, 0]
-    band_power = jnp.sum(band_re * band_re + band_im * band_im, axis=1)
-    br = band_re[None, None]
-    bi = band_im[None, None]
-    cross_re = jnp.sum(spec_re * br, axis=3) + jnp.sum(spec_im * bi, axis=3)
-    cross_im = jnp.sum(spec_im * br, axis=3) - jnp.sum(spec_re * bi, axis=3)
+    frame_power = jnp.sum(spec_re * spec_re + spec_im * spec_im, axis=0)[:, 0]
+    band_power = jnp.sum(band_re * band_re + band_im * band_im, axis=0)[0]
+    cross_re = jnp.sum(spec_re * band_re + spec_im * band_im, axis=0)
+    cross_im = jnp.sum(spec_im * band_re - spec_re * band_im, axis=0)
+    frame_power = frame_power.reshape(stripes, count_frames, columns)
     partial = jnp.concatenate(
         [
             cross_re.reshape(stripes, count_frames * steps, columns),

time: 115 us -> 100 us (0.87)
  waiting for transfers between devices: 29.3 us -> 16.8 us
  other arithmetic: 24 us -> 21.2 us
    all_to_all x1, waiting for transfers between devices: 18.7 us -> 6.83 us  [per_device(): lax.all_to_all(packed, ('stripe', 'frame'), split_axis=0, concat_axis=0,...]
    reshape x0 -> x4, local copies, waits for them, and re-layouts: none -> 2.37 us  [the longest x1 2.1 us: per_device(): band = jnp.dot(visited, forward, preferred_element_type=jnp.float32).asty...]
    reduce_sum x2 -> x1, other arithmetic: 5.29 us -> 3.2 us  [per_device(): cross_re = jnp.sum(spec_re * band_re + spec_im * band_im, axis=0)]
    reduce_sum x0 -> x2, local copies, waits for them, and re-layouts: none -> 1.19 us  [the longest x1 1.08 us: per_device(): cross_re = jnp.sum(spec_re * band_re + spec_im * band_im, axis=0)]
    mul x1 -> x2, other arithmetic: 2.17 us -> 2.48 us  [per_device(): cross_re = jnp.sum(spec_re * band_re + spec_im * band_im, axis=0)]
  transfers between devices with their start and end apart: 3 -> 3, of which waited for: 3 -> 3; matrix products, arithmetic and copies ran while one was open for 28% -> 44% of each run, Pallas kernels for 0% -> 0%
where the time goes in v9:
time: 100 us; the launch traced here: 99 us
  other arithmetic  21.2 us (21%)
  matrix products  20.7 us (21%)
  starting transfers between devices  18.7 us (19%)
  waiting for transfers between devices  16.8 us (17%)
  local copies, waits for them, and re-layouts  16.7 us (17%)
  between operations  4.86 us (5%)
    all_to_all x1, starting transfers between devices, per_device(): lax.all_to_all(packed, ('stripe', 'frame'), split_axis=0, concat_axis=0,...  9.6 us
    dot_general x1, matrix products, per_device(): jnp.dot(frame_rows_in, forward, preferred_element_type=jnp.float32)  6.9 us
    all_to_all x1, waiting for transfers between devices, per_device(): lax.all_to_all(packed, ('stripe', 'frame'), split_axis=0, concat_axis=0,...  6.83 us
    convert_element_type x1, other arithmetic, dft_table(): return (cos_t.astype(jnp.bfloat16), nsin_t.astype(jnp.bfloat16))  6.79 us
    all_to_all x1, waiting for transfers between devices, per_device(): lax.all_to_all(partial, 'stripe', split_axis=0, concat_axis=0, tiled=True)  6.54 us
    dot_general x1, matrix products, per_device(): jnp.dot(visited, forward, preferred_element_type=jnp.float32)  5.53 us
    all_to_all x1, starting transfers between devices, per_device(): lax.all_to_all(outbound, 'stripe', split_axis=0, concat_axis=0, tiled=True)  5.51 us
    dot_general x1, matrix products, per_device(): lax.dot_general(coherence.reshape(count_frames * steps, 2 * columns), for...  5.1 us
  transfers between devices with their start and end apart: 3, of which 3 were waited for; matrix products, arithmetic and copies ran while one was open for 44% of the time, Pallas kernels for 0%

profile of v9, /device:TPU:0, one launch (start us, length us, event | category | flops | bytes accessed | tf_op | source)
XLA Modules:
  0.0 99.0 jit_solution(5241863576285643914)
XLA Ops:
  0.6 1.4 %copy.47 = bf16[8,2,16,2048]{3,2,1,0:T(8,128)(2,1)S(1)} copy(bf16[8,2,16,2048]{3,2,0,1:T(8,128)(2,1)} %bitcast.66) | data formatting | bytes 2097152 | tf_op jit(solution)/shard_map/transpose | solution.py:44
  2.1 2.4 %pad_maximum_fusion.7 = bf16[8,48,2048]{2,1,0:T(8,128)(2,1)} fusion(bf16[8,16,2048]{2,1,0:T(8,128)(2,1)} %bitcast.69, bf16[8,32,2048]{2,1,0:T(8,128)(2,1)S(1)} %bitcast.65), kind=kLoop, calls=%fused_computation.19 | loop fusion | flops 3145728 | bytes 3145728 | tf_op jit(solution)/shard_map/concatenate | solution.py:47
  4.4 5.5 %all-to-all-start = ((bf16[8,48,2048]{2,1,0:T(8,128)(2,1)}), bf16[8,48,2048]{2,1,0:T(8,128)(2,1)}, u32[]{:S(2)}, u32[]{:S(2)}) async-start(bf16[8,48,2048]{2,1,0:T(8,128)(2,1)} %pad_maximum_fusion.7), calls=%async_computation | async-start | bytes 3145728 | tf_op jit(solution)/shard_map/all_to_all | solution.py:48
  9.9 1.2 %fusion.29 = (f32[64,1152]{1,0:T(8,128)S(1)}, f32[64,1152]{1,0:T(8,128)S(1)}) fusion(), kind=kLoop, calls=%fused_computation.63 | loop fusion | flops 1032192 | bytes 589824 | tf_op jit(solution)/shard_map/sin | solution.py:19
  11.2 0.6 fusion.52
  15.7 0.6 select_select_fusion
  16.3 0.7 fusion.39
  18.2 0.9 fusion.16
  19.1 0.7 convolution_convert_fusion.1
  20.2 6.8 %subtract_convert_fusion = (bf16[32,64,1152]{2,1,0:T(8,128)(2,1)}, bf16[32,64,1152]{2,1,0:T(8,128)(2,1)}) fusion(f32[64,1152]{1,0:T(8,128)S(1)} %get-tuple-element.28, f32[32,1152]{1,0:T(8,128)S(1)} %get-tuple-element.27, f32[64,1152]{1,0:T(8,128)S(1)} %get-tuple-element.29, f32[32,1152]{1,0:T(8,128)S(1)} %get-tuple-element.26), kind=kLoop, calls=%fused_computation.5 | loop fusion | flops 21233664 | bytes 10321920 | tf_op jit(solution)/shard_map/convert_element_type | solution.py:22
  27.0 3.5 %all-to-all-done = bf16[8,48,2048]{2,1,0:T(8,128)(2,1)} async-done(((bf16[8,48,2048]{2,1,0:T(8,128)(2,1)}), bf16[8,48,2048]{2,1,0:T(8,128)(2,1)}, u32[]{:S(2)}, u32[]{:S(2)}) %all-to-all-start) | async-done | bytes 1572896 | tf_op jit(solution)/shard_map/all_to_all | solution.py:48
  30.5 1.1 %slice.62 = bf16[8,16,2048]{2,1,0:T(8,128)(2,1)S(1)} slice(bf16[8,48,2048]{2,1,0:T(8,128)(2,1)} %all-to-all-done), slice={[0:8], [32:48], [0:2048]} | slice | bytes 1048576 | tf_op jit(solution)/shard_map/slice | solution.py:80
  31.5 0.6 gather_fusion
  32.4 3.1 %copy.52 = bf16[128,4,2176]{2,1,0:T(4,128)(2,1)} copy(bf16[128,4,2176]{2,0,1:T(8,128)(2,1)S(1)} %pad_maximum_fusion.4) | data formatting | bytes 4456448 | tf_op jit(solution)/shard_map/optimization_barrier | solution.py:72
  35.5 9.6 %all-to-all-start.1 = ((bf16[128,4,2176]{2,1,0:T(4,128)(2,1)}), bf16[128,4,2176]{2,1,0:T(4,128)(2,1)S(1)}, u32[]{:S(2)}, u32[]{:S(2)}) async-start(bf16[128,4,2176]{2,1,0:T(4,128)(2,1)} %copy.52), calls=%async_computation.1 | async-start | bytes 4456448 | tf_op jit(solution)/shard_map/all_to_all | solution.py:73
  45.1 5.5 %fusion.5 = f32[64,2304]{1,0:T(8,128)} fusion(bf16[64,2048]{1,0:T(8,128)(2,1)S(1)} %reshape.244, bf16[2048,1152]{1,0:T(8,128)(2,1)} %bitcast.62, bf16[2048,1152]{1,0:T(8,128)(2,1)} %bitcast.59), kind=kOutput, calls=%fused_computation.10 | convolution fusion | flops 623149056 | bytes 10289152 | tf_op jit(solution)/shard_map/dot_general | solution.py:90
  50.6 1.3 %slice.60 = bf16[8,32,2048]{2,1,0:T(8,128)(2,1)S(1)} slice(bf16[8,48,2048]{2,1,0:T(8,128)(2,1)} %all-to-all-done), slice={[0:8], [0:32], [0:2048]} | slice | bytes 2097152 | tf_op jit(solution)/shard_map/slice | solution.py:75
  51.9 2.1 %reshape.251 = f32[16,1,4,2304]{3,2,0,1:T(4,128)} reshape(f32[64,2304]{1,0:T(8,128)} %fusion.5) | data formatting | bytes 1179648 | tf_op jit(solution)/shard_map/reshape | solution.py:93
  54.0 6.9 %fusion.2 = f32[16,16,1,2304]{3,1,0,2:T(8,128)S(1)} fusion(bf16[2048,1152]{1,0:T(8,128)(2,1)} %bitcast.63, bf16[2048,1152]{1,0:T(8,128)(2,1)} %bitcast.60, bf16[16,16,2048]{2,0,1:T(8,128)(2,1)S(1)} %bitcast.68), kind=kOutput, calls=%fused_computation.8 | convolution fusion | flops 2434793472 | bytes 12845056 | tf_op jit(solution)/shard_map/dot_general | solution.py:84
  60.9 1.3 %slice_bitcast_fusion.1 = (f32[16,16,1152]{2,1,0:T(8,128)S(1)}, f32[16,1152]{1,0:T(8,128)S(1)}, f32[16,16,1152]{2,1,0:T(8,128)}) fusion(f32[16,16,1,2304]{3,1,0,2:T(8,128)S(1)} %fusion.2), kind=kLoop, calls=%fused_computation.22 | loop fusion | flops 1161216 | bytes 4792320 | tf_op jit(solution)/shard_map/mul | solution.py:99
  62.2 1.2 %slice_bitcast_fusion.5 = (f32[16,4,1152]{2,1,0:T(4,128)S(1)}, f32[4,1152]{1,0:T(4,128)S(1)}, f32[16,4,1152]{2,1,0:T(4,128)S(1)}) fusion(f32[16,1,4,2304]{3,2,0,1:T(4,128)} %reshape.251), kind=kLoop, calls=%fused_computation.56 | loop fusion | flops 290304 | bytes 1198080 | tf_op jit(solution)/shard_map/mul | solution.py:99
  63.4 3.2 %add_reduce_fusion = (f32[16,4,1152]{2,0,1:T(8,128)}, f32[16,4,1152]{2,0,1:T(8,128)S(1)}) fusion(f32[16,4,1152]{2,1,0:T(4,128)S(1)} %get-tuple-element.21, f32[16,16,1152]{2,1,0:T(8,128)} %get-tuple-element.14, f32[16,4,1152]{2,1,0:T(4,128)S(1)} %get-tuple-element.19, f32[16,16,1152]{2,1,0:T(8,128)S(1)} %get-tuple-element.12), kind=kLoop, calls=%fused_computation.7 | loop fusion | flops 9289728 | bytes 3538944 | tf_op jit(solution)/shard_map/reduce_sum | solution.py:99
  66.9 1.1 %copy.50 = f32[16,4,1152]{2,1,0:T(4,128)S(1)} copy(f32[16,4,1152]{2,0,1:T(8,128)} %get-tuple-element.10) | data formatting | bytes 589824 | tf_op jit(solution)/shard_map/reduce_sum | solution.py:99
  68.1 1.0 %pad_maximum_fusion.8 = f32[8,22,1152]{2,1,0:T(8,128)} fusion(f32[8,4,1152]{2,1,0:T(4,128)S(1)} %broadcast_in_dim.41, f32[8,2,1152]{2,1,0:T(2,128)S(1)} %reshape_squeeze.3, f32[8,8,1152]{2,1,0:T(8,128)S(1)} %reshape.248, f32[8,8,1152]{2,1,0:T(8,128)S(1)} %reshape.247), kind=kLoop, calls=%fused_computation.31 | loop fusion | flops 608256 | bytes 1622016 | tf_op jit(solution)/shard_map/concatenate | solution.py:102
  69.1 6.8 %all-to-all-done.1 = bf16[128,4,2176]{2,1,0:T(4,128)(2,1)S(1)} async-done(((bf16[128,4,2176]{2,1,0:T(4,128)(2,1)}), bf16[128,4,2176]{2,1,0:T(4,128)(2,1)S(1)}, u32[]{:S(2)}, u32[]{:S(2)}) %all-to-all-start.1) | async-done | bytes 2228256 | tf_op jit(solution)/shard_map/all_to_all | solution.py:73
  75.9 3.6 %all-to-all-start.2 = ((f32[8,22,1152]{2,1,0:T(8,128)}), f32[8,22,1152]{2,1,0:T(8,128)S(1)}, u32[]{:S(2)}, u32[]{:S(2)}) async-start(f32[8,22,1152]{2,1,0:T(8,128)} %pad_maximum_fusion.8), calls=%async_computation.2 | async-start | bytes 1769472 | tf_op jit(solution)/shard_map/all_to_all | solution.py:113
  79.5 3.6 %copy.54 = bf16[128,4,2176]{0,1,2:T(4,128)(2,1)} copy(bf16[128,4,2176]{2,1,0:T(4,128)(2,1)S(1)} %all-to-all-done.1) | data formatting | bytes 4456448 | tf_op jit(solution)/shard_map/optimization_barrier | solution.py:111
  83.1 0.6 fusion.47
  84.1 2.5 %fusion.8 = f32[128,2048]{1,0:T(8,128)} fusion(bf16[128,4,2176]{2,0,1:T(8,128)(2,1)S(1)} %copy.55, bf16[128,2048]{1,0:T(8,128)(2,1)} %param.6, f32[128]{0:T(128)S(1)} %broadcast_add_fusion, f32[128,4]{0,1:T(4,128)S(1)} %fusion.47), kind=kOutput, calls=%fused_computation.15 | convolution fusion | flops 269287424 | bytes 3672576 | tf_op jit(solution)/shard_map/tps,psx->tx/dot_general | solution.py:136
  86.5 6.5 %all-to-all-done.2 = f32[8,22,1152]{2,1,0:T(8,128)S(1)} async-done(((f32[8,22,1152]{2,1,0:T(8,128)}), f32[8,22,1152]{2,1,0:T(8,128)S(1)}, u32[]{:S(2)}, u32[]{:S(2)}) %all-to-all-start.2) | async-done | bytes 811040 | tf_op jit(solution)/shard_map/all_to_all | solution.py:113
  93.2 5.1 %fusion.9 = f32[8,2048]{1,0:T(8,128)S(1)} fusion(bf16[2048,1152]{1,0:T(8,128)(2,1)} %bitcast.64, bf16[2048,1152]{1,0:T(8,128)(2,1)} %bitcast.61, bf16[8,1152]{1,0:T(8,128)(2,1)S(1)} %get-tuple-element.23, bf16[8,1152]{1,0:T(8,128)(2,1)S(1)} %get-tuple-element.22), kind=kOutput, calls=%fused_computation.17 | convolution fusion | flops 94461952 | bytes 9539584 | tf_op jit(solution)/shard_map/dot_general | solution.py:125
  98.3 0.7 reshape.249
  (46 shorter events, 2.7 us)
Async XLA Ops:
  0.6 10.5 %copy-start = (bf16[2,128,2048]{2,1,0:T(8,128)(2,1)S(1)}, bf16[2,128,2048]{2,1,0:T(8,128)(2,1)}, u32[]{:S(2)}) copy-start(bf16[2,128,2048]{2,1,0:T(8,128)(2,1)} %param.7) | copy-start | bytes 3145732
  2.0 9.2 %copy-start.3 = (s32[2]{0:T(128)S(1)}, s32[2]{0:T(128)}, u32[]{:S(2)}) copy-start(s32[2]{0:T(128)} %param.8) | copy-start | bytes 28
  2.0 14.9 %copy-start.2 = (s32[256,1]{0,1:T(1,128)S(1)}, s32[256,1]{0,1:T(1,128)}, u32[]{:S(2)}) copy-start(s32[256,1]{0,1:T(1,128)} %param.9) | copy-start | bytes 3076
  2.0 15.8 %copy-start.4 = (s32[256]{0:T(256)S(1)}, s32[256]{0:T(256)}, u32[]{:S(2)}) copy-start(s32[256]{0:T(256)} %param.10) | copy-start | bytes 3076
  2.1 16.1 %copy-start.5 = (s32[4]{0:T(128)S(1)}, s32[4]{0:T(128)}, u32[]{:S(2)}) copy-start(s32[4]{0:T(128)} %param.11) | copy-start | bytes 52
  4.4 26.0 %all-to-all-start = ((bf16[8,48,2048]{2,1,0:T(8,128)(2,1)}), bf16[8,48,2048]{2,1,0:T(8,128)(2,1)}, u32[]{:S(2)}, u32[]{:S(2)}) async-start(bf16[8,48,2048]{2,1,0:T(8,128)(2,1)} %pad_maximum_fusion.7), calls=%async_computation | async-start | bytes 3145728 | tf_op jit(solution)/shard_map/all_to_all | solution.py:48
  35.5 40.5 %all-to-all-start.1 = ((bf16[128,4,2176]{2,1,0:T(4,128)(2,1)}), bf16[128,4,2176]{2,1,0:T(4,128)(2,1)S(1)}, u32[]{:S(2)}, u32[]{:S(2)}) async-start(bf16[128,4,2176]{2,1,0:T(4,128)(2,1)} %copy.52), calls=%async_computation.1 | async-start | bytes 4456448 | tf_op jit(solution)/shard_map/all_to_all | solution.py:73
  75.9 17.1 %all-to-all-start.2 = ((f32[8,22,1152]{2,1,0:T(8,128)}), f32[8,22,1152]{2,1,0:T(8,128)S(1)}, u32[]{:S(2)}, u32[]{:S(2)}) async-start(f32[8,22,1152]{2,1,0:T(8,128)} %pad_maximum_fusion.8), calls=%async_computation.2 | async-start | bytes 1769472 | tf_op jit(solution)/shard_map/all_to_all | solution.py:113
  83.9 9.3 %copy-start.1 = (f32[1152]{0:T(1024)S(1)}, f32[1152]{0:T(1024)}, u32[]{:S(2)}) copy-start(f32[1152]{0:T(1024)} %select_select_fusion) | copy-start | bytes 13828

commit v10 on v9

--- a/solution.py
+++ b/solution.py
@@ -69,7 +69,6 @@
     lanes = 128
     index_cols = jnp.broadcast_to(out_index[:, :, None], (num_devices, capacity, lanes))
     packed = jnp.concatenate([outgoing, index_cols], axis=2)
-    packed, inbound = lax.optimization_barrier((packed, inbound))
     received = lax.all_to_all(packed, ("stripe", "frame"), split_axis=0, concat_axis=0, tiled=True)
     frame_rows_in = (
         inbound[:, : count_frames * chunk]

time: 100 us -> 100 us (level)
  waiting for transfers between devices: 16.8 us -> 12.7 us
  other arithmetic: 21.2 us -> 23 us
  starting transfers between devices: 18.7 us -> 20.4 us
    all_to_all x1, waiting for transfers between devices: 3.46 us -> 0.01 us  [per_device(): lax.all_to_all(outbound, 'stripe', split_axis=0, concat_axis=0, tiled=True)]
    concatenate x0 -> x1, local copies, waits for them, and re-layouts: none -> 3.08 us  [per_device(): packed = jnp.concatenate([outgoing, index_cols], axis=2)]
    optimization_barrier x1 -> x0, local copies, waits for them, and re-layouts: 3.08 us -> none  [per_device(): packed, inbound = lax.optimization_barrier((packed, inbound))]
    all_to_all x1, starting transfers between devices: 9.6 us -> 11.3 us  [per_device(): lax.all_to_all(packed, ('stripe', 'frame'), split_axis=0, concat_axis=0,...]
    slice x1 -> x2, local copies, waits for them, and re-layouts: 1.29 us -> 0.01 us  [per_device(): inbound[:, :count_frames * chunk]]
    unnamed x12 -> x16, local copies, waits for them, and re-layouts: 0.04 us -> 1.24 us
    concatenate x1, other arithmetic: 0.92 us -> 1.96 us  [shift_rows(): doubled = jnp.concatenate([frame_img, frame_img], axis=1)]
  transfers between devices with their start and end apart: 3 -> 3, of which waited for: 3 -> 2; matrix products, arithmetic and copies ran while one was open for 44% -> 51% of each run, Pallas kernels for 0% -> 0%
where the time goes in v10:
time: 100 us; the launch traced here: 98.7 us
  other arithmetic  23 us (23%)
  matrix products  20.8 us (21%)
  starting transfers between devices  20.4 us (20%)
  local copies, waits for them, and re-layouts  17.3 us (17%)
  waiting for transfers between devices  12.7 us (13%)
  between operations  4.53 us (5%)
    all_to_all x1, starting transfers between devices, per_device(): lax.all_to_all(packed, ('stripe', 'frame'), split_axis=0, concat_axis=0,...  11.3 us
    dot_general x1, matrix products, per_device(): jnp.dot(frame_rows_in, forward, preferred_element_type=jnp.float32)  6.9 us
    convert_element_type x1, other arithmetic, dft_table(): return (cos_t.astype(jnp.bfloat16), nsin_t.astype(jnp.bfloat16))  6.79 us
    all_to_all x1, waiting for transfers between devices, per_device(): lax.all_to_all(partial, 'stripe', split_axis=0, concat_axis=0, tiled=True)  6.54 us
    all_to_all x1, waiting for transfers between devices, per_device(): lax.all_to_all(packed, ('stripe', 'frame'), split_axis=0, concat_axis=0,...  6.12 us
    dot_general x1, matrix products, per_device(): jnp.dot(visited, forward, preferred_element_type=jnp.float32)  5.6 us
    all_to_all x1, starting transfers between devices, per_device(): lax.all_to_all(outbound, 'stripe', split_axis=0, concat_axis=0, tiled=True)  5.51 us
    dot_general x1, matrix products, per_device(): lax.dot_general(coherence.reshape(count_frames * steps, 2 * columns), for...  5.1 us
  transfers between devices with their start and end apart: 3, of which 2 were waited for; matrix products, arithmetic and copies ran while one was open for 51% of the time, Pallas kernels for 0%

profile of v10, /device:TPU:0, one launch (start us, length us, event | category | flops | bytes accessed | tf_op | source)
XLA Modules:
  0.0 98.7 jit_solution(7835961745931329007)
XLA Ops:
  0.6 1.4 %copy.45 = bf16[8,2,16,2048]{3,2,1,0:T(8,128)(2,1)S(1)} copy(bf16[8,2,16,2048]{3,2,0,1:T(8,128)(2,1)} %bitcast.67) | data formatting | bytes 2097152 | tf_op jit(solution)/shard_map/transpose | solution.py:44
  2.1 2.4 %pad_maximum_fusion.7 = bf16[8,48,2048]{2,1,0:T(8,128)(2,1)} fusion(bf16[8,16,2048]{2,1,0:T(8,128)(2,1)} %bitcast.69, bf16[8,32,2048]{2,1,0:T(8,128)(2,1)S(1)} %bitcast.66), kind=kLoop, calls=%fused_computation.19 | loop fusion | flops 3145728 | bytes 3145728 | tf_op jit(solution)/shard_map/concatenate | solution.py:47
  4.5 5.5 %all-to-all-start = ((bf16[8,48,2048]{2,1,0:T(8,128)(2,1)}), bf16[8,48,2048]{2,1,0:T(8,128)(2,1)S(1)}, u32[]{:S(2)}, u32[]{:S(2)}) async-start(bf16[8,48,2048]{2,1,0:T(8,128)(2,1)} %pad_maximum_fusion.7), calls=%async_computation | async-start | bytes 3145728 | tf_op jit(solution)/shard_map/all_to_all | solution.py:48
  10.0 1.8 %fusion.29 = (f32[64,1152]{1,0:T(8,128)S(1)}, f32[64,1152]{1,0:T(8,128)}) fusion(), kind=kLoop, calls=%fused_computation.63 | loop fusion | flops 1032192 | bytes 589824 | tf_op jit(solution)/shard_map/sin | solution.py:19
  11.8 0.9 slice_bitcast_fusion.3
  12.7 0.6 fusion.52
  16.8 0.6 select_select_fusion
  18.6 2.0 %fusion.16 = (bf16[128,2048]{1,0:T(8,128)(2,1)S(1)}, bf16[128,2048]{1,0:T(8,128)(2,1)S(1)}) fusion(s32[]{:T(128)S(6)} %select_n.72, bf16[128,2048]{1,0:T(8,128)(2,1)} %get-tuple-element.12, s32[]{:T(128)S(6)} %select_n.71, bf16[128,2048]{1,0:T(8,128)(2,1)S(1)} %get-tuple-element.11), kind=kLoop, calls=%fused_computation.36 | loop fusion | flops 2097152 | bytes 2097160 | tf_op jit(solution)/shard_map/concatenate | solution.py:27
  20.6 0.7 convolution_convert_fusion.1
  21.7 3.1 %copy.52 = bf16[128,4,2176]{2,1,0:T(4,128)(2,1)} copy(bf16[128,4,2176]{2,0,1:T(8,128)(2,1)S(1)} %pad_maximum_fusion.4) | data formatting | bytes 4456448 | tf_op jit(solution)/shard_map/concatenate | solution.py:71
  24.8 0.7 fusion.39
  25.5 6.8 %subtract_convert_fusion = (bf16[32,64,1152]{2,1,0:T(8,128)(2,1)}, bf16[32,64,1152]{2,1,0:T(8,128)(2,1)}) fusion(f32[64,1152]{1,0:T(8,128)S(1)} %get-tuple-element.24, f32[32,1152]{1,0:T(8,128)S(1)} %get-tuple-element.23, f32[64,1152]{1,0:T(8,128)S(1)} %copy-done.2, f32[32,1152]{1,0:T(8,128)S(1)} %get-tuple-element.22), kind=kLoop, calls=%fused_computation.5 | loop fusion | flops 21233664 | bytes 10321920 | tf_op jit(solution)/shard_map/convert_element_type | solution.py:22
  32.3 1.2 %copy-done = bf16[8,48,2048]{2,1,0:T(8,128)(2,1)} copy-done((bf16[8,48,2048]{2,1,0:T(8,128)(2,1)}, bf16[8,48,2048]{2,1,0:T(8,128)(2,1)S(1)}, u32[]{:S(2)}) %copy-start) | copy-done | bytes 1572888
  33.5 11.3 %all-to-all-start.1 = ((bf16[128,4,2176]{2,1,0:T(4,128)(2,1)}), bf16[128,4,2176]{2,1,0:T(4,128)(2,1)S(1)}, u32[]{:S(2)}, u32[]{:S(2)}) async-start(bf16[128,4,2176]{2,1,0:T(4,128)(2,1)} %copy.52), calls=%async_computation.1 | async-start | bytes 4456448 | tf_op jit(solution)/shard_map/all_to_all | solution.py:72
  44.8 1.1 %slice.76 = bf16[8,16,2048]{2,1,0:T(8,128)(2,1)S(1)} slice(bf16[8,48,2048]{2,1,0:T(8,128)(2,1)} %copy-done), slice={[0:8], [32:48], [0:2048]} | slice | bytes 1048576 | tf_op jit(solution)/shard_map/slice | solution.py:79
  45.9 0.6 gather_fusion
  46.8 5.6 %fusion.5 = f32[64,2304]{1,0:T(8,128)} fusion(bf16[64,2048]{1,0:T(8,128)(2,1)S(1)} %reshape.243, bf16[2048,1152]{1,0:T(8,128)(2,1)} %bitcast.63, bf16[2048,1152]{1,0:T(8,128)(2,1)} %bitcast.60), kind=kOutput, calls=%fused_computation.10 | convolution fusion | flops 623149056 | bytes 10289152 | tf_op jit(solution)/shard_map/dot_general | solution.py:89
  52.4 2.1 %reshape.251 = f32[16,1,4,2304]{3,2,0,1:T(4,128)} reshape(f32[64,2304]{1,0:T(8,128)} %fusion.5) | data formatting | bytes 1179648 | tf_op jit(solution)/shard_map/reshape | solution.py:92
  54.5 6.9 %fusion.2 = f32[16,16,1,2304]{3,1,0,2:T(8,128)S(1)} fusion(bf16[2048,1152]{1,0:T(8,128)(2,1)} %bitcast.64, bf16[2048,1152]{1,0:T(8,128)(2,1)} %bitcast.61, bf16[16,16,2048]{2,0,1:T(8,128)(2,1)S(1)} %bitcast.59), kind=kOutput, calls=%fused_computation.8 | convolution fusion | flops 2434793472 | bytes 12845056 | tf_op jit(solution)/shard_map/dot_general | solution.py:83
  61.4 1.3 %slice_bitcast_fusion.1 = (f32[16,16,1152]{2,1,0:T(8,128)S(1)}, f32[16,1152]{1,0:T(8,128)S(1)}, f32[16,16,1152]{2,1,0:T(8,128)}) fusion(f32[16,16,1,2304]{3,1,0,2:T(8,128)S(1)} %fusion.2), kind=kLoop, calls=%fused_computation.22 | loop fusion | flops 1161216 | bytes 4792320 | tf_op jit(solution)/shard_map/mul | solution.py:98
  62.7 1.2 %slice_bitcast_fusion.5 = (f32[16,4,1152]{2,1,0:T(4,128)S(1)}, f32[4,1152]{1,0:T(4,128)S(1)}, f32[16,4,1152]{2,1,0:T(4,128)S(1)}) fusion(f32[16,1,4,2304]{3,2,0,1:T(4,128)} %reshape.251), kind=kLoop, calls=%fused_computation.56 | loop fusion | flops 290304 | bytes 1198080 | tf_op jit(solution)/shard_map/mul | solution.py:98
  63.9 3.2 %add_reduce_fusion = (f32[16,4,1152]{2,0,1:T(8,128)}, f32[16,4,1152]{2,0,1:T(8,128)S(1)}) fusion(f32[16,4,1152]{2,1,0:T(4,128)S(1)} %get-tuple-element.17, f32[16,16,1152]{2,1,0:T(8,128)} %get-tuple-element.10, f32[16,4,1152]{2,1,0:T(4,128)S(1)} %get-tuple-element.15, f32[16,16,1152]{2,1,0:T(8,128)S(1)} %get-tuple-element.8), kind=kLoop, calls=%fused_computation.7 | loop fusion | flops 9289728 | bytes 3538944 | tf_op jit(solution)/shard_map/reduce_sum | solution.py:98
  67.3 1.1 %copy.48 = f32[16,4,1152]{2,1,0:T(4,128)S(1)} copy(f32[16,4,1152]{2,0,1:T(8,128)} %get-tuple-element.6) | data formatting | bytes 589824 | tf_op jit(solution)/shard_map/reduce_sum | solution.py:98
  68.5 1.0 %pad_maximum_fusion.8 = f32[8,22,1152]{2,1,0:T(8,128)} fusion(f32[8,4,1152]{2,1,0:T(4,128)S(1)} %broadcast_in_dim.37, f32[8,2,1152]{2,1,0:T(2,128)S(1)} %reshape_squeeze.3, f32[8,8,1152]{2,1,0:T(8,128)S(1)} %reshape.247, f32[8,8,1152]{2,1,0:T(8,128)S(1)} %reshape.246), kind=kLoop, calls=%fused_computation.31 | loop fusion | flops 608256 | bytes 1622016 | tf_op jit(solution)/shard_map/concatenate | solution.py:101
  69.6 6.1 %all-to-all-done.1 = bf16[128,4,2176]{2,1,0:T(4,128)(2,1)S(1)} async-done(((bf16[128,4,2176]{2,1,0:T(4,128)(2,1)}), bf16[128,4,2176]{2,1,0:T(4,128)(2,1)S(1)}, u32[]{:S(2)}, u32[]{:S(2)}) %all-to-all-start.1) | async-done | bytes 2228256 | tf_op jit(solution)/shard_map/all_to_all | solution.py:72
  75.7 3.6 %all-to-all-start.2 = ((f32[8,22,1152]{2,1,0:T(8,128)}), f32[8,22,1152]{2,1,0:T(8,128)S(1)}, u32[]{:S(2)}, u32[]{:S(2)}) async-start(f32[8,22,1152]{2,1,0:T(8,128)} %pad_maximum_fusion.8), calls=%async_computation.2 | async-start | bytes 1769472 | tf_op jit(solution)/shard_map/all_to_all | solution.py:112
  79.2 3.6 %copy.54 = bf16[128,4,2176]{0,1,2:T(4,128)(2,1)} copy(bf16[128,4,2176]{2,1,0:T(4,128)(2,1)S(1)} %all-to-all-done.1) | data formatting | bytes 4456448 | tf_op jit(solution)/shard_map/optimization_barrier | solution.py:110
  82.8 0.6 fusion.47
  83.8 2.5 %fusion.8 = f32[128,2048]{1,0:T(8,128)} fusion(bf16[128,4,2176]{2,0,1:T(8,128)(2,1)S(1)} %copy.55, bf16[128,2048]{1,0:T(8,128)(2,1)} %param.6, f32[128]{0:T(128)S(1)} %broadcast_add_fusion, f32[128,4]{0,1:T(4,128)S(1)} %fusion.47), kind=kOutput, calls=%fused_computation.15 | convolution fusion | flops 269287424 | bytes 3672576 | tf_op jit(solution)/shard_map/tps,psx->tx/dot_general | solution.py:135
  86.3 6.5 %all-to-all-done.2 = f32[8,22,1152]{2,1,0:T(8,128)S(1)} async-done(((f32[8,22,1152]{2,1,0:T(8,128)}), f32[8,22,1152]{2,1,0:T(8,128)S(1)}, u32[]{:S(2)}, u32[]{:S(2)}) %all-to-all-start.2) | async-done | bytes 811040 | tf_op jit(solution)/shard_map/all_to_all | solution.py:112
  93.0 5.1 %fusion.9 = f32[8,2048]{1,0:T(8,128)S(1)} fusion(bf16[2048,1152]{1,0:T(8,128)(2,1)} %bitcast.65, bf16[2048,1152]{1,0:T(8,128)(2,1)} %bitcast.62, bf16[8,1152]{1,0:T(8,128)(2,1)S(1)} %get-tuple-element.19, bf16[8,1152]{1,0:T(8,128)(2,1)S(1)} %get-tuple-element.18), kind=kOutput, calls=%fused_computation.17 | convolution fusion | flops 94461952 | bytes 9539584 | tf_op jit(solution)/shard_map/dot_general | solution.py:124
  98.1 0.7 reshape.249
  (51 shorter events, 2.7 us)
Async XLA Ops:
  0.6 11.2 %copy-start.1 = (bf16[2,128,2048]{2,1,0:T(8,128)(2,1)S(1)}, bf16[2,128,2048]{2,1,0:T(8,128)(2,1)}, u32[]{:S(2)}) copy-start(bf16[2,128,2048]{2,1,0:T(8,128)(2,1)} %param.7) | copy-start | bytes 3145732
  2.0 10.7 %copy-start.5 = (s32[2]{0:T(128)S(1)}, s32[2]{0:T(128)}, u32[]{:S(2)}) copy-start(s32[2]{0:T(128)} %param.8) | copy-start | bytes 28
  2.0 15.4 %copy-start.7 = (s32[4]{0:T(128)S(1)}, s32[4]{0:T(128)}, u32[]{:S(2)}) copy-start(s32[4]{0:T(128)} %param.11) | copy-start | bytes 52
  2.0 15.4 %copy-start.4 = (s32[256,1]{0,1:T(1,128)S(1)}, s32[256,1]{0,1:T(1,128)}, u32[]{:S(2)}) copy-start(s32[256,1]{0,1:T(1,128)} %param.9) | copy-start | bytes 3076
  2.1 16.3 %copy-start.6 = (s32[256]{0:T(256)S(1)}, s32[256]{0:T(256)}, u32[]{:S(2)}) copy-start(s32[256]{0:T(256)} %param.10) | copy-start | bytes 3076
  4.5 27.8 %all-to-all-start = ((bf16[8,48,2048]{2,1,0:T(8,128)(2,1)}), bf16[8,48,2048]{2,1,0:T(8,128)(2,1)S(1)}, u32[]{:S(2)}, u32[]{:S(2)}) async-start(bf16[8,48,2048]{2,1,0:T(8,128)(2,1)} %pad_maximum_fusion.7), calls=%async_computation | async-start | bytes 3145728 | tf_op jit(solution)/shard_map/all_to_all | solution.py:48
  21.4 4.1 %copy-start.2 = (f32[64,1152]{1,0:T(8,128)S(1)}, f32[64,1152]{1,0:T(8,128)}, u32[]{:S(2)}) copy-start(f32[64,1152]{1,0:T(8,128)} %get-tuple-element.25) | copy-start | bytes 884740
  32.3 1.2 %copy-start = (bf16[8,48,2048]{2,1,0:T(8,128)(2,1)}, bf16[8,48,2048]{2,1,0:T(8,128)(2,1)S(1)}, u32[]{:S(2)}) copy-start(bf16[8,48,2048]{2,1,0:T(8,128)(2,1)S(1)} %all-to-all-done) | copy-start | bytes 4718596
  33.5 42.2 %all-to-all-start.1 = ((bf16[128,4,2176]{2,1,0:T(4,128)(2,1)}), bf16[128,4,2176]{2,1,0:T(4,128)(2,1)S(1)}, u32[]{:S(2)}, u32[]{:S(2)}) async-start(bf16[128,4,2176]{2,1,0:T(4,128)(2,1)} %copy.52), calls=%async_computation.1 | async-start | bytes 4456448 | tf_op jit(solution)/shard_map/all_to_all | solution.py:72
  46.8 7.7 %slice-start = ((bf16[8,48,2048]{2,1,0:T(8,128)(2,1)}), bf16[8,32,2048]{2,1,0:T(8,128)(2,1)S(1)}, s32[]{:S(2)}) async-start(bf16[8,48,2048]{2,1,0:T(8,128)(2,1)} %copy-done), calls=%async_computation.3 | async-start | bytes 2097152 | tf_op jit(solution)/shard_map/slice | solution.py:74
  75.7 17.1 %all-to-all-start.2 = ((f32[8,22,1152]{2,1,0:T(8,128)}), f32[8,22,1152]{2,1,0:T(8,128)S(1)}, u32[]{:S(2)}, u32[]{:S(2)}) async-start(f32[8,22,1152]{2,1,0:T(8,128)} %pad_maximum_fusion.8), calls=%async_computation.2 | async-start | bytes 1769472 | tf_op jit(solution)/shard_map/all_to_all | solution.py:112
  83.7 9.3 %copy-start.3 = (f32[1152]{0:T(1024)S(1)}, f32[1152]{0:T(1024)}, u32[]{:S(2)}) copy-start(f32[1152]{0:T(1024)} %select_select_fusion) | copy-start | bytes 13828

commit v11 on v10

--- a/solution.py
+++ b/solution.py
@@ -120,12 +120,24 @@
     magnitude = jnp.sqrt(frame_power[:, None, :] * band_power[None, :, :] + 1e-06)
     coh_re = (cross_re / magnitude).astype(jnp.bfloat16).astype(jnp.float32) * weight
     coh_im = (cross_im / magnitude).astype(jnp.bfloat16).astype(jnp.float32) * weight
-    coherence = jnp.concatenate([coh_re, coh_im], axis=2).astype(jnp.bfloat16)
-    surface = lax.dot_general(
-        coherence.reshape(count_frames * steps, 2 * columns),
-        forward,
+    zeros = jnp.zeros_like(coh_re)
+    coherence = jnp.concatenate(
+        [
+            jnp.concatenate([coh_re, zeros], axis=2),
+            jnp.concatenate([zeros, coh_im], axis=2),
+        ],
+        axis=0,
+    ).astype(jnp.bfloat16)
+    parts = lax.dot_general(
+        coherence.reshape(2 * count_frames * steps, 2 * columns),
+        forward[:columns],
         (((1,), (1,)), ((), ())),
         preferred_element_type=jnp.float32,
+    )
+    even = parts[: count_frames * steps]
+    odd = parts[count_frames * steps :]
+    surface = jnp.concatenate(
+        [(even + odd)[:, : half + 1], lax.rev((even - odd)[:, 1:half], (1,))], axis=1
     )
     correlation = (surface * math.sqrt(band_rows / pixels)).reshape(count_frames, steps, pixels)
 

time: 100 us -> 99.7 us (level)
  matrix products: 20.8 us -> 19.4 us
    dot_general x1, matrix products: 5.1 us -> 3.66 us  [per_device(): lax.dot_general(coherence.reshape(2 * count_frames * steps, 2 * columns),...]
where the time goes in v11:
time: 99.7 us; the launch traced here: 98.5 us
  other arithmetic  23.8 us (24%)
  starting transfers between devices  20.4 us (20%)
  matrix products  19.4 us (19%)
  local copies, waits for them, and re-layouts  17.5 us (18%)
  waiting for transfers between devices  12.7 us (13%)
  between operations  4.72 us (5%)
    all_to_all x1, starting transfers between devices, per_device(): lax.all_to_all(packed, ('stripe', 'frame'), split_axis=0, concat_axis=0,...  11.4 us
    dot_general x1, matrix products, per_device(): jnp.dot(frame_rows_in, forward, preferred_element_type=jnp.float32)  6.9 us
    convert_element_type x1, other arithmetic, dft_table(): return (cos_t.astype(jnp.bfloat16), nsin_t.astype(jnp.bfloat16))  6.79 us
    all_to_all x1, waiting for transfers between devices, per_device(): lax.all_to_all(partial, 'stripe', split_axis=0, concat_axis=0, tiled=True)  6.54 us
    all_to_all x1, waiting for transfers between devices, per_device(): lax.all_to_all(packed, ('stripe', 'frame'), split_axis=0, concat_axis=0,...  6.12 us
    dot_general x1, matrix products, per_device(): jnp.dot(visited, forward, preferred_element_type=jnp.float32)  5.6 us
    all_to_all x1, starting transfers between devices, per_device(): lax.all_to_all(outbound, 'stripe', split_axis=0, concat_axis=0, tiled=True)  5.51 us
    optimization_barrier x2, local copies, waits for them, and re-layouts, per_device(): partial, received = lax.optimization_barrier((partial, received))  3.78 us
  transfers between devices with their start and end apart: 3, of which 2 were waited for; matrix products, arithmetic and copies ran while one was open for 51% of the time, Pallas kernels for 0%

profile of v11, /device:TPU:0, one launch (start us, length us, event | category | flops | bytes accessed | tf_op | source)
XLA Modules:
  0.0 98.5 jit_solution(6744875486069292965)
XLA Ops:
  0.6 1.4 %copy.45 = bf16[8,2,16,2048]{3,2,1,0:T(8,128)(2,1)S(1)} copy(bf16[8,2,16,2048]{3,2,0,1:T(8,128)(2,1)} %bitcast.69) | data formatting | bytes 2097152 | tf_op jit(solution)/shard_map/transpose | solution.py:44
  2.1 2.4 %pad_maximum_fusion.8 = bf16[8,48,2048]{2,1,0:T(8,128)(2,1)} fusion(bf16[8,16,2048]{2,1,0:T(8,128)(2,1)} %bitcast.71, bf16[8,32,2048]{2,1,0:T(8,128)(2,1)S(1)} %bitcast.68), kind=kLoop, calls=%fused_computation.22 | loop fusion | flops 3145728 | bytes 3145728 | tf_op jit(solution)/shard_map/concatenate | solution.py:47
  4.5 5.5 %all-to-all-start = ((bf16[8,48,2048]{2,1,0:T(8,128)(2,1)}), bf16[8,48,2048]{2,1,0:T(8,128)(2,1)S(1)}, u32[]{:S(2)}, u32[]{:S(2)}) async-start(bf16[8,48,2048]{2,1,0:T(8,128)(2,1)} %pad_maximum_fusion.8), calls=%async_computation | async-start | bytes 3145728 | tf_op jit(solution)/shard_map/all_to_all | solution.py:48
  10.0 0.6 select_select_fusion
  10.6 1.8 %fusion.32 = (f32[64,1152]{1,0:T(8,128)S(1)}, f32[64,1152]{1,0:T(8,128)}) fusion(), kind=kLoop, calls=%fused_computation.68 | loop fusion | flops 1032192 | bytes 589824 | tf_op jit(solution)/shard_map/sin | solution.py:19
  12.4 0.9 slice_bitcast_fusion.3
  13.3 0.7 fusion.59
  18.9 2.0 %fusion.19 = (bf16[128,2048]{1,0:T(8,128)(2,1)S(1)}, bf16[128,2048]{1,0:T(8,128)(2,1)S(1)}) fusion(s32[]{:T(128)S(6)} %select_n.72, bf16[128,2048]{1,0:T(8,128)(2,1)} %get-tuple-element.12, s32[]{:T(128)S(6)} %select_n.71, bf16[128,2048]{1,0:T(8,128)(2,1)S(1)} %get-tuple-element.11), kind=kLoop, calls=%fused_computation.39 | loop fusion | flops 2097152 | bytes 2097160 | tf_op jit(solution)/shard_map/concatenate | solution.py:27
  20.8 0.7 convolution_convert_fusion
  22.0 3.1 %copy.52 = bf16[128,4,2176]{2,1,0:T(4,128)(2,1)} copy(bf16[128,4,2176]{2,0,1:T(8,128)(2,1)S(1)} %pad_maximum_fusion.7) | data formatting | bytes 4456448 | tf_op jit(solution)/shard_map/concatenate | solution.py:71
  25.0 0.7 fusion.45
  25.7 6.8 %subtract_convert_fusion = (bf16[32,64,1152]{2,1,0:T(8,128)(2,1)}, bf16[32,64,1152]{2,1,0:T(8,128)(2,1)}) fusion(f32[64,1152]{1,0:T(8,128)S(1)} %get-tuple-element.28, f32[32,1152]{1,0:T(8,128)S(1)} %get-tuple-element.27, f32[64,1152]{1,0:T(8,128)S(1)} %copy-done.2, f32[32,1152]{1,0:T(8,128)S(1)} %get-tuple-element.26), kind=kLoop, calls=%fused_computation.7 | loop fusion | flops 21233664 | bytes 10321920 | tf_op jit(solution)/shard_map/convert_element_type | solution.py:22
  32.5 1.2 %copy-done = bf16[8,48,2048]{2,1,0:T(8,128)(2,1)} copy-done((bf16[8,48,2048]{2,1,0:T(8,128)(2,1)}, bf16[8,48,2048]{2,1,0:T(8,128)(2,1)S(1)}, u32[]{:S(2)}) %copy-start) | copy-done | bytes 1572888
  33.7 11.4 %all-to-all-start.1 = ((bf16[128,4,2176]{2,1,0:T(4,128)(2,1)}), bf16[128,4,2176]{2,1,0:T(4,128)(2,1)S(1)}, u32[]{:S(2)}, u32[]{:S(2)}) async-start(bf16[128,4,2176]{2,1,0:T(4,128)(2,1)} %copy.52), calls=%async_computation.1 | async-start | bytes 4456448 | tf_op jit(solution)/shard_map/all_to_all | solution.py:72
  45.1 1.1 %slice.96 = bf16[8,16,2048]{2,1,0:T(8,128)(2,1)S(1)} slice(bf16[8,48,2048]{2,1,0:T(8,128)(2,1)} %copy-done), slice={[0:8], [32:48], [0:2048]} | slice | bytes 1048576 | tf_op jit(solution)/shard_map/slice | solution.py:79
  47.0 5.6 %fusion.10 = f32[64,2304]{1,0:T(8,128)} fusion(bf16[64,2048]{1,0:T(8,128)(2,1)S(1)} %reshape.239, bf16[2048,1152]{1,0:T(8,128)(2,1)} %bitcast.65, bf16[2048,1152]{1,0:T(8,128)(2,1)} %bitcast.62), kind=kOutput, calls=%fused_computation.15 | convolution fusion | flops 623149056 | bytes 10289152 | tf_op jit(solution)/shard_map/dot_general | solution.py:89
  52.6 2.1 %reshape.248 = f32[16,1,4,2304]{3,2,0,1:T(4,128)} reshape(f32[64,2304]{1,0:T(8,128)} %fusion.10) | data formatting | bytes 1179648 | tf_op jit(solution)/shard_map/reshape | solution.py:92
  54.7 6.9 %fusion.6 = f32[16,16,1,2304]{3,1,0,2:T(8,128)S(1)} fusion(bf16[2048,1152]{1,0:T(8,128)(2,1)} %bitcast.66, bf16[2048,1152]{1,0:T(8,128)(2,1)} %bitcast.63, bf16[16,16,2048]{2,0,1:T(8,128)(2,1)S(1)} %bitcast.61), kind=kOutput, calls=%fused_computation.13 | convolution fusion | flops 2434793472 | bytes 12845056 | tf_op jit(solution)/shard_map/dot_general | solution.py:83
  61.6 1.3 %slice_bitcast_fusion.1 = (f32[16,16,1152]{2,1,0:T(8,128)S(1)}, f32[16,1152]{1,0:T(8,128)S(1)}, f32[16,16,1152]{2,1,0:T(8,128)}) fusion(f32[16,16,1,2304]{3,1,0,2:T(8,128)S(1)} %fusion.6), kind=kLoop, calls=%fused_computation.25 | loop fusion | flops 1161216 | bytes 4792320 | tf_op jit(solution)/shard_map/mul | solution.py:98
  62.9 1.2 %slice_bitcast_fusion.5 = (f32[16,4,1152]{2,1,0:T(4,128)S(1)}, f32[4,1152]{1,0:T(4,128)S(1)}, f32[16,4,1152]{2,1,0:T(4,128)S(1)}) fusion(f32[16,1,4,2304]{3,2,0,1:T(4,128)} %reshape.248), kind=kLoop, calls=%fused_computation.59 | loop fusion | flops 290304 | bytes 1198080 | tf_op jit(solution)/shard_map/mul | solution.py:98
  64.1 3.2 %add_reduce_fusion = (f32[16,4,1152]{2,0,1:T(8,128)}, f32[16,4,1152]{2,0,1:T(8,128)S(1)}) fusion(f32[16,4,1152]{2,1,0:T(4,128)S(1)} %get-tuple-element.17, f32[16,16,1152]{2,1,0:T(8,128)} %get-tuple-element.10, f32[16,4,1152]{2,1,0:T(4,128)S(1)} %get-tuple-element.15, f32[16,16,1152]{2,1,0:T(8,128)S(1)} %get-tuple-element.8), kind=kLoop, calls=%fused_computation.12 | loop fusion | flops 9289728 | bytes 3538944 | tf_op jit(solution)/shard_map/reduce_sum | solution.py:98
  67.6 1.1 %copy.48 = f32[16,4,1152]{2,1,0:T(4,128)S(1)} copy(f32[16,4,1152]{2,0,1:T(8,128)} %get-tuple-element.6) | data formatting | bytes 589824 | tf_op jit(solution)/shard_map/reduce_sum | solution.py:98
  68.8 1.0 %pad_maximum_fusion.9 = f32[8,22,1152]{2,1,0:T(8,128)} fusion(f32[8,4,1152]{2,1,0:T(4,128)S(1)} %broadcast_in_dim.37, f32[8,2,1152]{2,1,0:T(2,128)S(1)} %reshape_squeeze.3, f32[8,8,1152]{2,1,0:T(8,128)S(1)} %reshape.243, f32[8,8,1152]{2,1,0:T(8,128)S(1)} %reshape.242), kind=kLoop, calls=%fused_computation.34 | loop fusion | flops 608256 | bytes 1622016 | tf_op jit(solution)/shard_map/concatenate | solution.py:101
  69.8 6.1 %all-to-all-done.1 = bf16[128,4,2176]{2,1,0:T(4,128)(2,1)S(1)} async-done(((bf16[128,4,2176]{2,1,0:T(4,128)(2,1)}), bf16[128,4,2176]{2,1,0:T(4,128)(2,1)S(1)}, u32[]{:S(2)}, u32[]{:S(2)}) %all-to-all-start.1) | async-done | bytes 2228256 | tf_op jit(solution)/shard_map/all_to_all | solution.py:72
  75.9 3.6 %all-to-all-start.2 = ((f32[8,22,1152]{2,1,0:T(8,128)}), f32[8,22,1152]{2,1,0:T(8,128)S(1)}, u32[]{:S(2)}, u32[]{:S(2)}) async-start(f32[8,22,1152]{2,1,0:T(8,128)} %pad_maximum_fusion.9), calls=%async_computation.2 | async-start | bytes 1769472 | tf_op jit(solution)/shard_map/all_to_all | solution.py:112
  79.5 3.6 %copy.54 = bf16[128,4,2176]{0,1,2:T(4,128)(2,1)} copy(bf16[128,4,2176]{2,1,0:T(4,128)(2,1)S(1)} %all-to-all-done.1) | data formatting | bytes 4456448 | tf_op jit(solution)/shard_map/optimization_barrier | solution.py:110
  83.0 0.6 fusion.52
  84.1 2.5 %fusion.12 = f32[128,2048]{1,0:T(8,128)} fusion(bf16[128,4,2176]{2,0,1:T(8,128)(2,1)S(1)} %copy.55, bf16[128,2048]{1,0:T(8,128)(2,1)} %param.6, f32[128]{0:T(128)S(1)} %broadcast_add_fusion, f32[128,4]{0,1:T(4,128)S(1)} %fusion.52), kind=kOutput, calls=%fused_computation.19 | convolution fusion | flops 269287424 | bytes 3672576 | tf_op jit(solution)/shard_map/tps,psx->tx/dot_general | solution.py:147
  86.5 6.5 %all-to-all-done.2 = f32[8,22,1152]{2,1,0:T(8,128)S(1)} async-done(((f32[8,22,1152]{2,1,0:T(8,128)}), f32[8,22,1152]{2,1,0:T(8,128)S(1)}, u32[]{:S(2)}, u32[]{:S(2)}) %all-to-all-start.2) | async-done | bytes 811040 | tf_op jit(solution)/shard_map/all_to_all | solution.py:112
  93.3 3.7 %fusion.4 = f32[16,1152]{1,0:T(8,128)S(1)} fusion(bf16[16,2304]{1,0:T(8,128)(2,1)S(1)} %convert_element_type.112, bf16[2048,1152]{1,0:T(8,128)(2,1)} %bitcast.64, bf16[2048,1152]{1,0:T(8,128)(2,1)} %bitcast.67), kind=kOutput, calls=%fused_computation.10 | convolution fusion | flops 95551488 | bytes 9584640 | tf_op jit(solution)/shard_map/dot_general | solution.py:131
  97.1 0.6 reverse
  97.8 0.7 maximum_multiply_fusion
  (61 shorter events, 3.5 us)
Async XLA Ops:
  0.6 11.8 %copy-start.1 = (bf16[2,128,2048]{2,1,0:T(8,128)(2,1)S(1)}, bf16[2,128,2048]{2,1,0:T(8,128)(2,1)}, u32[]{:S(2)}) copy-start(bf16[2,128,2048]{2,1,0:T(8,128)(2,1)} %param.7) | copy-start | bytes 3145732
  2.0 11.3 %copy-start.5 = (s32[2]{0:T(128)S(1)}, s32[2]{0:T(128)}, u32[]{:S(2)}) copy-start(s32[2]{0:T(128)} %param.8) | copy-start | bytes 28
  2.0 15.6 %copy-start.7 = (s32[4]{0:T(128)S(1)}, s32[4]{0:T(128)}, u32[]{:S(2)}) copy-start(s32[4]{0:T(128)} %param.11) | copy-start | bytes 52
  2.0 15.7 %copy-start.4 = (s32[256,1]{0,1:T(1,128)S(1)}, s32[256,1]{0,1:T(1,128)}, u32[]{:S(2)}) copy-start(s32[256,1]{0,1:T(1,128)} %param.9) | copy-start | bytes 3076
  2.1 16.6 %copy-start.6 = (s32[256]{0:T(256)S(1)}, s32[256]{0:T(256)}, u32[]{:S(2)}) copy-start(s32[256]{0:T(256)} %param.10) | copy-start | bytes 3076
  4.5 28.0 %all-to-all-start = ((bf16[8,48,2048]{2,1,0:T(8,128)(2,1)}), bf16[8,48,2048]{2,1,0:T(8,128)(2,1)S(1)}, u32[]{:S(2)}, u32[]{:S(2)}) async-start(bf16[8,48,2048]{2,1,0:T(8,128)(2,1)} %pad_maximum_fusion.8), calls=%async_computation | async-start | bytes 3145728 | tf_op jit(solution)/shard_map/all_to_all | solution.py:48
  21.6 4.1 %copy-start.2 = (f32[64,1152]{1,0:T(8,128)S(1)}, f32[64,1152]{1,0:T(8,128)}, u32[]{:S(2)}) copy-start(f32[64,1152]{1,0:T(8,128)} %get-tuple-element.29) | copy-start | bytes 884740
  32.5 1.2 %copy-start = (bf16[8,48,2048]{2,1,0:T(8,128)(2,1)}, bf16[8,48,2048]{2,1,0:T(8,128)(2,1)S(1)}, u32[]{:S(2)}) copy-start(bf16[8,48,2048]{2,1,0:T(8,128)(2,1)S(1)} %all-to-all-done) | copy-start | bytes 4718596
  33.7 42.2 %all-to-all-start.1 = ((bf16[128,4,2176]{2,1,0:T(4,128)(2,1)}), bf16[128,4,2176]{2,1,0:T(4,128)(2,1)S(1)}, u32[]{:S(2)}, u32[]{:S(2)}) async-start(bf16[128,4,2176]{2,1,0:T(4,128)(2,1)} %copy.52), calls=%async_computation.1 | async-start | bytes 4456448 | tf_op jit(solution)/shard_map/all_to_all | solution.py:72
  47.0 7.7 %slice-start = ((bf16[8,48,2048]{2,1,0:T(8,128)(2,1)}), bf16[8,32,2048]{2,1,0:T(8,128)(2,1)S(1)}, s32[]{:S(2)}) async-start(bf16[8,48,2048]{2,1,0:T(8,128)(2,1)} %copy-done), calls=%async_computation.3 | async-start | bytes 2097152 | tf_op jit(solution)/shard_map/slice | solution.py:74
  75.9 17.1 %all-to-all-start.2 = ((f32[8,22,1152]{2,1,0:T(8,128)}), f32[8,22,1152]{2,1,0:T(8,128)S(1)}, u32[]{:S(2)}, u32[]{:S(2)}) async-start(f32[8,22,1152]{2,1,0:T(8,128)} %pad_maximum_fusion.9), calls=%async_computation.2 | async-start | bytes 1769472 | tf_op jit(solution)/shard_map/all_to_all | solution.py:112
  83.9 9.3 %copy-start.3 = (f32[1152]{0:T(1024)S(1)}, f32[1152]{0:T(1024)}, u32[]{:S(2)}) copy-start(f32[1152]{0:T(1024)} %select_select_fusion) | copy-start | bytes 13828

commit v12 on v10

--- a/solution.py
+++ b/solution.py
@@ -41,10 +41,11 @@
     weight = jnp.where((col == 0) | (col == half), 1.0, jnp.where(col < half, 2.0, 0.0))
 
     chunk = band_rows // stripes
-    frame_part = frames.reshape(count_frames, stripes, chunk, pixels).transpose(1, 0, 2, 3)
-    frame_part = frame_part.reshape(stripes, count_frames * chunk, pixels)
-    band_part = reference_img.reshape(stripes, chunk, pixels)
-    outbound = jnp.concatenate([frame_part, band_part], axis=1)
+    outbound = jnp.concatenate(
+        [frames[f].reshape(stripes, chunk, pixels) for f in range(count_frames)]
+        + [reference_img.reshape(stripes, chunk, pixels)],
+        axis=1,
+    )
     inbound = lax.all_to_all(outbound, "stripe", split_axis=0, concat_axis=0, tiled=True)
     num_devices = lax.axis_size("stripe") * lax.axis_size("frame")
     frame_rows = count_frames * band_rows

time: 100 us -> 97.6 us (0.976)
  other arithmetic: 23 us -> 21.3 us
    transpose x1 -> x0, local copies, waits for them, and re-layouts: 1.38 us -> none  [per_device(): frames.reshape(count_frames, stripes, chunk, pixels).transpose(1, 0, 2, 3)]
    concatenate x1, other arithmetic: 1.96 us -> 0.93 us  [shift_rows(): doubled = jnp.concatenate([frame_img, frame_img], axis=1)]
  transfers between devices with their start and end apart: 3 -> 3, of which waited for: 2 -> 3; matrix products, arithmetic and copies ran while one was open for 51% -> 50% of each run, Pallas kernels for 0% -> 0%
where the time goes in v12:
time: 97.6 us; the launch traced here: 96.4 us
  other arithmetic  21.3 us (22%)
  matrix products  20.8 us (21%)
  starting transfers between devices  20 us (20%)
  local copies, waits for them, and re-layouts  16.5 us (17%)
  waiting for transfers between devices  13 us (13%)
  between operations  4.83 us (5%)
    all_to_all x1, starting transfers between devices, per_device(): lax.all_to_all(packed, ('stripe', 'frame'), split_axis=0, concat_axis=0,...  10.9 us
    dot_general x1, matrix products, per_device(): jnp.dot(frame_rows_in, forward, preferred_element_type=jnp.float32)  6.9 us
    convert_element_type x1, other arithmetic, dft_table(): return (cos_t.astype(jnp.bfloat16), nsin_t.astype(jnp.bfloat16))  6.79 us
    all_to_all x1, waiting for transfers between devices, per_device(): lax.all_to_all(partial, 'stripe', split_axis=0, concat_axis=0, tiled=True)  6.53 us
    all_to_all x1, waiting for transfers between devices, per_device(): lax.all_to_all(packed, ('stripe', 'frame'), split_axis=0, concat_axis=0,...  6.12 us
    dot_general x1, matrix products, per_device(): jnp.dot(visited, forward, preferred_element_type=jnp.float32)  5.6 us
    all_to_all x1, starting transfers between devices, per_device(): lax.all_to_all(outbound, 'stripe', split_axis=0, concat_axis=0, tiled=True)  5.51 us
    dot_general x1, matrix products, per_device(): lax.dot_general(coherence.reshape(count_frames * steps, 2 * columns), for...  5.1 us
  transfers between devices with their start and end apart: 3, of which 3 were waited for; matrix products, arithmetic and copies ran while one was open for 50% of the time, Pallas kernels for 0%

profile of v12, /device:TPU:0, one launch (start us, length us, event | category | flops | bytes accessed | tf_op | source)
XLA Modules:
  0.0 96.4 jit_solution(304663871793629343)
XLA Ops:
  0.7 1.4 %slice_bitcast_fusion.7 = (bf16[128,2048]{1,0:T(8,128)(2,1)S(1)}, bf16[128,2048]{1,0:T(8,128)(2,1)S(1)}, bf16[1,128,2048]{2,1,0:T(8,128)(2,1)S(1)}, bf16[1,128,2048]{2,1,0:T(8,128)(2,1)S(1)}) fusion(bf16[2,128,2048]{2,1,0:T(8,128)(2,1)} %param.7), kind=kLoop, calls=%fused_computation.105 | loop fusion | bytes 3145728 | tf_op jit(solution)/shard_map/squeeze | solution.py:54
  2.1 2.4 %pad_maximum_fusion.7 = bf16[8,48,2048]{2,1,0:T(8,128)(2,1)} fusion(bf16[8,16,2048]{2,1,0:T(8,128)(2,1)} %bitcast.67, bf16[8,16,2048]{2,1,0:T(8,128)(2,1)S(1)} %bitcast.64, bf16[8,16,2048]{2,1,0:T(8,128)(2,1)S(1)} %bitcast.65), kind=kLoop, calls=%fused_computation.19 | loop fusion | flops 4718592 | bytes 3145728 | tf_op jit(solution)/shard_map/concatenate | solution.py:44
  4.5 5.5 %all-to-all-start = ((bf16[8,48,2048]{2,1,0:T(8,128)(2,1)}), bf16[8,48,2048]{2,1,0:T(8,128)(2,1)S(1)}, u32[]{:S(2)}, u32[]{:S(2)}) async-start(bf16[8,48,2048]{2,1,0:T(8,128)(2,1)} %pad_maximum_fusion.7), calls=%async_computation | async-start | bytes 3145728 | tf_op jit(solution)/shard_map/all_to_all | solution.py:49
  10.0 1.2 %fusion.29 = (f32[64,1152]{1,0:T(8,128)S(1)}, f32[64,1152]{1,0:T(8,128)S(1)}) fusion(), kind=kLoop, calls=%fused_computation.61 | loop fusion | flops 1032192 | bytes 589824 | tf_op jit(solution)/shard_map/sin | solution.py:19
  11.2 0.6 fusion.52
  15.6 0.6 select_select_fusion
  17.4 0.9 fusion.16
  18.4 0.7 convolution_convert_fusion.1
  19.5 3.1 %copy.43 = bf16[128,4,2176]{2,1,0:T(4,128)(2,1)} copy(bf16[128,4,2176]{2,0,1:T(8,128)(2,1)S(1)} %pad_maximum_fusion.4) | data formatting | bytes 4456448 | tf_op jit(solution)/shard_map/concatenate | solution.py:72
  22.6 0.7 fusion.39
  23.2 6.8 %subtract_convert_fusion = (bf16[32,64,1152]{2,1,0:T(8,128)(2,1)}, bf16[32,64,1152]{2,1,0:T(8,128)(2,1)}) fusion(f32[64,1152]{1,0:T(8,128)S(1)} %get-tuple-element.26, f32[32,1152]{1,0:T(8,128)S(1)} %get-tuple-element.25, f32[64,1152]{1,0:T(8,128)S(1)} %get-tuple-element.27, f32[32,1152]{1,0:T(8,128)S(1)} %get-tuple-element.24), kind=kLoop, calls=%fused_computation.5 | loop fusion | flops 21233664 | bytes 10321920 | tf_op jit(solution)/shard_map/convert_element_type | solution.py:22
  30.0 0.4 all-to-all-done
  30.4 1.2 %copy-done = bf16[8,48,2048]{2,1,0:T(8,128)(2,1)} copy-done((bf16[8,48,2048]{2,1,0:T(8,128)(2,1)}, bf16[8,48,2048]{2,1,0:T(8,128)(2,1)S(1)}, u32[]{:S(2)}) %copy-start) | copy-done | bytes 1572888
  31.6 10.9 %all-to-all-start.1 = ((bf16[128,4,2176]{2,1,0:T(4,128)(2,1)}), bf16[128,4,2176]{2,1,0:T(4,128)(2,1)S(1)}, u32[]{:S(2)}, u32[]{:S(2)}) async-start(bf16[128,4,2176]{2,1,0:T(4,128)(2,1)} %copy.43), calls=%async_computation.1 | async-start | bytes 4456448 | tf_op jit(solution)/shard_map/all_to_all | solution.py:73
  42.5 1.1 %slice.78 = bf16[8,16,2048]{2,1,0:T(8,128)(2,1)S(1)} slice(bf16[8,48,2048]{2,1,0:T(8,128)(2,1)} %copy-done), slice={[0:8], [32:48], [0:2048]} | slice | bytes 1048576 | tf_op jit(solution)/shard_map/slice | solution.py:80
  43.6 0.6 gather_fusion
  44.4 5.6 %fusion.5 = f32[64,2304]{1,0:T(8,128)} fusion(bf16[64,2048]{1,0:T(8,128)(2,1)S(1)} %reshape.235, bf16[2048,1152]{1,0:T(8,128)(2,1)} %bitcast.61, bf16[2048,1152]{1,0:T(8,128)(2,1)} %bitcast.58), kind=kOutput, calls=%fused_computation.10 | convolution fusion | flops 623149056 | bytes 10289152 | tf_op jit(solution)/shard_map/dot_general | solution.py:90
  50.0 2.1 %reshape.243 = f32[16,1,4,2304]{3,2,0,1:T(4,128)} reshape(f32[64,2304]{1,0:T(8,128)} %fusion.5) | data formatting | bytes 1179648 | tf_op jit(solution)/shard_map/reshape | solution.py:93
  52.1 6.9 %fusion.2 = f32[16,16,1,2304]{3,1,0,2:T(8,128)S(1)} fusion(bf16[2048,1152]{1,0:T(8,128)(2,1)} %bitcast.62, bf16[2048,1152]{1,0:T(8,128)(2,1)} %bitcast.59, bf16[16,16,2048]{2,0,1:T(8,128)(2,1)S(1)} %bitcast.57), kind=kOutput, calls=%fused_computation.8 | convolution fusion | flops 2434793472 | bytes 12845056 | tf_op jit(solution)/shard_map/dot_general | solution.py:84
  59.0 1.3 %slice_bitcast_fusion.1 = (f32[16,16,1152]{2,1,0:T(8,128)S(1)}, f32[16,1152]{1,0:T(8,128)S(1)}, f32[16,16,1152]{2,1,0:T(8,128)}) fusion(f32[16,16,1,2304]{3,1,0,2:T(8,128)S(1)} %fusion.2), kind=kLoop, calls=%fused_computation.22 | loop fusion | flops 1161216 | bytes 4792320 | tf_op jit(solution)/shard_map/mul | solution.py:99
  60.4 1.2 %slice_bitcast_fusion.3 = (f32[16,4,1152]{2,1,0:T(4,128)S(1)}, f32[4,1152]{1,0:T(4,128)S(1)}, f32[16,4,1152]{2,1,0:T(4,128)S(1)}) fusion(f32[16,1,4,2304]{3,2,0,1:T(4,128)} %reshape.243), kind=kLoop, calls=%fused_computation.54 | loop fusion | flops 290304 | bytes 1198080 | tf_op jit(solution)/shard_map/mul | solution.py:99
  61.6 3.2 %add_reduce_fusion = (f32[16,4,1152]{2,0,1:T(8,128)}, f32[16,4,1152]{2,0,1:T(8,128)S(1)}) fusion(f32[16,4,1152]{2,1,0:T(4,128)S(1)} %get-tuple-element.19, f32[16,16,1152]{2,1,0:T(8,128)} %get-tuple-element.10, f32[16,4,1152]{2,1,0:T(4,128)S(1)} %get-tuple-element.17, f32[16,16,1152]{2,1,0:T(8,128)S(1)} %get-tuple-element.8), kind=kLoop, calls=%fused_computation.7 | loop fusion | flops 9289728 | bytes 3538944 | tf_op jit(solution)/shard_map/reduce_sum | solution.py:99
  65.0 1.1 %copy.39 = f32[16,4,1152]{2,1,0:T(4,128)S(1)} copy(f32[16,4,1152]{2,0,1:T(8,128)} %get-tuple-element.6) | data formatting | bytes 589824 | tf_op jit(solution)/shard_map/reduce_sum | solution.py:99
  66.2 1.0 %pad_maximum_fusion.8 = f32[8,22,1152]{2,1,0:T(8,128)} fusion(f32[8,4,1152]{2,1,0:T(4,128)S(1)} %broadcast_in_dim.37, f32[8,2,1152]{2,1,0:T(2,128)S(1)} %reshape_squeeze.11, f32[8,8,1152]{2,1,0:T(8,128)S(1)} %reshape.239, f32[8,8,1152]{2,1,0:T(8,128)S(1)} %reshape.238), kind=kLoop, calls=%fused_computation.31 | loop fusion | flops 608256 | bytes 1622016 | tf_op jit(solution)/shard_map/concatenate | solution.py:102
  67.2 6.1 %all-to-all-done.1 = bf16[128,4,2176]{2,1,0:T(4,128)(2,1)S(1)} async-done(((bf16[128,4,2176]{2,1,0:T(4,128)(2,1)}), bf16[128,4,2176]{2,1,0:T(4,128)(2,1)S(1)}, u32[]{:S(2)}, u32[]{:S(2)}) %all-to-all-start.1) | async-done | bytes 2228256 | tf_op jit(solution)/shard_map/all_to_all | solution.py:73
  73.4 3.6 %all-to-all-start.2 = ((f32[8,22,1152]{2,1,0:T(8,128)}), f32[8,22,1152]{2,1,0:T(8,128)S(1)}, u32[]{:S(2)}, u32[]{:S(2)}) async-start(f32[8,22,1152]{2,1,0:T(8,128)} %pad_maximum_fusion.8), calls=%async_computation.2 | async-start | bytes 1769472 | tf_op jit(solution)/shard_map/all_to_all | solution.py:113
  76.9 3.6 %copy.45 = bf16[128,4,2176]{0,1,2:T(4,128)(2,1)} copy(bf16[128,4,2176]{2,1,0:T(4,128)(2,1)S(1)} %all-to-all-done.1) | data formatting | bytes 4456448 | tf_op jit(solution)/shard_map/optimization_barrier | solution.py:111
  80.5 0.6 fusion.47
  81.5 2.5 %fusion.8 = f32[128,2048]{1,0:T(8,128)} fusion(bf16[128,4,2176]{2,0,1:T(8,128)(2,1)S(1)} %copy.46, bf16[128,2048]{1,0:T(8,128)(2,1)} %param.6, f32[128]{0:T(128)S(1)} %broadcast_add_fusion, f32[128,4]{0,1:T(4,128)S(1)} %fusion.47), kind=kOutput, calls=%fused_computation.15 | convolution fusion | flops 269287424 | bytes 3672576 | tf_op jit(solution)/shard_map/tps,psx->tx/dot_general | solution.py:136
  84.0 6.5 %all-to-all-done.2 = f32[8,22,1152]{2,1,0:T(8,128)S(1)} async-done(((f32[8,22,1152]{2,1,0:T(8,128)}), f32[8,22,1152]{2,1,0:T(8,128)S(1)}, u32[]{:S(2)}, u32[]{:S(2)}) %all-to-all-start.2) | async-done | bytes 811040 | tf_op jit(solution)/shard_map/all_to_all | solution.py:113
  90.7 5.1 %fusion.9 = f32[8,2048]{1,0:T(8,128)S(1)} fusion(bf16[2048,1152]{1,0:T(8,128)(2,1)} %bitcast.63, bf16[2048,1152]{1,0:T(8,128)(2,1)} %bitcast.60, bf16[8,1152]{1,0:T(8,128)(2,1)S(1)} %get-tuple-element.21, bf16[8,1152]{1,0:T(8,128)(2,1)S(1)} %get-tuple-element.20), kind=kOutput, calls=%fused_computation.17 | convolution fusion | flops 94461952 | bytes 9539584 | tf_op jit(solution)/shard_map/dot_general | solution.py:125
  95.8 0.7 reshape.241
  (46 shorter events, 2.6 us)
Async XLA Ops:
  0.6 10.5 %copy-start.3 = (s32[2]{0:T(128)S(1)}, s32[2]{0:T(128)}, u32[]{:S(2)}) copy-start(s32[2]{0:T(128)} %param.8) | copy-start | bytes 28
  0.6 15.6 %copy-start.5 = (s32[4]{0:T(128)S(1)}, s32[4]{0:T(128)}, u32[]{:S(2)}) copy-start(s32[4]{0:T(128)} %param.11) | copy-start | bytes 52
  0.7 15.6 %copy-start.2 = (s32[256,1]{0,1:T(1,128)S(1)}, s32[256,1]{0,1:T(1,128)}, u32[]{:S(2)}) copy-start(s32[256,1]{0,1:T(1,128)} %param.9) | copy-start | bytes 3076
  2.1 15.1 %copy-start.4 = (s32[256]{0:T(256)S(1)}, s32[256]{0:T(256)}, u32[]{:S(2)}) copy-start(s32[256]{0:T(256)} %param.10) | copy-start | bytes 3076
  4.5 25.9 %all-to-all-start = ((bf16[8,48,2048]{2,1,0:T(8,128)(2,1)}), bf16[8,48,2048]{2,1,0:T(8,128)(2,1)S(1)}, u32[]{:S(2)}, u32[]{:S(2)}) async-start(bf16[8,48,2048]{2,1,0:T(8,128)(2,1)} %pad_maximum_fusion.7), calls=%async_computation | async-start | bytes 3145728 | tf_op jit(solution)/shard_map/all_to_all | solution.py:49
  30.4 1.2 %copy-start = (bf16[8,48,2048]{2,1,0:T(8,128)(2,1)}, bf16[8,48,2048]{2,1,0:T(8,128)(2,1)S(1)}, u32[]{:S(2)}) copy-start(bf16[8,48,2048]{2,1,0:T(8,128)(2,1)S(1)} %all-to-all-done) | copy-start | bytes 4718596
  31.6 41.8 %all-to-all-start.1 = ((bf16[128,4,2176]{2,1,0:T(4,128)(2,1)}), bf16[128,4,2176]{2,1,0:T(4,128)(2,1)S(1)}, u32[]{:S(2)}, u32[]{:S(2)}) async-start(bf16[128,4,2176]{2,1,0:T(4,128)(2,1)} %copy.43), calls=%async_computation.1 | async-start | bytes 4456448 | tf_op jit(solution)/shard_map/all_to_all | solution.py:73
  44.4 7.7 %slice-start = ((bf16[8,48,2048]{2,1,0:T(8,128)(2,1)}), bf16[8,32,2048]{2,1,0:T(8,128)(2,1)S(1)}, s32[]{:S(2)}) async-start(bf16[8,48,2048]{2,1,0:T(8,128)(2,1)} %copy-done), calls=%async_computation.3 | async-start | bytes 2097152 | tf_op jit(solution)/shard_map/slice | solution.py:75
  73.4 17.1 %all-to-all-start.2 = ((f32[8,22,1152]{2,1,0:T(8,128)}), f32[8,22,1152]{2,1,0:T(8,128)S(1)}, u32[]{:S(2)}, u32[]{:S(2)}) async-start(f32[8,22,1152]{2,1,0:T(8,128)} %pad_maximum_fusion.8), calls=%async_computation.2 | async-start | bytes 1769472 | tf_op jit(solution)/shard_map/all_to_all | solution.py:113
  81.3 9.3 %copy-start.1 = (f32[1152]{0:T(1024)S(1)}, f32[1152]{0:T(1024)}, u32[]{:S(2)}) copy-start(f32[1152]{0:T(1024)} %select_select_fusion) | copy-start | bytes 13828

commit v13 on v12

--- a/solution.py
+++ b/solution.py
@@ -109,9 +109,10 @@
         axis=1,
     )
     partial, received = lax.optimization_barrier((partial, received))
-    total = jnp.sum(
-        lax.all_to_all(partial, "stripe", split_axis=0, concat_axis=0, tiled=True), axis=0
+    shares = lax.all_to_all(
+        partial.astype(jnp.bfloat16), "stripe", split_axis=0, concat_axis=0, tiled=True
     )
+    total = jnp.sum(shares.astype(jnp.float32), axis=0)
     pairs = count_frames * steps
     cross_re = total[:pairs].reshape(count_frames, steps, columns)
     cross_im = total[pairs : 2 * pairs].reshape(count_frames, steps, columns)

time: 97.6 us -> 92.9 us (0.952)
  waiting for transfers between devices: 13 us -> 9.12 us
  matrix products: 20.8 us -> 19.8 us
    all_to_all x1, waiting for transfers between devices: 6.53 us -> 3.19 us  [per_device(): lax.all_to_all(partial.astype(jnp.bfloat16), 'stripe', split_axis=0, conc...]
    dot_general x1, matrix products: 2.48 us -> 1.44 us  [per_device(): jnp.einsum('tps,psx->tx', hits.astype(jnp.bfloat16), incoming, preferred_...]
    reduce_sum x1, local copies, waits for them, and re-layouts: 1.08 us -> 0.06 us  [per_device(): cross_re = jnp.sum(spec_re * band_re + spec_im * band_im, axis=0)]
  transfers between devices with their start and end apart: 3 -> 3, of which waited for: 3 -> 3; matrix products, arithmetic and copies ran while one was open for 50% -> 51% of each run, Pallas kernels for 0% -> 0%
where the time goes in v13:
time: 92.9 us; the launch traced here: 92.2 us
  other arithmetic  22 us (24%)
  starting transfers between devices  19.9 us (21%)
  matrix products  19.8 us (21%)
  local copies, waits for them, and re-layouts  16.6 us (18%)
  waiting for transfers between devices  9.12 us (10%)
  between operations  4.84 us (5%)
    all_to_all x1, starting transfers between devices, per_device(): lax.all_to_all(packed, ('stripe', 'frame'), split_axis=0, concat_axis=0,...  10.9 us
    dot_general x1, matrix products, per_device(): jnp.dot(frame_rows_in, forward, preferred_element_type=jnp.float32)  6.9 us
    convert_element_type x1, other arithmetic, dft_table(): return (cos_t.astype(jnp.bfloat16), nsin_t.astype(jnp.bfloat16))  6.79 us
    dot_general x1, matrix products, per_device(): jnp.dot(visited, forward, preferred_element_type=jnp.float32)  5.6 us
    all_to_all x1, waiting for transfers between devices, per_device(): lax.all_to_all(packed, ('stripe', 'frame'), split_axis=0, concat_axis=0,...  5.54 us
    all_to_all x1, starting transfers between devices, per_device(): lax.all_to_all(outbound, 'stripe', split_axis=0, concat_axis=0, tiled=True)  5.51 us
    dot_general x1, matrix products, per_device(): lax.dot_general(coherence.reshape(count_frames * steps, 2 * columns), for...  5.1 us
    optimization_barrier x2, local copies, waits for them, and re-layouts, per_device(): partial, received = lax.optimization_barrier((partial, received))  3.78 us
  transfers between devices with their start and end apart: 3, of which 3 were waited for; matrix products, arithmetic and copies ran while one was open for 51% of the time, Pallas kernels for 0%

profile of v13, /device:TPU:0, one launch (start us, length us, event | category | flops | bytes accessed | tf_op | source)
XLA Modules:
  0.0 92.2 jit_solution(12465499991500729394)
XLA Ops:
  0.7 1.4 %slice_bitcast_fusion.7 = (bf16[128,2048]{1,0:T(8,128)(2,1)S(1)}, bf16[128,2048]{1,0:T(8,128)(2,1)S(1)}, bf16[1,128,2048]{2,1,0:T(8,128)(2,1)S(1)}, bf16[1,128,2048]{2,1,0:T(8,128)(2,1)S(1)}) fusion(bf16[2,128,2048]{2,1,0:T(8,128)(2,1)} %param.7), kind=kLoop, calls=%fused_computation.106 | loop fusion | bytes 3145728 | tf_op jit(solution)/shard_map/squeeze | solution.py:54
  2.1 2.4 %pad_maximum_fusion.7 = bf16[8,48,2048]{2,1,0:T(8,128)(2,1)} fusion(bf16[8,16,2048]{2,1,0:T(8,128)(2,1)} %bitcast.67, bf16[8,16,2048]{2,1,0:T(8,128)(2,1)S(1)} %bitcast.64, bf16[8,16,2048]{2,1,0:T(8,128)(2,1)S(1)} %bitcast.65), kind=kLoop, calls=%fused_computation.19 | loop fusion | flops 4718592 | bytes 3145728 | tf_op jit(solution)/shard_map/concatenate | solution.py:44
  4.5 5.5 %all-to-all-start = ((bf16[8,48,2048]{2,1,0:T(8,128)(2,1)}), bf16[8,48,2048]{2,1,0:T(8,128)(2,1)S(1)}, u32[]{:S(2)}, u32[]{:S(2)}) async-start(bf16[8,48,2048]{2,1,0:T(8,128)(2,1)} %pad_maximum_fusion.7), calls=%async_computation | async-start | bytes 3145728 | tf_op jit(solution)/shard_map/all_to_all | solution.py:49
  10.0 1.2 %fusion.29 = (f32[64,1152]{1,0:T(8,128)S(1)}, f32[64,1152]{1,0:T(8,128)S(1)}) fusion(), kind=kLoop, calls=%fused_computation.62 | loop fusion | flops 1032192 | bytes 589824 | tf_op jit(solution)/shard_map/sin | solution.py:19
  11.2 0.6 fusion.52
  15.6 0.6 select_select_fusion
  17.4 0.9 fusion.16
  18.4 0.7 convolution_convert_fusion.1
  19.5 3.1 %copy.55 = bf16[128,4,2176]{2,1,0:T(4,128)(2,1)} copy(bf16[128,4,2176]{2,0,1:T(8,128)(2,1)S(1)} %pad_maximum_fusion.4) | data formatting | bytes 4456448 | tf_op jit(solution)/shard_map/concatenate | solution.py:72
  22.5 0.7 fusion.39
  23.2 6.8 %subtract_convert_fusion = (bf16[32,64,1152]{2,1,0:T(8,128)(2,1)}, bf16[32,64,1152]{2,1,0:T(8,128)(2,1)}) fusion(f32[64,1152]{1,0:T(8,128)S(1)} %get-tuple-element.26, f32[32,1152]{1,0:T(8,128)S(1)} %get-tuple-element.25, f32[64,1152]{1,0:T(8,128)S(1)} %get-tuple-element.27, f32[32,1152]{1,0:T(8,128)S(1)} %get-tuple-element.24), kind=kLoop, calls=%fused_computation.5 | loop fusion | flops 21233664 | bytes 10321920 | tf_op jit(solution)/shard_map/convert_element_type | solution.py:22
  30.4 1.2 %copy-done = bf16[8,48,2048]{2,1,0:T(8,128)(2,1)} copy-done((bf16[8,48,2048]{2,1,0:T(8,128)(2,1)}, bf16[8,48,2048]{2,1,0:T(8,128)(2,1)S(1)}, u32[]{:S(2)}) %copy-start) | copy-done | bytes 1572888
  31.6 10.9 %all-to-all-start.1 = ((bf16[128,4,2176]{2,1,0:T(4,128)(2,1)}), bf16[128,4,2176]{2,1,0:T(4,128)(2,1)S(1)}, u32[]{:S(2)}, u32[]{:S(2)}) async-start(bf16[128,4,2176]{2,1,0:T(4,128)(2,1)} %copy.55), calls=%async_computation.1 | async-start | bytes 4456448 | tf_op jit(solution)/shard_map/all_to_all | solution.py:73
  42.5 1.1 %slice.78 = bf16[8,16,2048]{2,1,0:T(8,128)(2,1)S(1)} slice(bf16[8,48,2048]{2,1,0:T(8,128)(2,1)} %copy-done), slice={[0:8], [32:48], [0:2048]} | slice | bytes 1048576 | tf_op jit(solution)/shard_map/slice | solution.py:80
  43.6 0.6 gather_fusion
  44.4 5.6 %fusion.5 = f32[64,2304]{1,0:T(8,128)} fusion(bf16[64,2048]{1,0:T(8,128)(2,1)S(1)} %reshape.235, bf16[2048,1152]{1,0:T(8,128)(2,1)} %bitcast.61, bf16[2048,1152]{1,0:T(8,128)(2,1)} %bitcast.58), kind=kOutput, calls=%fused_computation.10 | convolution fusion | flops 623149056 | bytes 10289152 | tf_op jit(solution)/shard_map/dot_general | solution.py:90
  50.0 2.1 %reshape.243 = f32[16,1,4,2304]{3,2,0,1:T(4,128)} reshape(f32[64,2304]{1,0:T(8,128)} %fusion.5) | data formatting | bytes 1179648 | tf_op jit(solution)/shard_map/reshape | solution.py:93
  52.1 6.9 %fusion.2 = f32[16,16,1,2304]{3,1,0,2:T(8,128)S(1)} fusion(bf16[2048,1152]{1,0:T(8,128)(2,1)} %bitcast.62, bf16[2048,1152]{1,0:T(8,128)(2,1)} %bitcast.59, bf16[16,16,2048]{2,0,1:T(8,128)(2,1)S(1)} %bitcast.57), kind=kOutput, calls=%fused_computation.8 | convolution fusion | flops 2434793472 | bytes 12845056 | tf_op jit(solution)/shard_map/dot_general | solution.py:84
  59.0 1.3 %slice_bitcast_fusion.1 = (f32[16,16,1152]{2,1,0:T(8,128)S(1)}, bf16[16,1152]{1,0:T(8,128)(2,1)S(1)}, f32[16,16,1152]{2,1,0:T(8,128)}) fusion(f32[16,16,1,2304]{3,1,0,2:T(8,128)S(1)} %fusion.2), kind=kLoop, calls=%fused_computation.22 | loop fusion | flops 1161216 | bytes 4755456 | tf_op jit(solution)/shard_map/mul | solution.py:99
  60.3 0.6 reshape_squeeze.11
  60.9 1.8 %slice_bitcast_fusion.3 = (f32[16,4,1152]{2,1,0:T(4,128)S(1)}, bf16[4,1152]{1,0:T(4,128)(2,1)}, f32[16,4,1152]{2,1,0:T(4,128)S(1)}) fusion(f32[16,1,4,2304]{3,2,0,1:T(4,128)} %reshape.243), kind=kLoop, calls=%fused_computation.55 | loop fusion | flops 290304 | bytes 1188864 | tf_op jit(solution)/shard_map/mul | solution.py:99
  62.7 2.5 %add_reduce_fusion = (bf16[16,4,1152]{2,0,1:T(8,128)(2,1)S(1)}, bf16[16,4,1152]{2,0,1:T(8,128)(2,1)S(1)}) fusion(f32[16,4,1152]{2,1,0:T(4,128)S(1)} %get-tuple-element.19, f32[16,16,1152]{2,1,0:T(8,128)} %get-tuple-element.10, f32[16,4,1152]{2,1,0:T(4,128)S(1)} %get-tuple-element.17, f32[16,16,1152]{2,1,0:T(8,128)S(1)} %get-tuple-element.8), kind=kLoop, calls=%fused_computation.7 | loop fusion | flops 9289728 | bytes 3244032 | tf_op jit(solution)/shard_map/reduce_sum | solution.py:99
  65.4 0.7 broadcast_in_dim.37
  66.2 1.6 %pad_maximum_fusion.8 = bf16[8,22,1152]{2,1,0:T(8,128)(2,1)} fusion(bf16[8,4,1152]{2,1,0:T(4,128)(2,1)S(1)} %broadcast_in_dim.37, bf16[8,2,1152]{2,1,0:T(2,128)(2,1)} %reshape_squeeze.11, bf16[8,8,1152]{2,1,0:T(8,128)(2,1)S(1)} %reshape.239, bf16[8,8,1152]{2,1,0:T(8,128)(2,1)S(1)} %reshape.238), kind=kLoop, calls=%fused_computation.31 | loop fusion | flops 1622016 | bytes 811008 | tf_op jit(solution)/shard_map/concatenate | solution.py:102
  67.8 5.5 %all-to-all-done.1 = bf16[128,4,2176]{2,1,0:T(4,128)(2,1)S(1)} async-done(((bf16[128,4,2176]{2,1,0:T(4,128)(2,1)}), bf16[128,4,2176]{2,1,0:T(4,128)(2,1)S(1)}, u32[]{:S(2)}, u32[]{:S(2)}) %all-to-all-start.1) | async-done | bytes 2228256 | tf_op jit(solution)/shard_map/all_to_all | solution.py:73
  73.3 3.5 %all-to-all-start.2 = ((bf16[8,22,1152]{2,1,0:T(8,128)(2,1)}), bf16[8,22,1152]{2,1,0:T(8,128)(2,1)S(1)}, u32[]{:S(2)}, u32[]{:S(2)}) async-start(bf16[8,22,1152]{2,1,0:T(8,128)(2,1)} %pad_maximum_fusion.8), calls=%async_computation.2 | async-start | bytes 884736 | tf_op jit(solution)/shard_map/all_to_all | solution.py:112
  76.8 3.6 %copy.57 = bf16[128,4,2176]{0,1,2:T(4,128)(2,1)} copy(bf16[128,4,2176]{2,1,0:T(4,128)(2,1)S(1)} %all-to-all-done.1) | data formatting | bytes 4456448 | tf_op jit(solution)/shard_map/optimization_barrier | solution.py:111
  80.4 0.6 fusion.47
  81.4 1.4 %fusion.8 = f32[128,2048]{1,0:T(8,128)} fusion(bf16[128,4,2176]{2,0,1:T(8,128)(2,1)S(1)} %copy.58, bf16[128,2048]{1,0:T(8,128)(2,1)S(1)} %copy-done.1, f32[128]{0:T(128)S(1)} %broadcast_add_fusion, f32[128,4]{0,1:T(4,128)S(1)} %fusion.47), kind=kOutput, calls=%fused_computation.15 | convolution fusion | flops 269287424 | bytes 3672576 | tf_op jit(solution)/shard_map/tps,psx->tx/dot_general | solution.py:137
  82.8 3.2 %all-to-all-done.2 = bf16[8,22,1152]{2,1,0:T(8,128)(2,1)S(1)} async-done(((bf16[8,22,1152]{2,1,0:T(8,128)(2,1)}), bf16[8,22,1152]{2,1,0:T(8,128)(2,1)S(1)}, u32[]{:S(2)}, u32[]{:S(2)}) %all-to-all-start.2) | async-done | bytes 405536 | tf_op jit(solution)/shard_map/all_to_all | solution.py:112
  86.4 5.1 %fusion.9 = f32[8,2048]{1,0:T(8,128)S(1)} fusion(bf16[2048,1152]{1,0:T(8,128)(2,1)} %bitcast.63, bf16[2048,1152]{1,0:T(8,128)(2,1)} %bitcast.60, bf16[8,1152]{1,0:T(8,128)(2,1)S(1)} %get-tuple-element.21, bf16[8,1152]{1,0:T(8,128)(2,1)S(1)} %get-tuple-element.20), kind=kOutput, calls=%fused_computation.17 | convolution fusion | flops 94461952 | bytes 9539584 | tf_op jit(solution)/shard_map/dot_general | solution.py:126
  91.5 0.7 reshape.241
  (48 shorter events, 3.1 us)
Async XLA Ops:
  0.6 10.5 %copy-start.4 = (s32[2]{0:T(128)S(1)}, s32[2]{0:T(128)}, u32[]{:S(2)}) copy-start(s32[2]{0:T(128)} %param.8) | copy-start | bytes 28
  0.6 15.6 %copy-start.6 = (s32[4]{0:T(128)S(1)}, s32[4]{0:T(128)}, u32[]{:S(2)}) copy-start(s32[4]{0:T(128)} %param.11) | copy-start | bytes 52
  0.7 15.6 %copy-start.3 = (s32[256,1]{0,1:T(1,128)S(1)}, s32[256,1]{0,1:T(1,128)}, u32[]{:S(2)}) copy-start(s32[256,1]{0,1:T(1,128)} %param.9) | copy-start | bytes 3076
  2.1 15.1 %copy-start.5 = (s32[256]{0:T(256)S(1)}, s32[256]{0:T(256)}, u32[]{:S(2)}) copy-start(s32[256]{0:T(256)} %param.10) | copy-start | bytes 3076
  4.5 25.9 %all-to-all-start = ((bf16[8,48,2048]{2,1,0:T(8,128)(2,1)}), bf16[8,48,2048]{2,1,0:T(8,128)(2,1)S(1)}, u32[]{:S(2)}, u32[]{:S(2)}) async-start(bf16[8,48,2048]{2,1,0:T(8,128)(2,1)} %pad_maximum_fusion.7), calls=%async_computation | async-start | bytes 3145728 | tf_op jit(solution)/shard_map/all_to_all | solution.py:49
  30.4 1.2 %copy-start = (bf16[8,48,2048]{2,1,0:T(8,128)(2,1)}, bf16[8,48,2048]{2,1,0:T(8,128)(2,1)S(1)}, u32[]{:S(2)}) copy-start(bf16[8,48,2048]{2,1,0:T(8,128)(2,1)S(1)} %all-to-all-done) | copy-start | bytes 4718596
  31.6 41.8 %all-to-all-start.1 = ((bf16[128,4,2176]{2,1,0:T(4,128)(2,1)}), bf16[128,4,2176]{2,1,0:T(4,128)(2,1)S(1)}, u32[]{:S(2)}, u32[]{:S(2)}) async-start(bf16[128,4,2176]{2,1,0:T(4,128)(2,1)} %copy.55), calls=%async_computation.1 | async-start | bytes 4456448 | tf_op jit(solution)/shard_map/all_to_all | solution.py:73
  44.4 7.7 %slice-start = ((bf16[8,48,2048]{2,1,0:T(8,128)(2,1)}), bf16[8,32,2048]{2,1,0:T(8,128)(2,1)S(1)}, s32[]{:S(2)}) async-start(bf16[8,48,2048]{2,1,0:T(8,128)(2,1)} %copy-done), calls=%async_computation.3 | async-start | bytes 2097152 | tf_op jit(solution)/shard_map/slice | solution.py:75
  67.8 13.6 %copy-start.1 = (bf16[128,2048]{1,0:T(8,128)(2,1)S(1)}, bf16[128,2048]{1,0:T(8,128)(2,1)}, u32[]{:S(2)}) copy-start(bf16[128,2048]{1,0:T(8,128)(2,1)} %param.6) | copy-start | bytes 1572868
  73.3 12.7 %all-to-all-start.2 = ((bf16[8,22,1152]{2,1,0:T(8,128)(2,1)}), bf16[8,22,1152]{2,1,0:T(8,128)(2,1)S(1)}, u32[]{:S(2)}, u32[]{:S(2)}) async-start(bf16[8,22,1152]{2,1,0:T(8,128)(2,1)} %pad_maximum_fusion.8), calls=%async_computation.2 | async-start | bytes 884736 | tf_op jit(solution)/shard_map/all_to_all | solution.py:112
  81.4 5.0 %copy-start.2 = (f32[1152]{0:T(1024)S(1)}, f32[1152]{0:T(1024)}, u32[]{:S(2)}) copy-start(f32[1152]{0:T(1024)} %select_select_fusion) | copy-start | bytes 13828

commit v14 on v13

--- a/solution.py
+++ b/solution.py
@@ -109,10 +109,21 @@
         axis=1,
     )
     partial, received = lax.optimization_barrier((partial, received))
+    rows = partial.shape[1]
+    nyquist = jnp.pad(partial[:, :, half], ((0, 0), (0, half - rows)))[:, None, :]
+    outgoing_sums = jnp.concatenate([partial[:, :, :half], nyquist], axis=1)
     shares = lax.all_to_all(
-        partial.astype(jnp.bfloat16), "stripe", split_axis=0, concat_axis=0, tiled=True
+        outgoing_sums.astype(jnp.bfloat16), "stripe", split_axis=0, concat_axis=0, tiled=True
     )
-    total = jnp.sum(shares.astype(jnp.float32), axis=0)
+    summed = jnp.sum(shares.astype(jnp.float32), axis=0)
+    total = jnp.concatenate(
+        [
+            summed[:rows],
+            summed[rows, :rows, None],
+            jnp.zeros((rows, columns - half - 1), jnp.float32),
+        ],
+        axis=1,
+    )
     pairs = count_frames * steps
     cross_re = total[:pairs].reshape(count_frames, steps, columns)
     cross_im = total[pairs : 2 * pairs].reshape(count_frames, steps, columns)

time: 92.9 us -> 98.6 us (1.061)
  waiting for transfers between devices: 9.12 us -> 11.6 us
  local copies, waits for them, and re-layouts: 16.6 us -> 18.3 us
  matrix products: 19.8 us -> 21.4 us
    all_to_all x1, waiting for transfers between devices: 3.19 us -> 4.9 us  [per_device(): lax.all_to_all(outgoing_sums.astype(jnp.bfloat16), 'stripe', split_axis=0...]
    dot_general x1, matrix products: 1.44 us -> 3.1 us  [per_device(): jnp.einsum('tps,psx->tx', hits.astype(jnp.bfloat16), incoming, preferred_...]
    optimization_barrier x2, local copies, waits for them, and re-layouts: 3.78 us -> 5.1 us  [per_device(): partial, received = lax.optimization_barrier((partial, received))]
  transfers between devices with their start and end apart: 3 -> 3, of which waited for: 3 -> 3; matrix products, arithmetic and copies ran while one was open for 51% -> 45% of each run, Pallas kernels for 0% -> 0%
where the time goes in v14:
time: 98.6 us; the launch traced here: 97.8 us
  other arithmetic  21.8 us (22%)
  matrix products  21.4 us (22%)
  starting transfers between devices  19.9 us (20%)
  local copies, waits for them, and re-layouts  18.3 us (19%)
  waiting for transfers between devices  11.6 us (12%)
  between operations  4.84 us (5%)
    all_to_all x1, starting transfers between devices, per_device(): lax.all_to_all(packed, ('stripe', 'frame'), split_axis=0, concat_axis=0,...  10.9 us
    dot_general x1, matrix products, per_device(): jnp.dot(frame_rows_in, forward, preferred_element_type=jnp.float32)  6.9 us
    convert_element_type x1, other arithmetic, dft_table(): return (cos_t.astype(jnp.bfloat16), nsin_t.astype(jnp.bfloat16))  6.79 us
    all_to_all x1, waiting for transfers between devices, per_device(): lax.all_to_all(packed, ('stripe', 'frame'), split_axis=0, concat_axis=0,...  6.3 us
    dot_general x1, matrix products, per_device(): jnp.dot(visited, forward, preferred_element_type=jnp.float32)  5.6 us
    all_to_all x1, starting transfers between devices, per_device(): lax.all_to_all(outbound, 'stripe', split_axis=0, concat_axis=0, tiled=True)  5.51 us
    optimization_barrier x2, local copies, waits for them, and re-layouts, per_device(): partial, received = lax.optimization_barrier((partial, received))  5.1 us
    dot_general x1, matrix products, per_device(): lax.dot_general(coherence.reshape(count_frames * steps, 2 * columns), for...  5.1 us
  transfers between devices with their start and end apart: 3, of which 3 were waited for; matrix products, arithmetic and copies ran while one was open for 45% of the time, Pallas kernels for 0%

profile of v14, /device:TPU:0, one launch (start us, length us, event | category | flops | bytes accessed | tf_op | source)
XLA Modules:
  0.0 97.8 jit_solution(14729597538367505961)
XLA Ops:
  0.7 1.4 %slice_bitcast_fusion.8 = (bf16[128,2048]{1,0:T(8,128)(2,1)S(1)}, bf16[128,2048]{1,0:T(8,128)(2,1)S(1)}, bf16[1,128,2048]{2,1,0:T(8,128)(2,1)S(1)}, bf16[1,128,2048]{2,1,0:T(8,128)(2,1)S(1)}) fusion(bf16[2,128,2048]{2,1,0:T(8,128)(2,1)} %param.7), kind=kLoop, calls=%fused_computation.110 | loop fusion | bytes 3145728 | tf_op jit(solution)/shard_map/squeeze | solution.py:54
  2.1 2.4 %pad_maximum_fusion.7 = bf16[8,48,2048]{2,1,0:T(8,128)(2,1)} fusion(bf16[8,16,2048]{2,1,0:T(8,128)(2,1)} %bitcast.72, bf16[8,16,2048]{2,1,0:T(8,128)(2,1)S(1)} %bitcast.69, bf16[8,16,2048]{2,1,0:T(8,128)(2,1)S(1)} %bitcast.70), kind=kLoop, calls=%fused_computation.19 | loop fusion | flops 4718592 | bytes 3145728 | tf_op jit(solution)/shard_map/concatenate | solution.py:44
  4.5 5.5 %all-to-all-start = ((bf16[8,48,2048]{2,1,0:T(8,128)(2,1)}), bf16[8,48,2048]{2,1,0:T(8,128)(2,1)S(1)}, u32[]{:S(2)}, u32[]{:S(2)}) async-start(bf16[8,48,2048]{2,1,0:T(8,128)(2,1)} %pad_maximum_fusion.7), calls=%async_computation | async-start | bytes 3145728 | tf_op jit(solution)/shard_map/all_to_all | solution.py:49
  10.0 1.2 %fusion.29 = (f32[64,1152]{1,0:T(8,128)S(1)}, f32[64,1152]{1,0:T(8,128)S(1)}) fusion(), kind=kLoop, calls=%fused_computation.63 | loop fusion | flops 1032192 | bytes 589824 | tf_op jit(solution)/shard_map/sin | solution.py:19
  15.6 0.6 select_select_fusion
  17.4 0.9 fusion.16
  18.4 0.7 convolution_convert_fusion.1
  19.5 3.1 %copy.54 = bf16[128,4,2176]{2,1,0:T(4,128)(2,1)} copy(bf16[128,4,2176]{2,0,1:T(8,128)(2,1)S(1)} %pad_maximum_fusion.4) | data formatting | bytes 4456448 | tf_op jit(solution)/shard_map/concatenate | solution.py:72
  22.6 0.7 fusion.39
  23.2 6.8 %subtract_convert_fusion = (bf16[32,64,1152]{2,1,0:T(8,128)(2,1)}, bf16[32,64,1152]{2,1,0:T(8,128)(2,1)}) fusion(f32[64,1152]{1,0:T(8,128)S(1)} %get-tuple-element.26, f32[32,1152]{1,0:T(8,128)S(1)} %get-tuple-element.25, f32[64,1152]{1,0:T(8,128)S(1)} %get-tuple-element.27, f32[32,1152]{1,0:T(8,128)S(1)} %get-tuple-element.24), kind=kLoop, calls=%fused_computation.5 | loop fusion | flops 21233664 | bytes 10321920 | tf_op jit(solution)/shard_map/convert_element_type | solution.py:22
  30.4 1.2 %copy-done = bf16[8,48,2048]{2,1,0:T(8,128)(2,1)} copy-done((bf16[8,48,2048]{2,1,0:T(8,128)(2,1)}, bf16[8,48,2048]{2,1,0:T(8,128)(2,1)S(1)}, u32[]{:S(2)}) %copy-start) | copy-done | bytes 1572888
  31.6 10.9 %all-to-all-start.1 = ((bf16[128,4,2176]{2,1,0:T(4,128)(2,1)}), bf16[128,4,2176]{2,1,0:T(4,128)(2,1)S(1)}, u32[]{:S(2)}, u32[]{:S(2)}) async-start(bf16[128,4,2176]{2,1,0:T(4,128)(2,1)} %copy.54), calls=%async_computation.1 | async-start | bytes 4456448 | tf_op jit(solution)/shard_map/all_to_all | solution.py:73
  42.5 1.1 %slice.96 = bf16[8,16,2048]{2,1,0:T(8,128)(2,1)S(1)} slice(bf16[8,48,2048]{2,1,0:T(8,128)(2,1)} %copy-done), slice={[0:8], [32:48], [0:2048]} | slice | bytes 1048576 | tf_op jit(solution)/shard_map/slice | solution.py:80
  44.5 5.6 %fusion.5 = f32[64,2304]{1,0:T(8,128)} fusion(bf16[64,2048]{1,0:T(8,128)(2,1)S(1)} %reshape.235, bf16[2048,1152]{1,0:T(8,128)(2,1)} %bitcast.66, bf16[2048,1152]{1,0:T(8,128)(2,1)} %bitcast.63), kind=kOutput, calls=%fused_computation.10 | convolution fusion | flops 623149056 | bytes 10289152 | tf_op jit(solution)/shard_map/dot_general | solution.py:90
  50.1 2.1 %reshape.243 = f32[16,1,4,2304]{3,2,0,1:T(4,128)} reshape(f32[64,2304]{1,0:T(8,128)} %fusion.5) | data formatting | bytes 1179648 | tf_op jit(solution)/shard_map/reshape | solution.py:93
  52.1 6.9 %fusion.2 = f32[16,16,1,2304]{3,1,0,2:T(8,128)S(1)} fusion(bf16[2048,1152]{1,0:T(8,128)(2,1)} %bitcast.67, bf16[2048,1152]{1,0:T(8,128)(2,1)} %bitcast.64, bf16[16,16,2048]{2,0,1:T(8,128)(2,1)S(1)} %bitcast.62), kind=kOutput, calls=%fused_computation.8 | convolution fusion | flops 2434793472 | bytes 12845056 | tf_op jit(solution)/shard_map/dot_general | solution.py:84
  59.1 1.3 %slice_bitcast_fusion.1 = (f32[16,16,1152]{2,1,0:T(8,128)S(1)}, bf16[16,1152]{1,0:T(8,128)(2,1)S(1)}, f32[16,16,1152]{2,1,0:T(8,128)}) fusion(f32[16,16,1,2304]{3,1,0,2:T(8,128)S(1)} %fusion.2), kind=kLoop, calls=%fused_computation.22 | loop fusion | flops 1161216 | bytes 4755456 | tf_op jit(solution)/shard_map/mul | solution.py:99
  60.3 0.6 reshape_squeeze.11
  61.0 1.8 %slice_bitcast_fusion.3 = (f32[16,4,1152]{2,1,0:T(4,128)S(1)}, bf16[4,1152]{1,0:T(4,128)(2,1)}, f32[16,4,1152]{2,1,0:T(4,128)S(1)}) fusion(f32[16,1,4,2304]{3,2,0,1:T(4,128)} %reshape.243), kind=kLoop, calls=%fused_computation.56 | loop fusion | flops 290304 | bytes 1188864 | tf_op jit(solution)/shard_map/mul | solution.py:99
  62.8 2.5 %add_reduce_fusion = (bf16[16,4,1152]{2,0,1:T(8,128)(2,1)S(1)}, bf16[16,4,1152]{2,0,1:T(8,128)(2,1)S(1)}) fusion(f32[16,4,1152]{2,1,0:T(4,128)S(1)} %get-tuple-element.19, f32[16,16,1152]{2,1,0:T(8,128)} %get-tuple-element.10, f32[16,4,1152]{2,1,0:T(4,128)S(1)} %get-tuple-element.17, f32[16,16,1152]{2,1,0:T(8,128)S(1)} %get-tuple-element.8), kind=kLoop, calls=%fused_computation.7 | loop fusion | flops 9289728 | bytes 3244032 | tf_op jit(solution)/shard_map/reduce_sum | solution.py:99
  65.5 0.7 broadcast_in_dim.42
  66.2 0.9 pad_maximum_fusion.8
  67.1 6.3 %all-to-all-done.1 = bf16[128,4,2176]{2,1,0:T(4,128)(2,1)S(1)} async-done(((bf16[128,4,2176]{2,1,0:T(4,128)(2,1)}), bf16[128,4,2176]{2,1,0:T(4,128)(2,1)S(1)}, u32[]{:S(2)}, u32[]{:S(2)}) %all-to-all-start.1) | async-done | bytes 2228256 | tf_op jit(solution)/shard_map/all_to_all | solution.py:73
  73.5 1.6 %copy.58 = bf16[128,4,2176]{2,0,1:T(8,128)(2,1)} copy(bf16[128,4,2176]{2,1,0:T(4,128)(2,1)S(1)} %all-to-all-done.1) | data formatting | bytes 4456448 | tf_op jit(solution)/shard_map/optimization_barrier | solution.py:111
  75.1 3.5 %copy.57 = bf16[128,4,2176]{0,1,2:T(4,128)(2,1)} copy(bf16[128,4,2176]{2,1,0:T(4,128)(2,1)S(1)} %all-to-all-done.1) | data formatting | bytes 4456448 | tf_op jit(solution)/shard_map/optimization_barrier | solution.py:111
  78.7 0.8 pad_maximum_fusion.9
  79.5 3.5 %all-to-all-start.2 = ((bf16[8,23,1024]{2,1,0:T(8,128)(2,1)}), bf16[8,23,1024]{2,1,0:T(8,128)(2,1)S(1)}, u32[]{:S(2)}, u32[]{:S(2)}) async-start(bf16[8,23,1024]{2,1,0:T(8,128)(2,1)} %pad_maximum_fusion.9), calls=%async_computation.2 | async-start | bytes 786432 | tf_op jit(solution)/shard_map/all_to_all | solution.py:115
  83.0 0.6 fusion.47
  83.7 3.1 %fusion.8 = f32[128,2048]{1,0:T(8,128)} fusion(bf16[128,4,2176]{2,0,1:T(8,128)(2,1)} %copy.58, bf16[128,2048]{1,0:T(8,128)(2,1)} %param.6, f32[128]{0:T(128)S(1)} %broadcast_add_fusion, f32[128,4]{0,1:T(4,128)S(1)} %fusion.47), kind=kOutput, calls=%fused_computation.15 | convolution fusion | flops 269287424 | bytes 3672576 | tf_op jit(solution)/shard_map/tps,psx->tx/dot_general | solution.py:148
  86.8 4.9 %all-to-all-done.2 = bf16[8,23,1024]{2,1,0:T(8,128)(2,1)S(1)} async-done(((bf16[8,23,1024]{2,1,0:T(8,128)(2,1)}), bf16[8,23,1024]{2,1,0:T(8,128)(2,1)S(1)}, u32[]{:S(2)}, u32[]{:S(2)}) %all-to-all-start.2) | async-done | bytes 376864 | tf_op jit(solution)/shard_map/all_to_all | solution.py:115
  92.1 5.1 %fusion.9 = f32[8,2048]{1,0:T(8,128)S(1)} fusion(bf16[2048,1152]{1,0:T(8,128)(2,1)} %bitcast.68, bf16[2048,1152]{1,0:T(8,128)(2,1)} %bitcast.65, bf16[8,1152]{1,0:T(8,128)(2,1)S(1)} %get-tuple-element.21, bf16[8,1152]{1,0:T(8,128)(2,1)S(1)} %get-tuple-element.20), kind=kOutput, calls=%fused_computation.17 | convolution fusion | flops 94461952 | bytes 9539584 | tf_op jit(solution)/shard_map/dot_general | solution.py:137
  97.2 0.7 reshape.241
  (55 shorter events, 4.1 us)
Async XLA Ops:
  0.6 10.5 %copy-start.3 = (s32[2]{0:T(128)S(1)}, s32[2]{0:T(128)}, u32[]{:S(2)}) copy-start(s32[2]{0:T(128)} %param.8) | copy-start | bytes 28
  0.6 15.6 %copy-start.5 = (s32[4]{0:T(128)S(1)}, s32[4]{0:T(128)}, u32[]{:S(2)}) copy-start(s32[4]{0:T(128)} %param.11) | copy-start | bytes 52
  0.7 15.6 %copy-start.2 = (s32[256,1]{0,1:T(1,128)S(1)}, s32[256,1]{0,1:T(1,128)}, u32[]{:S(2)}) copy-start(s32[256,1]{0,1:T(1,128)} %param.9) | copy-start | bytes 3076
  2.1 15.1 %copy-start.4 = (s32[256]{0:T(256)S(1)}, s32[256]{0:T(256)}, u32[]{:S(2)}) copy-start(s32[256]{0:T(256)} %param.10) | copy-start | bytes 3076
  4.5 25.9 %all-to-all-start = ((bf16[8,48,2048]{2,1,0:T(8,128)(2,1)}), bf16[8,48,2048]{2,1,0:T(8,128)(2,1)S(1)}, u32[]{:S(2)}, u32[]{:S(2)}) async-start(bf16[8,48,2048]{2,1,0:T(8,128)(2,1)} %pad_maximum_fusion.7), calls=%async_computation | async-start | bytes 3145728 | tf_op jit(solution)/shard_map/all_to_all | solution.py:49
  30.4 1.2 %copy-start = (bf16[8,48,2048]{2,1,0:T(8,128)(2,1)}, bf16[8,48,2048]{2,1,0:T(8,128)(2,1)S(1)}, u32[]{:S(2)}) copy-start(bf16[8,48,2048]{2,1,0:T(8,128)(2,1)S(1)} %all-to-all-done) | copy-start | bytes 4718596
  31.6 41.8 %all-to-all-start.1 = ((bf16[128,4,2176]{2,1,0:T(4,128)(2,1)}), bf16[128,4,2176]{2,1,0:T(4,128)(2,1)S(1)}, u32[]{:S(2)}, u32[]{:S(2)}) async-start(bf16[128,4,2176]{2,1,0:T(4,128)(2,1)} %copy.54), calls=%async_computation.1 | async-start | bytes 4456448 | tf_op jit(solution)/shard_map/all_to_all | solution.py:73
  44.5 7.7 %slice-start = ((bf16[8,48,2048]{2,1,0:T(8,128)(2,1)}), bf16[8,32,2048]{2,1,0:T(8,128)(2,1)S(1)}, s32[]{:S(2)}) async-start(bf16[8,48,2048]{2,1,0:T(8,128)(2,1)} %copy-done), calls=%async_computation.3 | async-start | bytes 2097152 | tf_op jit(solution)/shard_map/slice | solution.py:75
  78.6 13.4 %copy-start.1 = (f32[1152]{0:T(1024)S(1)}, f32[1152]{0:T(1024)}, u32[]{:S(2)}) copy-start(f32[1152]{0:T(1024)} %select_select_fusion) | copy-start | bytes 13828
  79.5 12.2 %all-to-all-start.2 = ((bf16[8,23,1024]{2,1,0:T(8,128)(2,1)}), bf16[8,23,1024]{2,1,0:T(8,128)(2,1)S(1)}, u32[]{:S(2)}, u32[]{:S(2)}) async-start(bf16[8,23,1024]{2,1,0:T(8,128)(2,1)} %pad_maximum_fusion.9), calls=%async_computation.2 | async-start | bytes 786432 | tf_op jit(solution)/shard_map/all_to_all | solution.py:115

commit v15 on v11

--- a/solution.py
+++ b/solution.py
@@ -41,10 +41,11 @@
     weight = jnp.where((col == 0) | (col == half), 1.0, jnp.where(col < half, 2.0, 0.0))
 
     chunk = band_rows // stripes
-    frame_part = frames.reshape(count_frames, stripes, chunk, pixels).transpose(1, 0, 2, 3)
-    frame_part = frame_part.reshape(stripes, count_frames * chunk, pixels)
-    band_part = reference_img.reshape(stripes, chunk, pixels)
-    outbound = jnp.concatenate([frame_part, band_part], axis=1)
+    outbound = jnp.concatenate(
+        [frames[f].reshape(stripes, chunk, pixels) for f in range(count_frames)]
+        + [reference_img.reshape(stripes, chunk, pixels)],
+        axis=1,
+    )
     inbound = lax.all_to_all(outbound, "stripe", split_axis=0, concat_axis=0, tiled=True)
     num_devices = lax.axis_size("stripe") * lax.axis_size("frame")
     frame_rows = count_frames * band_rows
@@ -108,9 +109,10 @@
         axis=1,
     )
     partial, received = lax.optimization_barrier((partial, received))
-    total = jnp.sum(
-        lax.all_to_all(partial, "stripe", split_axis=0, concat_axis=0, tiled=True), axis=0
+    shares = lax.all_to_all(
+        partial.astype(jnp.bfloat16), "stripe", split_axis=0, concat_axis=0, tiled=True
     )
+    total = jnp.sum(shares.astype(jnp.float32), axis=0)
     pairs = count_frames * steps
     cross_re = total[:pairs].reshape(count_frames, steps, columns)
     cross_im = total[pairs : 2 * pairs].reshape(count_frames, steps, columns)

time: 99.7 us -> 92.5 us (0.928)
  waiting for transfers between devices: 12.7 us -> 9.12 us
  matrix products: 19.4 us -> 18.3 us
  other arithmetic: 23.8 us -> 22.8 us
    all_to_all x1, waiting for transfers between devices: 6.54 us -> 3.19 us  [per_device(): lax.all_to_all(partial.astype(jnp.bfloat16), 'stripe', split_axis=0, conc...]
    transpose x1 -> x0, local copies, waits for them, and re-layouts: 1.38 us -> none  [per_device(): frames.reshape(count_frames, stripes, chunk, pixels).transpose(1, 0, 2, 3)]
    concatenate x1, other arithmetic: 1.96 us -> 0.92 us  [shift_rows(): doubled = jnp.concatenate([frame_img, frame_img], axis=1)]
    dot_general x1, matrix products: 2.48 us -> 1.44 us  [per_device(): jnp.einsum('tps,psx->tx', hits.astype(jnp.bfloat16), incoming, preferred_...]
    reduce_sum x1, local copies, waits for them, and re-layouts: 1.08 us -> 0.06 us  [per_device(): cross_re = jnp.sum(spec_re * band_re + spec_im * band_im, axis=0)]
  transfers between devices with their start and end apart: 3 -> 3, of which waited for: 2 -> 3; matrix products, arithmetic and copies ran while one was open for 51% -> 51% of each run, Pallas kernels for 0% -> 0%
where the time goes in v15:
time: 92.5 us; the launch traced here: 91.8 us
  other arithmetic  22.8 us (25%)
  starting transfers between devices  19.9 us (22%)
  matrix products  18.3 us (20%)
  local copies, waits for them, and re-layouts  16.7 us (18%)
  waiting for transfers between devices  9.12 us (10%)
  between operations  4.91 us (5%)
    all_to_all x1, starting transfers between devices, per_device(): lax.all_to_all(packed, ('stripe', 'frame'), split_axis=0, concat_axis=0,...  10.9 us
    dot_general x1, matrix products, per_device(): jnp.dot(frame_rows_in, forward, preferred_element_type=jnp.float32)  6.9 us
    convert_element_type x1, other arithmetic, dft_table(): return (cos_t.astype(jnp.bfloat16), nsin_t.astype(jnp.bfloat16))  6.79 us
    dot_general x1, matrix products, per_device(): jnp.dot(visited, forward, preferred_element_type=jnp.float32)  5.6 us
    all_to_all x1, waiting for transfers between devices, per_device(): lax.all_to_all(packed, ('stripe', 'frame'), split_axis=0, concat_axis=0,...  5.55 us
    all_to_all x1, starting transfers between devices, per_device(): lax.all_to_all(outbound, 'stripe', split_axis=0, concat_axis=0, tiled=True)  5.51 us
    optimization_barrier x2, local copies, waits for them, and re-layouts, per_device(): partial, received = lax.optimization_barrier((partial, received))  3.78 us
    dot_general x1, matrix products, per_device(): lax.dot_general(coherence.reshape(2 * count_frames * steps, 2 * columns),...  3.66 us
  transfers between devices with their start and end apart: 3, of which 3 were waited for; matrix products, arithmetic and copies ran while one was open for 51% of the time, Pallas kernels for 0%

profile of v15, /device:TPU:0, one launch (start us, length us, event | category | flops | bytes accessed | tf_op | source)
XLA Modules:
  0.0 91.8 jit_solution(3316110592325102039)
XLA Ops:
  0.7 1.4 %slice_bitcast_fusion.7 = (bf16[128,2048]{1,0:T(8,128)(2,1)S(1)}, bf16[128,2048]{1,0:T(8,128)(2,1)S(1)}, bf16[1,128,2048]{2,1,0:T(8,128)(2,1)S(1)}, bf16[1,128,2048]{2,1,0:T(8,128)(2,1)S(1)}) fusion(bf16[2,128,2048]{2,1,0:T(8,128)(2,1)} %param.7), kind=kLoop, calls=%fused_computation.114 | loop fusion | bytes 3145728 | tf_op jit(solution)/shard_map/squeeze | solution.py:54
  2.1 2.4 %pad_maximum_fusion.8 = bf16[8,48,2048]{2,1,0:T(8,128)(2,1)} fusion(bf16[8,16,2048]{2,1,0:T(8,128)(2,1)} %bitcast.69, bf16[8,16,2048]{2,1,0:T(8,128)(2,1)S(1)} %bitcast.66, bf16[8,16,2048]{2,1,0:T(8,128)(2,1)S(1)} %bitcast.67), kind=kLoop, calls=%fused_computation.22 | loop fusion | flops 4718592 | bytes 3145728 | tf_op jit(solution)/shard_map/concatenate | solution.py:44
  4.5 5.5 %all-to-all-start = ((bf16[8,48,2048]{2,1,0:T(8,128)(2,1)}), bf16[8,48,2048]{2,1,0:T(8,128)(2,1)S(1)}, u32[]{:S(2)}, u32[]{:S(2)}) async-start(bf16[8,48,2048]{2,1,0:T(8,128)(2,1)} %pad_maximum_fusion.8), calls=%async_computation | async-start | bytes 3145728 | tf_op jit(solution)/shard_map/all_to_all | solution.py:49
  10.0 0.6 select_select_fusion
  10.6 1.2 %fusion.32 = (f32[64,1152]{1,0:T(8,128)S(1)}, f32[64,1152]{1,0:T(8,128)S(1)}) fusion(), kind=kLoop, calls=%fused_computation.67 | loop fusion | flops 1032192 | bytes 589824 | tf_op jit(solution)/shard_map/sin | solution.py:19
  11.8 0.6 fusion.59
  17.4 0.9 %fusion.19 = (bf16[128,2048]{1,0:T(8,128)(2,1)S(1)}, bf16[128,2048]{1,0:T(8,128)(2,1)S(1)}) fusion(s32[]{:T(128)S(6)} %select_n.72, bf16[128,2048]{1,0:T(8,128)(2,1)S(1)} %get-tuple-element.12, s32[]{:T(128)S(6)} %select_n.71, bf16[128,2048]{1,0:T(8,128)(2,1)S(1)} %get-tuple-element.11), kind=kLoop, calls=%fused_computation.40 | loop fusion | flops 2097152 | bytes 2097160 | tf_op jit(solution)/shard_map/concatenate | solution.py:27
  18.4 0.7 convolution_convert_fusion
  19.5 3.1 %copy.55 = bf16[128,4,2176]{2,1,0:T(4,128)(2,1)} copy(bf16[128,4,2176]{2,0,1:T(8,128)(2,1)S(1)} %pad_maximum_fusion.7) | data formatting | bytes 4456448 | tf_op jit(solution)/shard_map/concatenate | solution.py:72
  22.6 0.7 fusion.45
  23.2 6.8 %subtract_convert_fusion = (bf16[32,64,1152]{2,1,0:T(8,128)(2,1)}, bf16[32,64,1152]{2,1,0:T(8,128)(2,1)}) fusion(f32[64,1152]{1,0:T(8,128)S(1)} %get-tuple-element.32, f32[32,1152]{1,0:T(8,128)S(1)} %get-tuple-element.29, f32[64,1152]{1,0:T(8,128)S(1)} %get-tuple-element.33, f32[32,1152]{1,0:T(8,128)S(1)} %get-tuple-element.28), kind=kLoop, calls=%fused_computation.7 | loop fusion | flops 21233664 | bytes 10321920 | tf_op jit(solution)/shard_map/convert_element_type | solution.py:22
  30.4 1.2 %copy-done = bf16[8,48,2048]{2,1,0:T(8,128)(2,1)} copy-done((bf16[8,48,2048]{2,1,0:T(8,128)(2,1)}, bf16[8,48,2048]{2,1,0:T(8,128)(2,1)S(1)}, u32[]{:S(2)}) %copy-start) | copy-done | bytes 1572888
  31.6 10.9 %all-to-all-start.1 = ((bf16[128,4,2176]{2,1,0:T(4,128)(2,1)}), bf16[128,4,2176]{2,1,0:T(4,128)(2,1)S(1)}, u32[]{:S(2)}, u32[]{:S(2)}) async-start(bf16[128,4,2176]{2,1,0:T(4,128)(2,1)} %copy.55), calls=%async_computation.1 | async-start | bytes 4456448 | tf_op jit(solution)/shard_map/all_to_all | solution.py:73
  42.5 1.1 %slice.98 = bf16[8,16,2048]{2,1,0:T(8,128)(2,1)S(1)} slice(bf16[8,48,2048]{2,1,0:T(8,128)(2,1)} %copy-done), slice={[0:8], [32:48], [0:2048]} | slice | bytes 1048576 | tf_op jit(solution)/shard_map/slice | solution.py:80
  44.5 5.6 %fusion.10 = f32[64,2304]{1,0:T(8,128)} fusion(bf16[64,2048]{1,0:T(8,128)(2,1)S(1)} %reshape.231, bf16[2048,1152]{1,0:T(8,128)(2,1)} %bitcast.63, bf16[2048,1152]{1,0:T(8,128)(2,1)} %bitcast.60), kind=kOutput, calls=%fused_computation.15 | convolution fusion | flops 623149056 | bytes 10289152 | tf_op jit(solution)/shard_map/dot_general | solution.py:90
  50.1 2.1 %reshape.240 = f32[16,1,4,2304]{3,2,0,1:T(4,128)} reshape(f32[64,2304]{1,0:T(8,128)} %fusion.10) | data formatting | bytes 1179648 | tf_op jit(solution)/shard_map/reshape | solution.py:93
  52.1 6.9 %fusion.6 = f32[16,16,1,2304]{3,1,0,2:T(8,128)S(1)} fusion(bf16[2048,1152]{1,0:T(8,128)(2,1)} %bitcast.64, bf16[2048,1152]{1,0:T(8,128)(2,1)} %bitcast.61, bf16[16,16,2048]{2,0,1:T(8,128)(2,1)S(1)} %bitcast.59), kind=kOutput, calls=%fused_computation.13 | convolution fusion | flops 2434793472 | bytes 12845056 | tf_op jit(solution)/shard_map/dot_general | solution.py:84
  59.1 1.3 %slice_bitcast_fusion.1 = (f32[16,16,1152]{2,1,0:T(8,128)S(1)}, bf16[16,1152]{1,0:T(8,128)(2,1)S(1)}, f32[16,16,1152]{2,1,0:T(8,128)}) fusion(f32[16,16,1,2304]{3,1,0,2:T(8,128)S(1)} %fusion.6), kind=kLoop, calls=%fused_computation.25 | loop fusion | flops 1161216 | bytes 4755456 | tf_op jit(solution)/shard_map/mul | solution.py:99
  60.3 0.6 reshape_squeeze.11
  61.0 1.8 %slice_bitcast_fusion.3 = (f32[16,4,1152]{2,1,0:T(4,128)S(1)}, bf16[4,1152]{1,0:T(4,128)(2,1)}, f32[16,4,1152]{2,1,0:T(4,128)S(1)}) fusion(f32[16,1,4,2304]{3,2,0,1:T(4,128)} %reshape.240), kind=kLoop, calls=%fused_computation.58 | loop fusion | flops 290304 | bytes 1188864 | tf_op jit(solution)/shard_map/mul | solution.py:99
  62.8 2.5 %add_reduce_fusion = (bf16[16,4,1152]{2,0,1:T(8,128)(2,1)S(1)}, bf16[16,4,1152]{2,0,1:T(8,128)(2,1)S(1)}) fusion(f32[16,4,1152]{2,1,0:T(4,128)S(1)} %get-tuple-element.19, f32[16,16,1152]{2,1,0:T(8,128)} %get-tuple-element.10, f32[16,4,1152]{2,1,0:T(4,128)S(1)} %get-tuple-element.17, f32[16,16,1152]{2,1,0:T(8,128)S(1)} %get-tuple-element.8), kind=kLoop, calls=%fused_computation.12 | loop fusion | flops 9289728 | bytes 3244032 | tf_op jit(solution)/shard_map/reduce_sum | solution.py:99
  65.5 0.7 broadcast_in_dim.37
  66.2 1.6 %pad_maximum_fusion.9 = bf16[8,22,1152]{2,1,0:T(8,128)(2,1)} fusion(bf16[8,4,1152]{2,1,0:T(4,128)(2,1)S(1)} %broadcast_in_dim.37, bf16[8,2,1152]{2,1,0:T(2,128)(2,1)} %reshape_squeeze.11, bf16[8,8,1152]{2,1,0:T(8,128)(2,1)S(1)} %reshape.235, bf16[8,8,1152]{2,1,0:T(8,128)(2,1)S(1)} %reshape.234), kind=kLoop, calls=%fused_computation.34 | loop fusion | flops 1622016 | bytes 811008 | tf_op jit(solution)/shard_map/concatenate | solution.py:102
  67.8 5.5 %all-to-all-done.1 = bf16[128,4,2176]{2,1,0:T(4,128)(2,1)S(1)} async-done(((bf16[128,4,2176]{2,1,0:T(4,128)(2,1)}), bf16[128,4,2176]{2,1,0:T(4,128)(2,1)S(1)}, u32[]{:S(2)}, u32[]{:S(2)}) %all-to-all-start.1) | async-done | bytes 2228256 | tf_op jit(solution)/shard_map/all_to_all | solution.py:73
  73.4 3.5 %all-to-all-start.2 = ((bf16[8,22,1152]{2,1,0:T(8,128)(2,1)}), bf16[8,22,1152]{2,1,0:T(8,128)(2,1)S(1)}, u32[]{:S(2)}, u32[]{:S(2)}) async-start(bf16[8,22,1152]{2,1,0:T(8,128)(2,1)} %pad_maximum_fusion.9), calls=%async_computation.2 | async-start | bytes 884736 | tf_op jit(solution)/shard_map/all_to_all | solution.py:112
  76.8 3.6 %copy.57 = bf16[128,4,2176]{0,1,2:T(4,128)(2,1)} copy(bf16[128,4,2176]{2,1,0:T(4,128)(2,1)S(1)} %all-to-all-done.1) | data formatting | bytes 4456448 | tf_op jit(solution)/shard_map/optimization_barrier | solution.py:111
  80.4 0.6 fusion.52
  81.4 1.4 %fusion.12 = f32[128,2048]{1,0:T(8,128)} fusion(bf16[128,4,2176]{2,0,1:T(8,128)(2,1)S(1)} %copy.58, bf16[128,2048]{1,0:T(8,128)(2,1)S(1)} %copy-done.1, f32[128]{0:T(128)S(1)} %broadcast_add_fusion, f32[128,4]{0,1:T(4,128)S(1)} %fusion.52), kind=kOutput, calls=%fused_computation.19 | convolution fusion | flops 269287424 | bytes 3672576 | tf_op jit(solution)/shard_map/tps,psx->tx/dot_general | solution.py:149
  82.9 3.2 %all-to-all-done.2 = bf16[8,22,1152]{2,1,0:T(8,128)(2,1)S(1)} async-done(((bf16[8,22,1152]{2,1,0:T(8,128)(2,1)}), bf16[8,22,1152]{2,1,0:T(8,128)(2,1)S(1)}, u32[]{:S(2)}, u32[]{:S(2)}) %all-to-all-start.2) | async-done | bytes 405536 | tf_op jit(solution)/shard_map/all_to_all | solution.py:112
  86.5 3.7 %fusion.4 = f32[16,1152]{1,0:T(8,128)S(1)} fusion(bf16[16,2304]{1,0:T(8,128)(2,1)S(1)} %convert_element_type.120, bf16[2048,1152]{1,0:T(8,128)(2,1)} %bitcast.62, bf16[2048,1152]{1,0:T(8,128)(2,1)} %bitcast.65), kind=kOutput, calls=%fused_computation.10 | convolution fusion | flops 95551488 | bytes 9584640 | tf_op jit(solution)/shard_map/dot_general | solution.py:133
  90.3 0.6 reverse
  91.0 0.7 maximum_multiply_fusion
  (58 shorter events, 3.9 us)
Async XLA Ops:
  0.6 11.1 %copy-start.4 = (s32[2]{0:T(128)S(1)}, s32[2]{0:T(128)}, u32[]{:S(2)}) copy-start(s32[2]{0:T(128)} %param.8) | copy-start | bytes 28
  0.6 15.6 %copy-start.6 = (s32[4]{0:T(128)S(1)}, s32[4]{0:T(128)}, u32[]{:S(2)}) copy-start(s32[4]{0:T(128)} %param.11) | copy-start | bytes 52
  0.7 15.6 %copy-start.3 = (s32[256,1]{0,1:T(1,128)S(1)}, s32[256,1]{0,1:T(1,128)}, u32[]{:S(2)}) copy-start(s32[256,1]{0,1:T(1,128)} %param.9) | copy-start | bytes 3076
  2.1 15.1 %copy-start.5 = (s32[256]{0:T(256)S(1)}, s32[256]{0:T(256)}, u32[]{:S(2)}) copy-start(s32[256]{0:T(256)} %param.10) | copy-start | bytes 3076
  4.5 25.9 %all-to-all-start = ((bf16[8,48,2048]{2,1,0:T(8,128)(2,1)}), bf16[8,48,2048]{2,1,0:T(8,128)(2,1)S(1)}, u32[]{:S(2)}, u32[]{:S(2)}) async-start(bf16[8,48,2048]{2,1,0:T(8,128)(2,1)} %pad_maximum_fusion.8), calls=%async_computation | async-start | bytes 3145728 | tf_op jit(solution)/shard_map/all_to_all | solution.py:49
  30.4 1.2 %copy-start = (bf16[8,48,2048]{2,1,0:T(8,128)(2,1)}, bf16[8,48,2048]{2,1,0:T(8,128)(2,1)S(1)}, u32[]{:S(2)}) copy-start(bf16[8,48,2048]{2,1,0:T(8,128)(2,1)S(1)} %all-to-all-done) | copy-start | bytes 4718596
  31.6 41.8 %all-to-all-start.1 = ((bf16[128,4,2176]{2,1,0:T(4,128)(2,1)}), bf16[128,4,2176]{2,1,0:T(4,128)(2,1)S(1)}, u32[]{:S(2)}, u32[]{:S(2)}) async-start(bf16[128,4,2176]{2,1,0:T(4,128)(2,1)} %copy.55), calls=%async_computation.1 | async-start | bytes 4456448 | tf_op jit(solution)/shard_map/all_to_all | solution.py:73
  44.5 7.7 %slice-start = ((bf16[8,48,2048]{2,1,0:T(8,128)(2,1)}), bf16[8,32,2048]{2,1,0:T(8,128)(2,1)S(1)}, s32[]{:S(2)}) async-start(bf16[8,48,2048]{2,1,0:T(8,128)(2,1)} %copy-done), calls=%async_computation.3 | async-start | bytes 2097152 | tf_op jit(solution)/shard_map/slice | solution.py:75
  67.8 13.6 %copy-start.1 = (bf16[128,2048]{1,0:T(8,128)(2,1)S(1)}, bf16[128,2048]{1,0:T(8,128)(2,1)}, u32[]{:S(2)}) copy-start(bf16[128,2048]{1,0:T(8,128)(2,1)} %param.6) | copy-start | bytes 1572868
  73.4 12.7 %all-to-all-start.2 = ((bf16[8,22,1152]{2,1,0:T(8,128)(2,1)}), bf16[8,22,1152]{2,1,0:T(8,128)(2,1)S(1)}, u32[]{:S(2)}, u32[]{:S(2)}) async-start(bf16[8,22,1152]{2,1,0:T(8,128)(2,1)} %pad_maximum_fusion.9), calls=%async_computation.2 | async-start | bytes 884736 | tf_op jit(solution)/shard_map/all_to_all | solution.py:112
  81.4 5.0 %copy-start.2 = (f32[1152]{0:T(1024)S(1)}, f32[1152]{0:T(1024)}, u32[]{:S(2)}) copy-start(f32[1152]{0:T(1024)} %select_select_fusion) | copy-start | bytes 13828
